TPU v7x, 256 devices: a whole 4x4x8 slice. The times are simulated.
256 devices in a mesh: band: 16 (over x, y_hi, core), req: 16 (over y_lo, z).
Axes of the slice: x: 4, y: 4 (y_hi: 2, y_lo: 2; y = y_hi * 2 + y_lo), z: 8, core: 2. Of those that a mesh axis runs over, the one named last changes fastest.
Arguments:
- latents: bfloat16 [16, 64, 512, 320], P('req', 'band'), may hold values from -40 to 40
- request_time_embedding: bfloat16 [16, 1280], P('req'), may hold values from -6 to 6
- request_adapter: int32 [16, 1], P('req'), may hold values from 0 to 255, as said below
- adapter_stored_row: int32 [256], replicated, may hold values from 0 to 255, as said below
- first_conv_weight: bfloat16 [3, 3, 320, 320], replicated, may hold values from -0.109375 to 0.109375
- stored_down_weight: bfloat16 [256, 3, 3, 320, 64], P(('band', 'req')), may hold values from -0.109375 to 0.109375
- stored_up_weight: bfloat16 [256, 64, 320], P(('band', 'req')), may hold values from -0.75 to 0.75
- second_conv_weight: bfloat16 [3, 3, 320, 320], replicated, may hold values from -0.109375 to 0.109375
- time_projection_weight: bfloat16 [1280, 320], replicated, may hold values from -0.15625 to 0.15625
Outputs:
- block_out: bfloat16 [16, 64, 512, 320], P('req', 'band')
Inputs may be any that keep to these rules, and one draw needn't show every extreme that they name: `request_adapter`: ids of adapters. `adapter_stored_row`: each stored row appears once.
All inputs are finite; a program needn't handle non-finite values.
Results may differ from a plain program's by a relative error of at most 0.0038.
Values may be sent and summed in bfloat16 or wider, within the bound.
No kernel may reach another device: no remote copies, remote signals or barrier semaphores. Data moves between devices by JAX's collectives and lax.ppermute only.
A program may use at most 128 MiB of HBM per device.

v0:
```python
import jax
import jax.numpy as jnp
from jax import lax
from jax.experimental import pallas as pl
from jax.sharding import PartitionSpec as P

G = 32


def with_halo(x, sides, width):
    for axis, dim in sides:
        count, length = (lax.axis_size(axis), x.shape[dim])
        up = [(i, (i + 1) % count) for i in range(count - 1)]
        down = [(j, i) for i, j in up]
        last = lax.slice_in_dim(x, length - width, length, axis=dim)
        initial = lax.slice_in_dim(x, 0, width, axis=dim)
        before = lax.ppermute(last, axis, up)
        after = lax.ppermute(initial, axis, down)
        x = jnp.concatenate([before, x, after], axis=dim)
    return x


def exchange(value, axis):
    count = lax.axis_size(axis)
    spread = jnp.broadcast_to(value[None], (count,) + value.shape)
    return lax.all_to_all(spread, axis, 0, 0, tiled=True)


def group_norm(field, groups):
    requests, rows, width, channels = field.shape
    grouped = field.reshape(requests, rows, width, groups, channels // groups)
    count = rows * width * (channels // groups)
    local_mean = jnp.sum(grouped, axis=(1, 2, 4)) / count
    deviation = grouped - local_mean[:, None, None, :, None]
    local_m2 = jnp.sum(deviation * deviation, axis=(1, 2, 4))
    stats = exchange(jnp.stack([local_mean, local_m2]), "band")
    means, m2s = stats[:, 0], stats[:, 1]
    bands = means.shape[0]
    mean = jnp.sum(means, axis=0) / bands
    gap = means - mean[None]
    m2 = jnp.sum(m2s, axis=0) + count * jnp.sum(gap * gap, axis=0)
    spread = m2 / (count * bands)
    centered = grouped - mean[:, None, None, :, None]
    normed = centered * lax.rsqrt(spread + 1e-05)[:, None, None, :, None]
    return normed.reshape(field.shape)


def padded_field(field):
    extended = with_halo(field, (("band", 1),), 1)
    return jnp.pad(extended, ((0, 0), (0, 0), (1, 1), (0, 0)))


def taps_by_column(padded):
    width = padded.shape[1] - 2
    return jnp.concatenate([padded[:, tap : tap + width] for tap in range(3)], axis=-1)


def first_conv_kernel(x_ref, w_ref, d_ref, u_ref, s_ref, o_ref):
    row = pl.program_id(0)
    main = None
    low = None
    for tap in range(3):
        piece = x_ref[row + tap]
        m = jnp.dot(piece, w_ref[tap], preferred_element_type=jnp.float32)
        l = jnp.dot(piece, d_ref[tap], preferred_element_type=jnp.float32)
        main = m if main is None else main + m
        low = l if low is None else low + l
    lifted = jnp.dot(low.astype(jnp.bfloat16), u_ref[...], preferred_element_type=jnp.float32)
    o_ref[0] = main + lifted + s_ref[...]


def second_conv_kernel(x_ref, w_ref, r_ref, o_ref):
    row = pl.program_id(0)
    total = None
    for tap in range(3):
        t = jnp.dot(x_ref[row + tap], w_ref[tap], preferred_element_type=jnp.float32)
        total = t if total is None else total + t
    o_ref[0] = (r_ref[0].astype(jnp.float32) + total).astype(o_ref.dtype)


def first_conv(cols, weight, down, up, shift):
    rows, width, wide = cols.shape[0] - 2, cols.shape[1], cols.shape[2]
    out = weight.shape[-1]
    rank = down.shape[-1]
    flops = 2 * rows * width * wide * (out + rank) + 2 * rows * width * rank * out
    return pl.pallas_call(
        first_conv_kernel,
        grid=(rows,),
        in_specs=[
            pl.BlockSpec(cols.shape, lambda h: (0, 0, 0)),
            pl.BlockSpec(weight.shape, lambda h: (0, 0, 0)),
            pl.BlockSpec(down.shape, lambda h: (0, 0, 0)),
            pl.BlockSpec(up.shape, lambda h: (0, 0)),
            pl.BlockSpec(shift.shape, lambda h: (0, 0)),
        ],
        out_specs=pl.BlockSpec((1, width, out), lambda h: (h, 0, 0)),
        out_shape=jax.ShapeDtypeStruct((rows, width, out), jnp.float32),
        cost_estimate=pl.CostEstimate(
            flops=flops, transcendentals=0,
            bytes_accessed=cols.size * 2 + weight.size * 2 + down.size * 2 + rows * width * out * 4,
        ),
    )(cols, weight, down, up, shift)


def second_conv(cols, weight, residual):
    rows, width, wide = cols.shape[0] - 2, cols.shape[1], cols.shape[2]
    out = weight.shape[-1]
    return pl.pallas_call(
        second_conv_kernel,
        grid=(rows,),
        in_specs=[
            pl.BlockSpec(cols.shape, lambda h: (0, 0, 0)),
            pl.BlockSpec(weight.shape, lambda h: (0, 0, 0)),
            pl.BlockSpec((1, width, out), lambda h: (h, 0, 0)),
        ],
        out_specs=pl.BlockSpec((1, width, out), lambda h: (h, 0, 0)),
        out_shape=jax.ShapeDtypeStruct((rows, width, out), residual.dtype),
        cost_estimate=pl.CostEstimate(
            flops=2 * rows * width * wide * out, transcendentals=0,
            bytes_accessed=cols.size * 2 + weight.size * 2 + rows * width * out * 4,
        ),
    )(cols, weight, residual)


def fetch_adapter(slots, down, up):
    bands, reqs = lax.axis_size("band"), lax.axis_size("req")
    flat = jnp.concatenate([down.reshape(-1), up.reshape(-1)])
    pieces = flat.reshape(bands, -1)
    by_band = lax.all_to_all(pieces, "band", 0, 0, tiled=True)
    wanted = jnp.take(by_band, slots // reqs, axis=0)
    by_req = lax.all_to_all(wanted, "req", 0, 0, tiled=True)
    own = lax.axis_index("req")
    mine = lax.dynamic_index_in_dim(by_req, slots[own] % reqs, 0, keepdims=True)
    whole = exchange(mine[0], "band").reshape(-1)
    down_size = down.size
    return whole[:down_size].reshape(down.shape[1:]), whole[down_size:].reshape(up.shape[1:])


def shards(
    latents,
    request_time_embedding,
    request_adapter,
    adapter_stored_row,
    first_conv_weight,
    stored_down_weight,
    stored_up_weight,
    second_conv_weight,
    time_projection_weight,
):
    requests, rows, width, channels = latents.shape
    every_adapter = exchange(request_adapter[0, 0], "req")
    slots = jnp.take(adapter_stored_row, every_adapter, axis=0)
    chosen_down, chosen_up = fetch_adapter(slots, stored_down_weight, stored_up_weight)
    shift = jnp.dot(
        jax.nn.silu(request_time_embedding.astype(jnp.float32)).astype(jnp.bfloat16),
        time_projection_weight,
        preferred_element_type=jnp.float32,
    )
    first = jax.nn.silu(group_norm(latents.astype(jnp.float32), G)).astype(jnp.bfloat16)
    wide = 3 * channels
    hidden = first_conv(
        taps_by_column(padded_field(first)[0]),
        first_conv_weight.reshape(3, wide, channels),
        chosen_down.reshape(3, wide, chosen_down.shape[-1]),
        chosen_up,
        shift,
    )[None]
    second = jax.nn.silu(group_norm(hidden, G)).astype(jnp.bfloat16)
    result = second_conv(
        taps_by_column(padded_field(second)[0]),
        second_conv_weight.reshape(3, wide, channels),
        latents[0],
    )
    return result[None]


def solution(mesh):
    in_specs = (
        P("req", "band", None, None),
        P("req", None),
        P("req", None),
        P(),
        P(),
        P(("band", "req"), None, None, None, None),
        P(("band", "req"), None, None),
        P(),
        P(),
    )
    out_specs = P("req", "band", None, None)
    return jax.shard_map(shards, mesh=mesh, in_specs=in_specs, out_specs=out_specs, check_vma=False)
```

profile of v0, /device:TPU:1, one launch (start us, length us, event | category | flops | bytes accessed | tf_op | source)
XLA Modules:
  0.0 192.9 jit_solution(17477241587512822961)
XLA Ops:
  1.3 10.2 %all-to-all-start.1 = ((s32[16,1,1]{2,1,0:T(1,128)}), s32[16,1,1]{2,1,0:T(1,128)}, u32[]{:S(2)}, u32[]{:S(2)}) async-start(s32[16,1,1]{2,1,0:T(1,128)} %broadcast_in_dim.54), calls=%async_computation.1 | async-start | bytes 16384 | tf_op jit(solution)/shard_map/all_to_all | solution.py:26
  21.6 3.9 %reduce.29 = bf16[16,12800]{1,0:T(8,128)(2,1)} reduce(bf16[16,1,12800]{2,1,0:T(2,128)(2,1)S(1)} %all_to_all.40, bf16[]{:T(256)} %broadcast.487), dimensions={1}, to_apply=%all_to_all.40.reduce_sub_computation | reduce | bytes 819202 | tf_op jit(solution)/shard_map/all_to_all | solution.py:129
  29.6 7.6 %all-to-all-start = ((f32[16,2,1,32]{3,2,1,0:T(1,128)}), f32[16,2,1,32]{3,2,1,0:T(1,128)S(1)}, u32[]{:S(2)}, u32[]{:S(2)}) async-start(f32[16,2,1,32]{3,2,1,0:T(1,128)} %broadcast_in_dim.29), calls=%async_computation | async-start | bytes 32768 | tf_op jit(solution)/shard_map/all_to_all | solution.py:26
  41.7 2.8 %all-to-all-done = f32[16,2,1,32]{3,2,1,0:T(1,128)S(1)} async-done(((f32[16,2,1,32]{3,2,1,0:T(1,128)}), f32[16,2,1,32]{3,2,1,0:T(1,128)S(1)}, u32[]{:S(2)}, u32[]{:S(2)}) %all-to-all-start) | async-done | bytes 4128 | tf_op jit(solution)/shard_map/all_to_all | solution.py:26
  44.5 4.5 %all-to-all-start.2 = ((bf16[16,2,6400]{2,1,0:T(2,128)(2,1)}), bf16[16,2,6400]{2,1,0:T(2,128)(2,1)S(1)}, u32[]{:S(2)}, u32[]{:S(2)}) async-start(bf16[16,2,6400]{2,1,0:T(2,128)(2,1)} %reshape.460), calls=%async_computation.2 | async-start | bytes 819200 | tf_op jit(solution)/shard_map/all_to_all | solution.py:129
  52.5 5.0 %collective-permute-start = (bf16[1,1,512,320]{3,2,1,0:T(8,128)(2,1)}, bf16[1,1,512,320]{3,2,1,0:T(8,128)(2,1)}, u32[]{:S(2)}, u32[]{:S(2)}) collective-permute-start(bf16[1,1,512,320]{3,2,1,0:T(8,128)(2,1)} %get-tuple-element.15), channel_id=1, source_target_pairs={{0,16},{16,32},{32,48},{48,64},{64,80},{80,96},{96,112},{112,128},... | collective-permute-start | bytes 983048 | tf_op jit(solution)/shard_map/ppermute | solution.py:17
  64.3 7.2 %all-to-all-start.3 = ((bf16[16,2,6400]{2,1,0:T(2,128)(2,1)}), bf16[16,2,6400]{2,1,0:T(2,128)(2,1)}, u32[]{:S(2)}, u32[]{:S(2)}) async-start(bf16[16,2,6400]{2,1,0:T(2,128)(2,1)} %reshape.462), calls=%async_computation.3 | async-start | bytes 819200 | tf_op jit(solution)/shard_map/all_to_all | solution.py:131
  71.6 2.6 %fusion.16 = bf16[6,514,320]{2,1,0:T(8,128)(2,1)S(1)} fusion(bf16[1,1,512,320]{3,2,1,0:T(8,128)(2,1)} %collective-permute-done.1, bf16[1,4,512,320]{3,2,1,0:T(8,128)(2,1)S(1)} %copy-done.4, bf16[1,1,512,320]{3,2,1,0:T(8,128)(2,1)} %collective-permute-done), kind=kLoop, calls=%fused_computation.29 | loop fusion | flops 11842560 | bytes 3939840 | tf_op jit(solution)/shard_map/squeeze | solution.py:162
  74.2 3.5 %fusion.31 = (bf16[6,512,320]{2,1,0:T(8,128)(2,1)S(1)}, bf16[6,512,320]{2,1,0:T(8,128)(2,1)}, bf16[6,512,320]{2,1,0:T(8,128)(2,1)}) fusion(bf16[6,514,320]{2,1,0:T(8,128)(2,1)S(1)} %fusion.16), kind=kLoop, calls=%fused_computation.76 | loop fusion | bytes 11796480 | tf_op jit(solution)/shard_map/slice | solution.py:55
  77.7 5.3 %all-to-all-done.3 = bf16[16,2,6400]{2,1,0:T(2,128)(2,1)} async-done(((bf16[16,2,6400]{2,1,0:T(2,128)(2,1)}), bf16[16,2,6400]{2,1,0:T(2,128)(2,1)}, u32[]{:S(2)}, u32[]{:S(2)}) %all-to-all-start.3) | async-done | bytes 409632 | tf_op jit(solution)/shard_map/all_to_all | solution.py:131
  83.1 3.5 %reshape.463 = bf16[16,1,12800]{2,1,0:T(2,128)(2,1)} reshape(bf16[16,2,6400]{2,1,0:T(2,128)(2,1)} %all-to-all-done.3) | data formatting | bytes 819200
  88.8 4.7 %reduce.31 = bf16[16,12800]{1,0:T(8,128)(2,1)} reduce(bf16[16,1,12800]{2,1,0:T(2,128)(2,1)} %broadcast_in_dim.57, bf16[]{:T(256)} %broadcast.487), dimensions={1}, to_apply=%broadcast_in_dim.57.reduce_sub_computation | reduce | bytes 819202 | tf_op jit(solution)/shard_map/broadcast_in_dim | solution.py:25
  95.4 8.6 %all-to-all-start.4 = ((bf16[16,2,6400]{2,1,0:T(2,128)(2,1)}), bf16[16,2,6400]{2,1,0:T(2,128)(2,1)}, u32[]{:S(2)}, u32[]{:S(2)}) async-start(bf16[16,2,6400]{2,1,0:T(2,128)(2,1)} %reshape.464), calls=%async_computation.4 | async-start | bytes 819200 | tf_op jit(solution)/shard_map/all_to_all | solution.py:26
  103.9 7.3 %pad_maximum_fusion.x_ref = bf16[6,512,960]{2,1,0:T(8,128)(2,1)} fusion(bf16[6,512,320]{2,1,0:T(8,128)(2,1)} %get-tuple-element.11, bf16[6,512,320]{2,1,0:T(8,128)(2,1)} %get-tuple-element.12, bf16[6,512,320]{2,1,0:T(8,128)(2,1)S(1)} %get-tuple-element.10), kind=kLoop, calls=%fused_computation.4 | loop fusion | flops 17694720 | bytes 11796480 | tf_op jit(solution)/shard_map/concatenate | solution.py:55
  111.2 3.1 %all-to-all-done.4 = bf16[16,2,6400]{2,1,0:T(2,128)(2,1)} async-done(((bf16[16,2,6400]{2,1,0:T(2,128)(2,1)}), bf16[16,2,6400]{2,1,0:T(2,128)(2,1)}, u32[]{:S(2)}, u32[]{:S(2)}) %all-to-all-start.4) | async-done | bytes 409632 | tf_op jit(solution)/shard_map/all_to_all | solution.py:26
  114.3 2.7 %reshape.465 = bf16[16,1,12800]{2,1,0:T(2,128)(2,1)S(1)} reshape(bf16[16,2,6400]{2,1,0:T(2,128)(2,1)} %all-to-all-done.4) | data formatting | bytes 819200
  122.4 15.7 %shard_map.91 = f32[4,512,320]{2,1,0:T(8,128)} custom-call(bf16[6,512,960]{2,1,0:T(8,128)(2,1)} %pad_maximum_fusion.x_ref, bf16[3,960,320]{2,1,0:T(8,128)(2,1)} %bitcast.55, bf16[3,960,64]{2,1,0:T(8,128)(2,1)} %reshape_reshape.3.d_ref, bf16[64,320]{1,0:T(8,128)(2,1)} %slice.80.u_ref, f32[1,320]{1,0:T(1,128)} %fusion.18.s_ref), custom_call_target="tpu_custom_call" | custom-call | flops 1593835520 | bytes 10731520 | tf_op jit(solution)/shard_map/pallas_call | solution.py:86
  143.2 11.3 %all_to_all.47 = f32[16,2,1,32]{3,2,1,0:T(1,128)S(1)} all-to-all(f32[16,2,1,32]{3,2,1,0:T(1,128)S(1)} %broadcast_in_dim.59), channel_id=1, replica_groups=mesh['band'=16,'req'=16] {'band'}, dimensions={0} | all-to-all | bytes 8192 | tf_op jit(solution)/shard_map/all_to_all | solution.py:26
  155.0 2.9 %fusion.17 = bf16[1,4,512,320]{3,2,1,0:T(8,128)(2,1)S(1)} fusion(f32[320]{0:T(512)S(1)} %mul.113, f32[4,512,320]{2,1,0:T(8,128)} %shard_map.91, f32[320]{0:T(512)S(1)} %sub.119), kind=kLoop, calls=%fused_computation.30 | loop fusion | flops 4587520 | bytes 3934720 | tf_op jit(solution)/shard_map/convert_element_type | solution.py:168
  162.7 2.5 %collective-permute-done.2 = bf16[1,1,512,320]{3,2,1,0:T(8,128)(2,1)S(1)} collective-permute-done((bf16[1,1,512,320]{3,2,1,0:T(8,128)(2,1)S(1)}, bf16[1,1,512,320]{3,2,1,0:T(8,128)(2,1)S(1)}, u32[]{:S(2)}, u32[]{:S(2)}) %collective-permute-start.2) | collective-permute-done | bytes 327712 | tf_op jit(solution)/shard_map/ppermute | solution.py:17
  165.2 5.9 %collective-permute-done.3 = bf16[1,1,512,320]{3,2,1,0:T(8,128)(2,1)S(1)} collective-permute-done((bf16[1,1,512,320]{3,2,1,0:T(8,128)(2,1)S(1)}, bf16[1,1,512,320]{3,2,1,0:T(8,128)(2,1)S(1)}, u32[]{:S(2)}, u32[]{:S(2)}) %collective-permute-start.3) | collective-permute-done | bytes 327712 | tf_op jit(solution)/shard_map/ppermute | solution.py:18
  174.0 4.8 %pad_maximum_fusion.1.x_ref = bf16[6,512,960]{2,1,0:T(8,128)(2,1)} fusion(bf16[6,512,320]{2,1,0:T(8,128)(2,1)S(1)} %get-tuple-element.8, bf16[6,512,320]{2,1,0:T(8,128)(2,1)S(1)} %get-tuple-element.9, bf16[6,512,320]{2,1,0:T(8,128)(2,1)S(1)} %get-tuple-element.7), kind=kLoop, calls=%fused_computation.5 | loop fusion | flops 17694720 | bytes 11796480 | tf_op jit(solution)/shard_map/concatenate | solution.py:55
  178.8 11.6 %shard_map.92 = bf16[4,512,320]{2,1,0:T(8,128)(2,1)} custom-call(bf16[6,512,960]{2,1,0:T(8,128)(2,1)} %pad_maximum_fusion.1.x_ref, bf16[3,960,320]{2,1,0:T(8,128)(2,1)} %bitcast.56, bf16[4,512,320]{2,1,0:T(8,128)(2,1)} %bitcast.52), custom_call_target="tpu_custom_call" | custom-call | flops 1258291200 | bytes 10362880 | tf_op jit(solution)/shard_map/pallas_call | solution.py:108
  190.4 2.5 %copy.43 = bf16[1,4,512,320]{2,3,1,0:T(8,128)(2,1)} copy(bf16[1,4,512,320]{3,2,1,0:T(8,128)(2,1)} %bitcast.54) | data formatting | bytes 2621440 | tf_op jit(solution)/shard_map/broadcast_in_dim | solution.py:174
  (99 shorter events, 50.0 us)
Async XLA Ops:
  0.0 25.5 %copy-start = (bf16[1280,320]{0,1:T(8,128)(2,1)S(1)}, bf16[1280,320]{0,1:T(8,128)(2,1)}, u32[]{:S(2)}) copy-start(bf16[1280,320]{0,1:T(8,128)(2,1)} %param.17) | copy-start | bytes 2457604
  1.3 27.7 %all-to-all-start.1 = ((s32[16,1,1]{2,1,0:T(1,128)}), s32[16,1,1]{2,1,0:T(1,128)}, u32[]{:S(2)}, u32[]{:S(2)}) async-start(s32[16,1,1]{2,1,0:T(1,128)} %broadcast_in_dim.54), calls=%async_computation.1 | async-start | bytes 16384 | tf_op jit(solution)/shard_map/all_to_all | solution.py:26
  13.4 36.1 %copy-start.2 = (bf16[1,4,512,320]{3,2,1,0:T(8,128)(2,1)}, bf16[1,4,512,320]{3,2,1,0:T(8,128)(2,1)S(1)}, u32[]{:S(2)}) copy-start(bf16[1,4,512,320]{3,2,1,0:T(8,128)(2,1)S(1)} %copy.34) | copy-start | bytes 3932164
  13.4 3.8 %copy-start.5 = (bf16[1,64,320]{2,1,0:T(8,128)(2,1)S(1)}, bf16[1,64,320]{2,1,0:T(8,128)(2,1)}, u32[]{:S(2)}) copy-start(bf16[1,64,320]{2,1,0:T(8,128)(2,1)} %param.15) | copy-start | bytes 122884
  16.8 21.5 %copy-start.1 = (s32[256]{0:T(256)S(1)}, s32[256]{0:T(256)}, u32[]{:S(2)}) copy-start(s32[256]{0:T(256)} %param.12) | copy-start | bytes 3076
  29.6 14.9 %all-to-all-start = ((f32[16,2,1,32]{3,2,1,0:T(1,128)}), f32[16,2,1,32]{3,2,1,0:T(1,128)S(1)}, u32[]{:S(2)}, u32[]{:S(2)}) async-start(f32[16,2,1,32]{3,2,1,0:T(1,128)} %broadcast_in_dim.29), calls=%async_computation | async-start | bytes 32768 | tf_op jit(solution)/shard_map/all_to_all | solution.py:26
  44.5 15.0 %all-to-all-start.2 = ((bf16[16,2,6400]{2,1,0:T(2,128)(2,1)}), bf16[16,2,6400]{2,1,0:T(2,128)(2,1)S(1)}, u32[]{:S(2)}, u32[]{:S(2)}) async-start(bf16[16,2,6400]{2,1,0:T(2,128)(2,1)} %reshape.460), calls=%async_computation.2 | async-start | bytes 819200 | tf_op jit(solution)/shard_map/all_to_all | solution.py:129
  50.4 1.2 copy-start.3
  52.5 19.1 %collective-permute-start = (bf16[1,1,512,320]{3,2,1,0:T(8,128)(2,1)}, bf16[1,1,512,320]{3,2,1,0:T(8,128)(2,1)}, u32[]{:S(2)}, u32[]{:S(2)}) collective-permute-start(bf16[1,1,512,320]{3,2,1,0:T(8,128)(2,1)} %get-tuple-element.15), channel_id=1, source_target_pairs={{0,16},{16,32},{32,48},{48,64},{64,80},{80,96},{96,112},{112,128},... | collective-permute-start | bytes 983048 | tf_op jit(solution)/shard_map/ppermute | solution.py:17
  57.6 14.0 %collective-permute-start.1 = (bf16[1,1,512,320]{3,2,1,0:T(8,128)(2,1)}, bf16[1,1,512,320]{3,2,1,0:T(8,128)(2,1)}, u32[]{:S(2)}, u32[]{:S(2)}) collective-permute-start(bf16[1,1,512,320]{3,2,1,0:T(8,128)(2,1)} %get-tuple-element.16), channel_id=1, source_target_pairs={{16,0},{32,16},{48,32},{64,48},{80,64},{96,80},{112,96},{128,112},... | collective-permute-start | bytes 983048 | tf_op jit(solution)/shard_map/ppermute | solution.py:18
  59.9 11.7 %copy-start.4 = (bf16[1,4,512,320]{3,2,1,0:T(8,128)(2,1)S(1)}, bf16[1,4,512,320]{3,2,1,0:T(8,128)(2,1)}, u32[]{:S(2)}) copy-start(bf16[1,4,512,320]{3,2,1,0:T(8,128)(2,1)} %copy-done.3) | copy-start | bytes 3932164
  64.3 18.7 %all-to-all-start.3 = ((bf16[16,2,6400]{2,1,0:T(2,128)(2,1)}), bf16[16,2,6400]{2,1,0:T(2,128)(2,1)}, u32[]{:S(2)}, u32[]{:S(2)}) async-start(bf16[16,2,6400]{2,1,0:T(2,128)(2,1)} %reshape.462), calls=%async_computation.3 | async-start | bytes 819200 | tf_op jit(solution)/shard_map/all_to_all | solution.py:131
  95.4 18.9 %all-to-all-start.4 = ((bf16[16,2,6400]{2,1,0:T(2,128)(2,1)}), bf16[16,2,6400]{2,1,0:T(2,128)(2,1)}, u32[]{:S(2)}, u32[]{:S(2)}) async-start(bf16[16,2,6400]{2,1,0:T(2,128)(2,1)} %reshape.464), calls=%async_computation.4 | async-start | bytes 819200 | tf_op jit(solution)/shard_map/all_to_all | solution.py:26
  158.0 7.2 %collective-permute-start.2 = (bf16[1,1,512,320]{3,2,1,0:T(8,128)(2,1)S(1)}, bf16[1,1,512,320]{3,2,1,0:T(8,128)(2,1)S(1)}, u32[]{:S(2)}, u32[]{:S(2)}) collective-permute-start(bf16[1,1,512,320]{3,2,1,0:T(8,128)(2,1)S(1)} %get-tuple-element.13), channel_id=1, source_target_pairs={{0,16},{16,32},{32,48},{48,64},{64,80},{80,96},{96,112},{112,128},... | collective-permute-start | bytes 983048 | tf_op jit(solution)/shard_map/ppermute | solution.py:17
  160.5 10.6 %collective-permute-start.3 = (bf16[1,1,512,320]{3,2,1,0:T(8,128)(2,1)S(1)}, bf16[1,1,512,320]{3,2,1,0:T(8,128)(2,1)S(1)}, u32[]{:S(2)}, u32[]{:S(2)}) collective-permute-start(bf16[1,1,512,320]{3,2,1,0:T(8,128)(2,1)S(1)} %get-tuple-element.14), channel_id=1, source_target_pairs={{16,0},{32,16},{48,32},{64,48},{80,64},{96,80},{112,96},{128,112},... | collective-permute-start | bytes 983048 | tf_op jit(solution)/shard_map/ppermute | solution.py:18
where the time goes:
time: 195 us; the launch traced here: 193 us
  starting transfers between devices  49.7 us (25%)
  other arithmetic  42.2 us (22%)
  local copies, waits for them, and re-layouts  38.1 us (20%)
  Pallas kernels  27.3 us (14%)
  waiting for transfers between devices  19.6 us (10%)
  blocking collectives  11.3 us (6%)
  between operations  3.18 us (2%)
    all_to_all x3, starting transfers between devices, exchange(): return lax.all_to_all(spread, axis, 0, 0, tiled=True)  26.3 us
    pallas_call x1, Pallas kernels, first_conv(): pl.pallas_call(first_conv_kernel, grid=(rows,), in_specs=[pl.BlockSpec(co...  15.7 us
    unnamed x21, local copies, waits for them, and re-layouts  15.6 us
    concatenate x2, other arithmetic, taps_by_column(): jnp.concatenate([padded[:, tap:tap + width] for tap in range(3)], axis=-1)  12.1 us
    pallas_call x1, Pallas kernels, second_conv(): pl.pallas_call(second_conv_kernel, grid=(rows,), in_specs=[pl.BlockSpec(c...  11.6 us
    all_to_all x1, blocking collectives, exchange(): return lax.all_to_all(spread, axis, 0, 0, tiled=True)  11.3 us
    ppermute x2, starting transfers between devices, with_halo(): before = lax.ppermute(last, axis, up)  7.53 us
    all_to_all x1, starting transfers between devices, fetch_adapter(): by_req = lax.all_to_all(wanted, 'req', 0, 0, tiled=True)  7.23 us
  transfers between devices with their start and end apart: 9, of which 5 were waited for; matrix products, arithmetic and copies ran while one was open for 20% of the time, Pallas kernels for 0%

commit v1 on v0

--- a/solution.py
+++ b/solution.py
@@ -125,15 +125,20 @@
 def fetch_adapter(slots, down, up):
     bands, reqs = lax.axis_size("band"), lax.axis_size("req")
     flat = jnp.concatenate([down.reshape(-1), up.reshape(-1)])
-    pieces = flat.reshape(bands, -1)
+    lanes, sublanes = 128, 16
+    piece_rows = -(-flat.size // (bands * lanes * sublanes)) * sublanes
+    flat = jnp.pad(flat, (0, bands * piece_rows * lanes - flat.size))
+    pieces = flat.reshape(bands, piece_rows, lanes)
     by_band = lax.all_to_all(pieces, "band", 0, 0, tiled=True)
     wanted = jnp.take(by_band, slots // reqs, axis=0)
     by_req = lax.all_to_all(wanted, "req", 0, 0, tiled=True)
     own = lax.axis_index("req")
-    mine = lax.dynamic_index_in_dim(by_req, slots[own] % reqs, 0, keepdims=True)
-    whole = exchange(mine[0], "band").reshape(-1)
+    mine = lax.dynamic_index_in_dim(by_req, slots[own] % reqs, 0, keepdims=False)
+    whole = exchange(mine, "band").reshape(-1)
     down_size = down.size
-    return whole[:down_size].reshape(down.shape[1:]), whole[down_size:].reshape(up.shape[1:])
+    chosen_down = whole[:down_size].reshape(down.shape[1:])
+    chosen_up = whole[down_size : down_size + up.size].reshape(up.shape[1:])
+    return chosen_down, chosen_up
 
 
 def shards(

time: 195 us -> 172 us (0.88)
  local copies, waits for them, and re-layouts: 38.1 us -> 19.6 us
  waiting for transfers between devices: 19.6 us -> 34.4 us
  other arithmetic: 42.2 us -> 28.9 us
  starting transfers between devices: 49.7 us -> 45.4 us
    unnamed x21 -> x16, local copies, waits for them, and re-layouts: 15.6 us -> 4 us
    all_to_all x1, waiting for transfers between devices: 0.01 us -> 8.15 us  [fetch_adapter(): by_band = lax.all_to_all(pieces, 'band', 0, 0, tiled=True)]
    ppermute x2, waiting for transfers between devices: 2.51 us -> 10.1 us  [with_halo(): before = lax.ppermute(last, axis, up)]
    all_to_all x1, waiting for transfers between devices: 5.34 us -> 0.01 us  [fetch_adapter(): by_req = lax.all_to_all(wanted, 'req', 0, 0, tiled=True)]
    broadcast_in_dim x1 -> x0, other arithmetic: 4.75 us -> none  [exchange(): spread = jnp.broadcast_to(value[None], (count,) + value.shape)]
    all_to_all x3, waiting for transfers between devices: 5.84 us -> 10.2 us  [exchange(): return lax.all_to_all(spread, axis, 0, 0, tiled=True)]
    all_to_all x1 -> x0, other arithmetic: 3.9 us -> none  [fetch_adapter(): by_band = lax.all_to_all(pieces, 'band', 0, 0, tiled=True)]
    all_to_all x2 -> x0, local copies, waits for them, and re-layouts: 2.91 us -> none  [fetch_adapter(): by_band = lax.all_to_all(pieces, 'band', 0, 0, tiled=True)]
  transfers between devices with their start and end apart: 9 -> 9, of which waited for: 5 -> 7; matrix products, arithmetic and copies ran while one was open for 20% -> 13% of each run, Pallas kernels for 0% -> 0%
where the time goes in v1:
time: 172 us; the launch traced here: 170 us
  starting transfers between devices  45.4 us (26%)
  waiting for transfers between devices  34.4 us (20%)
  other arithmetic  28.9 us (17%)
  Pallas kernels  27.3 us (16%)
  local copies, waits for them, and re-layouts  19.6 us (11%)
  blocking collectives  10.8 us (6%)
  between operations  2.73 us (2%)
    all_to_all x3, starting transfers between devices, exchange(): return lax.all_to_all(spread, axis, 0, 0, tiled=True)  25.4 us
    pallas_call x1, Pallas kernels, first_conv(): pl.pallas_call(first_conv_kernel, grid=(rows,), in_specs=[pl.BlockSpec(co...  15.7 us
    pallas_call x1, Pallas kernels, second_conv(): pl.pallas_call(second_conv_kernel, grid=(rows,), in_specs=[pl.BlockSpec(c...  11.6 us
    all_to_all x1, blocking collectives, exchange(): return lax.all_to_all(spread, axis, 0, 0, tiled=True)  10.8 us
    all_to_all x3, waiting for transfers between devices, exchange(): return lax.all_to_all(spread, axis, 0, 0, tiled=True)  10.2 us
    ppermute x2, waiting for transfers between devices, with_halo(): before = lax.ppermute(last, axis, up)  10.1 us
    concatenate x2, other arithmetic, taps_by_column(): jnp.concatenate([padded[:, tap:tap + width] for tap in range(3)], axis=-1)  9.63 us
    all_to_all x1, waiting for transfers between devices, fetch_adapter(): by_band = lax.all_to_all(pieces, 'band', 0, 0, tiled=True)  8.15 us
  transfers between devices with their start and end apart: 9, of which 7 were waited for; matrix products, arithmetic and copies ran while one was open for 13% of the time, Pallas kernels for 0%

profile of v1, /device:TPU:1, one launch (start us, length us, event | category | flops | bytes accessed | tf_op | source)
XLA Modules:
  0.0 170.0 jit_solution(15312925610248648978)
XLA Ops:
  1.3 10.2 %all-to-all-start.1 = ((s32[16,1,1]{2,1,0:T(1,128)}), s32[16,1,1]{2,1,0:T(1,128)}, u32[]{:S(2)}, u32[]{:S(2)}) async-start(s32[16,1,1]{2,1,0:T(1,128)} %broadcast_in_dim.57), calls=%async_computation.1 | async-start | bytes 16384 | tf_op jit(solution)/shard_map/all_to_all | solution.py:26
  19.4 8.8 %all-to-all-start = ((f32[16,2,1,32]{3,2,1,0:T(1,128)}), f32[16,2,1,32]{3,2,1,0:T(1,128)S(1)}, u32[]{:S(2)}, u32[]{:S(2)}) async-start(f32[16,2,1,32]{3,2,1,0:T(1,128)} %broadcast_in_dim.31), calls=%async_computation | async-start | bytes 32768 | tf_op jit(solution)/shard_map/all_to_all | solution.py:26
  29.9 5.5 %all-to-all-done = f32[16,2,1,32]{3,2,1,0:T(1,128)S(1)} async-done(((f32[16,2,1,32]{3,2,1,0:T(1,128)}), f32[16,2,1,32]{3,2,1,0:T(1,128)S(1)}, u32[]{:S(2)}, u32[]{:S(2)}) %all-to-all-start) | async-done | bytes 4128 | tf_op jit(solution)/shard_map/all_to_all | solution.py:26
  35.4 3.7 %all-to-all-start.2 = ((bf16[16,112,128]{2,1,0:T(8,128)(2,1)}), bf16[16,112,128]{2,1,0:T(8,128)(2,1)S(1)}, u32[]{:S(2)}, u32[]{:S(2)}) async-start(bf16[16,112,128]{2,1,0:T(8,128)(2,1)} %bitcast.10), calls=%async_computation.2 | async-start | bytes 917504 | tf_op jit(solution)/shard_map/all_to_all | solution.py:132
  41.7 8.2 %all-to-all-done.2 = bf16[16,112,128]{2,1,0:T(8,128)(2,1)S(1)} async-done(((bf16[16,112,128]{2,1,0:T(8,128)(2,1)}), bf16[16,112,128]{2,1,0:T(8,128)(2,1)S(1)}, u32[]{:S(2)}, u32[]{:S(2)}) %all-to-all-start.2) | async-done | bytes 458784 | tf_op jit(solution)/shard_map/all_to_all | solution.py:132
  51.4 6.0 %all-to-all-start.3 = ((bf16[16,112,128]{2,1,0:T(8,128)(2,1)}), bf16[16,112,128]{2,1,0:T(8,128)(2,1)}, u32[]{:S(2)}, u32[]{:S(2)}) async-start(bf16[16,112,128]{2,1,0:T(8,128)(2,1)} %broadcast_select_fusion), calls=%async_computation.3 | async-start | bytes 917504 | tf_op jit(solution)/shard_map/all_to_all | solution.py:134
  57.5 3.7 %collective-permute-start = (bf16[1,1,512,320]{3,2,1,0:T(8,128)(2,1)S(1)}, bf16[1,1,512,320]{3,2,1,0:T(8,128)(2,1)S(1)}, u32[]{:S(2)}, u32[]{:S(2)}) collective-permute-start(bf16[1,1,512,320]{3,2,1,0:T(8,128)(2,1)S(1)} %get-tuple-element.15), channel_id=1, source_target_pairs={{0,16},{16,32},{32,48},{48,64},{64,80},{80,96},{96,112},{112,128},... | collective-permute-start | bytes 983048 | tf_op jit(solution)/shard_map/ppermute | solution.py:17
  66.3 7.5 %collective-permute-done = bf16[1,1,512,320]{3,2,1,0:T(8,128)(2,1)S(1)} collective-permute-done((bf16[1,1,512,320]{3,2,1,0:T(8,128)(2,1)S(1)}, bf16[1,1,512,320]{3,2,1,0:T(8,128)(2,1)S(1)}, u32[]{:S(2)}, u32[]{:S(2)}) %collective-permute-start) | collective-permute-done | bytes 327712 | tf_op jit(solution)/shard_map/ppermute | solution.py:17
  74.6 2.8 %fusion.16 = bf16[6,514,320]{2,1,0:T(8,128)(2,1)S(1)} fusion(bf16[1,1,512,320]{3,2,1,0:T(8,128)(2,1)} %collective-permute-done.1, bf16[1,4,512,320]{3,2,1,0:T(8,128)(2,1)} %fusion.9, bf16[1,1,512,320]{3,2,1,0:T(8,128)(2,1)} %copy-done.4), kind=kLoop, calls=%fused_computation.29 | loop fusion | flops 11842560 | bytes 3939840 | tf_op jit(solution)/shard_map/squeeze | solution.py:167
  79.0 6.5 %all-to-all-start.4 = ((bf16[16,112,128]{2,1,0:T(8,128)(2,1)}), bf16[16,112,128]{2,1,0:T(8,128)(2,1)}, u32[]{:S(2)}, u32[]{:S(2)}) async-start(bf16[16,112,128]{2,1,0:T(8,128)(2,1)} %broadcast_in_dim.61), calls=%async_computation.4 | async-start | bytes 917504 | tf_op jit(solution)/shard_map/all_to_all | solution.py:26
  86.8 4.8 %pad_maximum_fusion.x_ref = bf16[6,512,960]{2,1,0:T(8,128)(2,1)} fusion(bf16[6,512,320]{2,1,0:T(8,128)(2,1)S(1)} %get-tuple-element.11, bf16[6,512,320]{2,1,0:T(8,128)(2,1)S(1)} %get-tuple-element.12, bf16[6,512,320]{2,1,0:T(8,128)(2,1)S(1)} %get-tuple-element.10), kind=kLoop, calls=%fused_computation.4 | loop fusion | flops 17694720 | bytes 11796480 | tf_op jit(solution)/shard_map/concatenate | solution.py:55
  91.6 4.7 %all-to-all-done.4 = bf16[16,112,128]{2,1,0:T(8,128)(2,1)} async-done(((bf16[16,112,128]{2,1,0:T(8,128)(2,1)}), bf16[16,112,128]{2,1,0:T(8,128)(2,1)}, u32[]{:S(2)}, u32[]{:S(2)}) %all-to-all-start.4) | async-done | bytes 458784 | tf_op jit(solution)/shard_map/all_to_all | solution.py:26
  100.0 15.7 %shard_map.91 = f32[4,512,320]{2,1,0:T(8,128)} custom-call(bf16[6,512,960]{2,1,0:T(8,128)(2,1)} %pad_maximum_fusion.x_ref, bf16[3,960,320]{2,1,0:T(8,128)(2,1)} %bitcast.53, bf16[3,960,64]{2,1,0:T(8,128)(2,1)} %reshape_reshape.3.d_ref, bf16[64,320]{1,0:T(8,128)(2,1)} %reshape.399.u_ref, f32[1,320]{1,0:T(1,128)} %fusion.21.s_ref), custom_call_target="tpu_custom_call" | custom-call | flops 1593835520 | bytes 10731520 | tf_op jit(solution)/shard_map/pallas_call | solution.py:86
  115.7 2.2 %reduce_sum.127 = f32[320]{0:T(512)S(1)} reduce(f32[4,512,320]{2,1,0:T(8,128)} %shard_map.91, f32[]{:T(128)} %constant.69.clone.1), dimensions={0,1}, to_apply=%region_7.8 | reduce | flops 655040 | bytes 2622724 | tf_op jit(solution)/shard_map/reduce_sum | solution.py:33
  118.3 2.3 %multiply_reduce_fusion = f32[320]{0:T(512)S(1)} fusion(f32[4,512,320]{2,1,0:T(8,128)} %shard_map.91, f32[320]{0:T(512)S(1)} %sub.115), kind=kLoop, calls=%fused_computation.20 | loop fusion | flops 1965760 | bytes 2624000 | tf_op jit(solution)/shard_map/reduce_sum | solution.py:35
  120.9 10.8 %all_to_all.37 = f32[16,2,1,32]{3,2,1,0:T(1,128)S(1)} all-to-all(f32[16,2,1,32]{3,2,1,0:T(1,128)S(1)} %broadcast_in_dim.63), channel_id=1, replica_groups=mesh['band'=16,'req'=16] {'band'}, dimensions={0} | all-to-all | bytes 8192 | tf_op jit(solution)/shard_map/all_to_all | solution.py:26
  132.1 2.9 %fusion.17 = bf16[1,4,512,320]{3,2,1,0:T(8,128)(2,1)S(1)} fusion(f32[320]{0:T(512)S(1)} %mul.113, f32[4,512,320]{2,1,0:T(8,128)} %shard_map.91, f32[320]{0:T(512)S(1)} %sub.119), kind=kLoop, calls=%fused_computation.30 | loop fusion | flops 4587520 | bytes 3934720 | tf_op jit(solution)/shard_map/convert_element_type | solution.py:173
  135.1 2.5 %collective-permute-start.2 = (bf16[1,1,512,320]{3,2,1,0:T(8,128)(2,1)S(1)}, bf16[1,1,512,320]{3,2,1,0:T(8,128)(2,1)S(1)}, u32[]{:S(2)}, u32[]{:S(2)}) collective-permute-start(bf16[1,1,512,320]{3,2,1,0:T(8,128)(2,1)S(1)} %get-tuple-element.13), channel_id=1, source_target_pairs={{0,16},{16,32},{32,48},{48,64},{64,80},{80,96},{96,112},{112,128},... | collective-permute-start | bytes 983048 | tf_op jit(solution)/shard_map/ppermute | solution.py:17
  137.6 2.1 %collective-permute-start.3 = (bf16[1,1,512,320]{3,2,1,0:T(8,128)(2,1)S(1)}, bf16[1,1,512,320]{3,2,1,0:T(8,128)(2,1)S(1)}, u32[]{:S(2)}, u32[]{:S(2)}) collective-permute-start(bf16[1,1,512,320]{3,2,1,0:T(8,128)(2,1)S(1)} %get-tuple-element.14), channel_id=1, source_target_pairs={{16,0},{32,16},{48,32},{64,48},{80,64},{96,80},{112,96},{128,112},... | collective-permute-start | bytes 983048 | tf_op jit(solution)/shard_map/ppermute | solution.py:18
  139.8 2.6 %collective-permute-done.2 = bf16[1,1,512,320]{3,2,1,0:T(8,128)(2,1)S(1)} collective-permute-done((bf16[1,1,512,320]{3,2,1,0:T(8,128)(2,1)S(1)}, bf16[1,1,512,320]{3,2,1,0:T(8,128)(2,1)S(1)}, u32[]{:S(2)}, u32[]{:S(2)}) %collective-permute-start.2) | collective-permute-done | bytes 327712 | tf_op jit(solution)/shard_map/ppermute | solution.py:17
  142.3 5.9 %collective-permute-done.3 = bf16[1,1,512,320]{3,2,1,0:T(8,128)(2,1)S(1)} collective-permute-done((bf16[1,1,512,320]{3,2,1,0:T(8,128)(2,1)S(1)}, bf16[1,1,512,320]{3,2,1,0:T(8,128)(2,1)S(1)}, u32[]{:S(2)}, u32[]{:S(2)}) %collective-permute-start.3) | collective-permute-done | bytes 327712 | tf_op jit(solution)/shard_map/ppermute | solution.py:18
  151.1 4.8 %pad_maximum_fusion.1.x_ref = bf16[6,512,960]{2,1,0:T(8,128)(2,1)} fusion(bf16[6,512,320]{2,1,0:T(8,128)(2,1)S(1)} %get-tuple-element.8, bf16[6,512,320]{2,1,0:T(8,128)(2,1)S(1)} %get-tuple-element.9, bf16[6,512,320]{2,1,0:T(8,128)(2,1)S(1)} %get-tuple-element.7), kind=kLoop, calls=%fused_computation.5 | loop fusion | flops 17694720 | bytes 11796480 | tf_op jit(solution)/shard_map/concatenate | solution.py:55
  155.9 11.6 %shard_map.92 = bf16[4,512,320]{2,1,0:T(8,128)(2,1)} custom-call(bf16[6,512,960]{2,1,0:T(8,128)(2,1)} %pad_maximum_fusion.1.x_ref, bf16[3,960,320]{2,1,0:T(8,128)(2,1)} %bitcast.54, bf16[4,512,320]{2,1,0:T(8,128)(2,1)} %bitcast.51), custom_call_target="tpu_custom_call" | custom-call | flops 1258291200 | bytes 10362880 | tf_op jit(solution)/shard_map/pallas_call | solution.py:108
  167.5 2.5 %copy.36 = bf16[1,4,512,320]{2,3,1,0:T(8,128)(2,1)} copy(bf16[1,4,512,320]{3,2,1,0:T(8,128)(2,1)} %bitcast.52) | data formatting | bytes 2621440 | tf_op jit(solution)/shard_map/broadcast_in_dim | solution.py:179
  (87 shorter events, 29.1 us)
Async XLA Ops:
  0.0 63.2 %copy-start = (bf16[1280,320]{0,1:T(8,128)(2,1)S(1)}, bf16[1280,320]{0,1:T(8,128)(2,1)}, u32[]{:S(2)}) copy-start(bf16[1280,320]{0,1:T(8,128)(2,1)} %param.17) | copy-start | bytes 2457604
  1.3 17.4 %all-to-all-start.1 = ((s32[16,1,1]{2,1,0:T(1,128)}), s32[16,1,1]{2,1,0:T(1,128)}, u32[]{:S(2)}, u32[]{:S(2)}) async-start(s32[16,1,1]{2,1,0:T(1,128)} %broadcast_in_dim.57), calls=%async_computation.1 | async-start | bytes 16384 | tf_op jit(solution)/shard_map/all_to_all | solution.py:26
  13.4 26.3 %copy-start.2 = (bf16[1,4,512,320]{3,2,1,0:T(8,128)(2,1)}, bf16[1,4,512,320]{3,2,1,0:T(8,128)(2,1)S(1)}, u32[]{:S(2)}) copy-start(bf16[1,4,512,320]{3,2,1,0:T(8,128)(2,1)S(1)} %copy.29) | copy-start | bytes 3932164
  13.4 3.7 %copy-start.5 = (bf16[1,64,320]{2,1,0:T(8,128)(2,1)S(1)}, bf16[1,64,320]{2,1,0:T(8,128)(2,1)}, u32[]{:S(2)}) copy-start(bf16[1,64,320]{2,1,0:T(8,128)(2,1)} %param.15) | copy-start | bytes 122884
  13.4 15.8 %copy-start.1 = (s32[256]{0:T(256)S(1)}, s32[256]{0:T(256)}, u32[]{:S(2)}) copy-start(s32[256]{0:T(256)} %param.12) | copy-start | bytes 3076
  19.4 16.1 %all-to-all-start = ((f32[16,2,1,32]{3,2,1,0:T(1,128)}), f32[16,2,1,32]{3,2,1,0:T(1,128)S(1)}, u32[]{:S(2)}, u32[]{:S(2)}) async-start(f32[16,2,1,32]{3,2,1,0:T(1,128)} %broadcast_in_dim.31), calls=%async_computation | async-start | bytes 32768 | tf_op jit(solution)/shard_map/all_to_all | solution.py:26
  35.4 14.5 %all-to-all-start.2 = ((bf16[16,112,128]{2,1,0:T(8,128)(2,1)}), bf16[16,112,128]{2,1,0:T(8,128)(2,1)S(1)}, u32[]{:S(2)}, u32[]{:S(2)}) async-start(bf16[16,112,128]{2,1,0:T(8,128)(2,1)} %bitcast.10), calls=%async_computation.2 | async-start | bytes 917504 | tf_op jit(solution)/shard_map/all_to_all | solution.py:132
  39.6 23.6 %copy-start.6 = (bf16[1,1280]{1,0:T(2,128)(2,1)S(1)}, bf16[1,1280]{1,0:T(2,128)(2,1)}, u32[]{:S(2)}) copy-start(bf16[1,1280]{1,0:T(2,128)(2,1)} %param.10) | copy-start | bytes 7684
  41.7 15.7 %copy-start.3 = (bf16[1,4,512,320]{3,2,1,0:T(8,128)(2,1)S(1)}, bf16[1,4,512,320]{3,2,1,0:T(8,128)(2,1)}, u32[]{:S(2)}) copy-start(bf16[1,4,512,320]{3,2,1,0:T(8,128)(2,1)} %fusion.9) | copy-start | bytes 3932164
  51.4 26.0 %all-to-all-start.3 = ((bf16[16,112,128]{2,1,0:T(8,128)(2,1)}), bf16[16,112,128]{2,1,0:T(8,128)(2,1)}, u32[]{:S(2)}, u32[]{:S(2)}) async-start(bf16[16,112,128]{2,1,0:T(8,128)(2,1)} %broadcast_select_fusion), calls=%async_computation.3 | async-start | bytes 917504 | tf_op jit(solution)/shard_map/all_to_all | solution.py:134
  57.5 16.3 %collective-permute-start = (bf16[1,1,512,320]{3,2,1,0:T(8,128)(2,1)S(1)}, bf16[1,1,512,320]{3,2,1,0:T(8,128)(2,1)S(1)}, u32[]{:S(2)}, u32[]{:S(2)}) collective-permute-start(bf16[1,1,512,320]{3,2,1,0:T(8,128)(2,1)S(1)} %get-tuple-element.15), channel_id=1, source_target_pairs={{0,16},{16,32},{32,48},{48,64},{64,80},{80,96},{96,112},{112,128},... | collective-permute-start | bytes 983048 | tf_op jit(solution)/shard_map/ppermute | solution.py:17
  61.3 13.3 %collective-permute-start.1 = (bf16[1,1,512,320]{3,2,1,0:T(8,128)(2,1)S(1)}, bf16[1,1,512,320]{3,2,1,0:T(8,128)(2,1)}, u32[]{:S(2)}, u32[]{:S(2)}) collective-permute-start(bf16[1,1,512,320]{3,2,1,0:T(8,128)(2,1)S(1)} %get-tuple-element.16), channel_id=1, source_target_pairs={{16,0},{32,16},{48,32},{64,48},{80,64},{96,80},{112,96},{128,112},... | collective-permute-start | bytes 983048 | tf_op jit(solution)/shard_map/ppermute | solution.py:18
  73.9 0.7 copy-start.4
  79.0 17.3 %all-to-all-start.4 = ((bf16[16,112,128]{2,1,0:T(8,128)(2,1)}), bf16[16,112,128]{2,1,0:T(8,128)(2,1)}, u32[]{:S(2)}, u32[]{:S(2)}) async-start(bf16[16,112,128]{2,1,0:T(8,128)(2,1)} %broadcast_in_dim.61), calls=%async_computation.4 | async-start | bytes 917504 | tf_op jit(solution)/shard_map/all_to_all | solution.py:26
  135.1 7.2 %collective-permute-start.2 = (bf16[1,1,512,320]{3,2,1,0:T(8,128)(2,1)S(1)}, bf16[1,1,512,320]{3,2,1,0:T(8,128)(2,1)S(1)}, u32[]{:S(2)}, u32[]{:S(2)}) collective-permute-start(bf16[1,1,512,320]{3,2,1,0:T(8,128)(2,1)S(1)} %get-tuple-element.13), channel_id=1, source_target_pairs={{0,16},{16,32},{32,48},{48,64},{64,80},{80,96},{96,112},{112,128},... | collective-permute-start | bytes 983048 | tf_op jit(solution)/shard_map/ppermute | solution.py:17
  137.6 10.6 %collective-permute-start.3 = (bf16[1,1,512,320]{3,2,1,0:T(8,128)(2,1)S(1)}, bf16[1,1,512,320]{3,2,1,0:T(8,128)(2,1)S(1)}, u32[]{:S(2)}, u32[]{:S(2)}) collective-permute-start(bf16[1,1,512,320]{3,2,1,0:T(8,128)(2,1)S(1)} %get-tuple-element.14), channel_id=1, source_target_pairs={{16,0},{32,16},{48,32},{64,48},{80,64},{96,80},{112,96},{128,112},... | collective-permute-start | bytes 983048 | tf_op jit(solution)/shard_map/ppermute | solution.py:18

commit v2 on v1

--- a/solution.py
+++ b/solution.py
@@ -26,7 +26,8 @@
     return lax.all_to_all(spread, axis, 0, 0, tiled=True)
 
 
-def group_norm(field, groups):
+def norm_stats(field, groups):
+    field = field.astype(jnp.float32)
     requests, rows, width, channels = field.shape
     grouped = field.reshape(requests, rows, width, groups, channels // groups)
     count = rows * width * (channels // groups)
@@ -40,14 +41,26 @@
     gap = means - mean[None]
     m2 = jnp.sum(m2s, axis=0) + count * jnp.sum(gap * gap, axis=0)
     spread = m2 / (count * bands)
-    centered = grouped - mean[:, None, None, :, None]
-    normed = centered * lax.rsqrt(spread + 1e-05)[:, None, None, :, None]
-    return normed.reshape(field.shape)
-
-
-def padded_field(field):
+    return mean, lax.rsqrt(spread + 1e-05)
+
+
+def norm_silu(field, mean, scale, groups):
+    field = field.astype(jnp.float32)
+    requests, rows, width, channels = field.shape
+    grouped = field.reshape(requests, rows, width, groups, channels // groups)
+    normed = (grouped - mean[:, None, None, :, None]) * scale[:, None, None, :, None]
+    return jax.nn.silu(normed.reshape(field.shape)).astype(jnp.bfloat16)
+
+
+def conv_input(field, groups):
     extended = with_halo(field, (("band", 1),), 1)
-    return jnp.pad(extended, ((0, 0), (0, 0), (1, 1), (0, 0)))
+    mean, scale = norm_stats(field, groups)
+    normed = norm_silu(extended, mean, scale, groups)
+    band, bands = lax.axis_index("band"), lax.axis_size("band")
+    row = lax.broadcasted_iota(jnp.int32, (1, normed.shape[1], 1, 1), 1)
+    outside = ((row == 0) & (band == 0)) | ((row == normed.shape[1] - 1) & (band == bands - 1))
+    normed = jnp.where(outside, jnp.zeros((), normed.dtype), normed)
+    return jnp.pad(normed, ((0, 0), (0, 0), (1, 1), (0, 0)))
 
 
 def taps_by_column(padded):
@@ -55,16 +68,15 @@
     return jnp.concatenate([padded[:, tap : tap + width] for tap in range(3)], axis=-1)
 
 
-def first_conv_kernel(x_ref, w_ref, d_ref, u_ref, s_ref, o_ref):
+def first_conv_kernel(x_ref, w_ref, u_ref, s_ref, o_ref):
     row = pl.program_id(0)
-    main = None
-    low = None
+    total = None
     for tap in range(3):
-        piece = x_ref[row + tap]
-        m = jnp.dot(piece, w_ref[tap], preferred_element_type=jnp.float32)
-        l = jnp.dot(piece, d_ref[tap], preferred_element_type=jnp.float32)
-        main = m if main is None else main + m
-        low = l if low is None else low + l
+        t = jnp.dot(x_ref[row + tap], w_ref[tap], preferred_element_type=jnp.float32)
+        total = t if total is None else total + t
+    rank = u_ref.shape[0]
+    low = total[:, :rank]
+    main = total[:, w_ref.shape[-1] - o_ref.shape[-1] :]
     lifted = jnp.dot(low.astype(jnp.bfloat16), u_ref[...], preferred_element_type=jnp.float32)
     o_ref[0] = main + lifted + s_ref[...]
 
@@ -82,14 +94,16 @@
     rows, width, wide = cols.shape[0] - 2, cols.shape[1], cols.shape[2]
     out = weight.shape[-1]
     rank = down.shape[-1]
-    flops = 2 * rows * width * wide * (out + rank) + 2 * rows * width * rank * out
+    lead = -(-rank // 128) * 128
+    gap = jnp.zeros(down.shape[:-1] + (lead - rank,), down.dtype)
+    weight = jnp.concatenate([down, gap, weight], axis=-1)
+    flops = 2 * rows * width * wide * (out + lead) + 2 * rows * width * rank * out
     return pl.pallas_call(
         first_conv_kernel,
         grid=(rows,),
         in_specs=[
             pl.BlockSpec(cols.shape, lambda h: (0, 0, 0)),
             pl.BlockSpec(weight.shape, lambda h: (0, 0, 0)),
-            pl.BlockSpec(down.shape, lambda h: (0, 0, 0)),
             pl.BlockSpec(up.shape, lambda h: (0, 0)),
             pl.BlockSpec(shift.shape, lambda h: (0, 0)),
         ],
@@ -97,9 +111,9 @@
         out_shape=jax.ShapeDtypeStruct((rows, width, out), jnp.float32),
         cost_estimate=pl.CostEstimate(
             flops=flops, transcendentals=0,
-            bytes_accessed=cols.size * 2 + weight.size * 2 + down.size * 2 + rows * width * out * 4,
+            bytes_accessed=cols.size * 2 + weight.size * 2 + rows * width * out * 4,
         ),
-    )(cols, weight, down, up, shift)
+    )(cols, weight, up, shift)
 
 
 def second_conv(cols, weight, residual):
@@ -161,18 +175,16 @@
         time_projection_weight,
         preferred_element_type=jnp.float32,
     )
-    first = jax.nn.silu(group_norm(latents.astype(jnp.float32), G)).astype(jnp.bfloat16)
     wide = 3 * channels
     hidden = first_conv(
-        taps_by_column(padded_field(first)[0]),
+        taps_by_column(conv_input(latents, G)[0]),
         first_conv_weight.reshape(3, wide, channels),
         chosen_down.reshape(3, wide, chosen_down.shape[-1]),
         chosen_up,
         shift,
     )[None]
-    second = jax.nn.silu(group_norm(hidden, G)).astype(jnp.bfloat16)
     result = second_conv(
-        taps_by_column(padded_field(second)[0]),
+        taps_by_column(conv_input(hidden, G)[0]),
         second_conv_weight.reshape(3, wide, channels),
         latents[0],
     )

time: 172 us -> 175 us (1.017)
  blocking collectives: 10.8 us -> 0 us
  starting transfers between devices: 45.4 us -> 53.8 us
  waiting for transfers between devices: 34.4 us -> 39.8 us
  Pallas kernels: 27.3 us -> 24 us
  local copies, waits for them, and re-layouts: 19.6 us -> 22.2 us
    all_to_all x1 -> x0, blocking collectives: 10.8 us -> none  [exchange(): return lax.all_to_all(spread, axis, 0, 0, tiled=True)]
    all_to_all x1, waiting for transfers between devices: 0.01 us -> 8.69 us  [fetch_adapter(): by_req = lax.all_to_all(wanted, 'req', 0, 0, tiled=True)]
    select_n x0 -> x2, other arithmetic: none -> 5.6 us  [conv_input(): normed = jnp.where(outside, jnp.zeros((), normed.dtype), normed)]
    convert_element_type x2 -> x0, other arithmetic: 5 us -> none  [the longest x1 2.91 us: shards(): second = jax.nn.silu(group_norm(hidden, G)).astype(jnp.bfloat16)]
    squeeze x2 -> x0, other arithmetic: 4.34 us -> none  [the longest x1 2.82 us: shards(): padded_field(first)[0]]
    pallas_call x1, Pallas kernels: 15.7 us -> 12.3 us  [first_conv(): pl.pallas_call(first_conv_kernel, grid=(rows,), in_specs=[pl.BlockSpec(co...]
    ppermute x2, starting transfers between devices: 4.06 us -> 7.41 us  [with_halo(): after = lax.ppermute(initial, axis, down)]
    ppermute x2, waiting for transfers between devices: 10.1 us -> 7.11 us  [with_halo(): before = lax.ppermute(last, axis, up)]
  transfers between devices with their start and end apart: 9 -> 10, of which waited for: 7 -> 6; matrix products, arithmetic and copies ran while one was open for 13% -> 15% of each run, Pallas kernels for 0% -> 0%
where the time goes in v2:
time: 175 us; the launch traced here: 174 us
  starting transfers between devices  53.8 us (31%)
  waiting for transfers between devices  39.8 us (23%)
  other arithmetic  29.2 us (17%)
  Pallas kernels  24 us (14%)
  local copies, waits for them, and re-layouts  22.2 us (13%)
  between operations  2.95 us (2%)
    all_to_all x4, starting transfers between devices, exchange(): return lax.all_to_all(spread, axis, 0, 0, tiled=True)  27.9 us
    pallas_call x1, Pallas kernels, first_conv(): pl.pallas_call(first_conv_kernel, grid=(rows,), in_specs=[pl.BlockSpec(co...  12.3 us
    pallas_call x1, Pallas kernels, second_conv(): pl.pallas_call(second_conv_kernel, grid=(rows,), in_specs=[pl.BlockSpec(c...  11.7 us
    all_to_all x1, waiting for transfers between devices, fetch_adapter(): by_band = lax.all_to_all(pieces, 'band', 0, 0, tiled=True)  10.3 us
    concatenate x2, other arithmetic, taps_by_column(): jnp.concatenate([padded[:, tap:tap + width] for tap in range(3)], axis=-1)  9.62 us
    all_to_all x1, waiting for transfers between devices, fetch_adapter(): by_req = lax.all_to_all(wanted, 'req', 0, 0, tiled=True)  8.69 us
    all_to_all x4, waiting for transfers between devices, exchange(): return lax.all_to_all(spread, axis, 0, 0, tiled=True)  8.15 us
    ppermute x2, starting transfers between devices, with_halo(): before = lax.ppermute(last, axis, up)  7.77 us
  transfers between devices with their start and end apart: 10, of which 6 were waited for; matrix products, arithmetic and copies ran while one was open for 15% of the time, Pallas kernels for 0%

profile of v2, /device:TPU:1, one launch (start us, length us, event | category | flops | bytes accessed | tf_op | source)
XLA Modules:
  0.0 173.5 jit_solution(15472107951979134059)
XLA Ops:
  3.0 5.1 %collective-permute-start.1 = (bf16[1,1,512,320]{3,2,1,0:T(8,128)(2,1)}, bf16[1,1,512,320]{3,2,1,0:T(8,128)(2,1)}, u32[]{:S(2)}, u32[]{:S(2)}) collective-permute-start(bf16[1,1,512,320]{3,2,1,0:T(8,128)(2,1)} %get-tuple-element.16), channel_id=1, source_target_pairs={{16,0},{32,16},{48,32},{64,48},{80,64},{96,80},{112,96},{128,112},... | collective-permute-start | bytes 983048 | tf_op jit(solution)/shard_map/ppermute | solution.py:18
  8.1 3.0 %collective-permute-start = (bf16[1,1,512,320]{3,2,1,0:T(8,128)(2,1)}, bf16[1,1,512,320]{3,2,1,0:T(8,128)(2,1)}, u32[]{:S(2)}, u32[]{:S(2)}) collective-permute-start(bf16[1,1,512,320]{3,2,1,0:T(8,128)(2,1)} %get-tuple-element.15), channel_id=1, source_target_pairs={{0,16},{16,32},{32,48},{48,64},{64,80},{80,96},{96,112},{112,128},... | collective-permute-start | bytes 983048 | tf_op jit(solution)/shard_map/ppermute | solution.py:17
  12.4 9.1 %all-to-all-start.1 = ((s32[16,1,1]{2,1,0:T(1,128)}), s32[16,1,1]{2,1,0:T(1,128)S(1)}, u32[]{:S(2)}, u32[]{:S(2)}) async-start(s32[16,1,1]{2,1,0:T(1,128)} %broadcast_in_dim.81), calls=%async_computation.1 | async-start | bytes 16384 | tf_op jit(solution)/shard_map/all_to_all | solution.py:26
  31.7 7.7 %all-to-all-start = ((f32[16,2,1,32]{3,2,1,0:T(1,128)}), f32[16,2,1,32]{3,2,1,0:T(1,128)S(1)}, u32[]{:S(2)}, u32[]{:S(2)}) async-start(f32[16,2,1,32]{3,2,1,0:T(1,128)} %broadcast_in_dim.79), calls=%async_computation | async-start | bytes 32768 | tf_op jit(solution)/shard_map/all_to_all | solution.py:26
  43.1 3.6 %all-to-all-done = f32[16,2,1,32]{3,2,1,0:T(1,128)S(1)} async-done(((f32[16,2,1,32]{3,2,1,0:T(1,128)}), f32[16,2,1,32]{3,2,1,0:T(1,128)S(1)}, u32[]{:S(2)}, u32[]{:S(2)}) %all-to-all-start) | async-done | bytes 4128 | tf_op jit(solution)/shard_map/all_to_all | solution.py:26
  46.7 3.7 %all-to-all-start.2 = ((bf16[16,112,128]{2,1,0:T(8,128)(2,1)}), bf16[16,112,128]{2,1,0:T(8,128)(2,1)S(1)}, u32[]{:S(2)}, u32[]{:S(2)}) async-start(bf16[16,112,128]{2,1,0:T(8,128)(2,1)} %bitcast.9), calls=%async_computation.2 | async-start | bytes 917504 | tf_op jit(solution)/shard_map/all_to_all | solution.py:146
  50.9 10.3 %all-to-all-done.2 = bf16[16,112,128]{2,1,0:T(8,128)(2,1)S(1)} async-done(((bf16[16,112,128]{2,1,0:T(8,128)(2,1)}), bf16[16,112,128]{2,1,0:T(8,128)(2,1)S(1)}, u32[]{:S(2)}, u32[]{:S(2)}) %all-to-all-start.2) | async-done | bytes 458784 | tf_op jit(solution)/shard_map/all_to_all | solution.py:146
  62.7 7.0 %all-to-all-start.3 = ((bf16[16,112,128]{2,1,0:T(8,128)(2,1)}), bf16[16,112,128]{2,1,0:T(8,128)(2,1)S(1)}, u32[]{:S(2)}, u32[]{:S(2)}) async-start(bf16[16,112,128]{2,1,0:T(8,128)(2,1)} %broadcast_select_fusion), calls=%async_computation.3 | async-start | bytes 917504 | tf_op jit(solution)/shard_map/all_to_all | solution.py:148
  69.7 2.6 %fusion.3 = bf16[1,6,512,320]{3,2,1,0:T(8,128)(2,1)S(1)} fusion(bf16[1,1,512,320]{3,2,1,0:T(8,128)(2,1)} %collective-permute-done.1, bf16[1,4,512,320]{3,2,1,0:T(8,128)(2,1)S(1)} %copy.51, bf16[1,1,512,320]{3,2,1,0:T(8,128)(2,1)} %collective-permute-done, f32[320]{0:T(512)S(1)} %mul.131, f32[320]{0:T(512)S(1)} %sub.121, pred[6]{0:T(512)(128)(4,1)S(1)} %and_or_fusion), kind=kLoop, calls=%fused_computation.16 | loop fusion | flops 10813440 | bytes 3934726 | tf_op jit(solution)/shard_map/jit(_where)/select_n | solution.py:62
  73.0 8.7 %all-to-all-done.3 = bf16[16,112,128]{2,1,0:T(8,128)(2,1)S(1)} async-done(((bf16[16,112,128]{2,1,0:T(8,128)(2,1)}), bf16[16,112,128]{2,1,0:T(8,128)(2,1)S(1)}, u32[]{:S(2)}, u32[]{:S(2)}) %all-to-all-start.3) | async-done | bytes 458784 | tf_op jit(solution)/shard_map/all_to_all | solution.py:148
  82.5 6.9 %all-to-all-start.4 = ((bf16[16,112,128]{2,1,0:T(8,128)(2,1)}), bf16[16,112,128]{2,1,0:T(8,128)(2,1)S(1)}, u32[]{:S(2)}, u32[]{:S(2)}) async-start(bf16[16,112,128]{2,1,0:T(8,128)(2,1)} %broadcast_in_dim.85), calls=%async_computation.4 | async-start | bytes 917504 | tf_op jit(solution)/shard_map/all_to_all | solution.py:26
  90.6 4.8 %pad_maximum_fusion.x_ref = bf16[6,512,960]{2,1,0:T(8,128)(2,1)} fusion(bf16[6,512,320]{2,1,0:T(8,128)(2,1)S(1)} %get-tuple-element.13, bf16[6,512,320]{2,1,0:T(8,128)(2,1)S(1)} %get-tuple-element.14, bf16[6,512,320]{2,1,0:T(8,128)(2,1)S(1)} %get-tuple-element.12), kind=kLoop, calls=%fused_computation.2 | loop fusion | flops 17694720 | bytes 11796480 | tf_op jit(solution)/shard_map/concatenate | solution.py:68
  95.5 4.6 %all-to-all-done.4 = bf16[16,112,128]{2,1,0:T(8,128)(2,1)S(1)} async-done(((bf16[16,112,128]{2,1,0:T(8,128)(2,1)}), bf16[16,112,128]{2,1,0:T(8,128)(2,1)S(1)}, u32[]{:S(2)}, u32[]{:S(2)}) %all-to-all-start.4) | async-done | bytes 458784 | tf_op jit(solution)/shard_map/all_to_all | solution.py:26
  103.3 12.3 %shard_map.91 = f32[4,512,320]{2,1,0:T(8,128)} custom-call(bf16[6,512,960]{2,1,0:T(8,128)(2,1)} %pad_maximum_fusion.x_ref, bf16[3,960,448]{2,1,0:T(8,128)(2,1)} %pad_maximum_fusion.2.w_ref, bf16[64,320]{1,0:T(8,128)(2,1)} %reshape.610.u_ref, f32[1,320]{1,0:T(1,128)} %fusion.8.s_ref), custom_call_target="tpu_custom_call" | custom-call | flops 1845493760 | bytes 11100160 | tf_op jit(solution)/shard_map/pallas_call | solution.py:101
  118.2 2.3 %multiply_reduce_fusion = f32[320]{0:T(512)S(1)} fusion(f32[4,512,320]{2,1,0:T(8,128)} %shard_map.91, f32[320]{0:T(512)S(1)} %sub.129), kind=kLoop, calls=%fused_computation.10 | loop fusion | flops 1965760 | bytes 2624000 | tf_op jit(solution)/shard_map/reduce_sum | solution.py:36
  121.4 4.3 %all-to-all-start.5 = ((f32[16,2,1,32]{3,2,1,0:T(1,128)}), f32[16,2,1,32]{3,2,1,0:T(1,128)S(1)}, u32[]{:S(2)}, u32[]{:S(2)}) async-start(f32[16,2,1,32]{3,2,1,0:T(1,128)} %broadcast_in_dim.89), calls=%async_computation.5 | async-start | bytes 32768 | tf_op jit(solution)/shard_map/all_to_all | solution.py:26
  127.4 2.3 %collective-permute-start.3 = (f32[1,1,512,320]{2,3,1,0:T(8,128)S(1)}, f32[1,1,512,320]{2,3,1,0:T(8,128)S(1)}, u32[]{:S(2)}, u32[]{:S(2)}) collective-permute-start(f32[1,1,512,320]{2,3,1,0:T(8,128)S(1)} %copy.58), channel_id=1, source_target_pairs={{16,0},{32,16},{48,32},{64,48},{80,64},{96,80},{112,96},{128,112},... | collective-permute-start | bytes 1966088 | tf_op jit(solution)/shard_map/ppermute | solution.py:18
  130.0 4.8 %collective-permute-start.2 = (f32[1,1,512,320]{2,3,1,0:T(8,128)S(1)}, f32[1,1,512,320]{2,3,1,0:T(8,128)}, u32[]{:S(2)}, u32[]{:S(2)}) collective-permute-start(f32[1,1,512,320]{2,3,1,0:T(8,128)S(1)} %copy.57), channel_id=1, source_target_pairs={{0,16},{16,32},{32,48},{48,64},{64,80},{80,96},{96,112},{112,128},... | collective-permute-start | bytes 1966088 | tf_op jit(solution)/shard_map/ppermute | solution.py:17
  135.3 5.6 %collective-permute-done.3 = f32[1,1,512,320]{2,3,1,0:T(8,128)S(1)} collective-permute-done((f32[1,1,512,320]{2,3,1,0:T(8,128)S(1)}, f32[1,1,512,320]{2,3,1,0:T(8,128)S(1)}, u32[]{:S(2)}, u32[]{:S(2)}) %collective-permute-start.3) | collective-permute-done | bytes 655392 | tf_op jit(solution)/shard_map/ppermute | solution.py:18
  141.1 7.1 %collective-permute-done.2 = f32[1,1,512,320]{2,3,1,0:T(8,128)} collective-permute-done((f32[1,1,512,320]{2,3,1,0:T(8,128)S(1)}, f32[1,1,512,320]{2,3,1,0:T(8,128)}, u32[]{:S(2)}, u32[]{:S(2)}) %collective-permute-start.2) | collective-permute-done | bytes 655392 | tf_op jit(solution)/shard_map/ppermute | solution.py:17
  149.6 3.0 %fusion.4 = bf16[1,6,512,320]{3,2,1,0:T(8,128)(2,1)S(1)} fusion(f32[320]{0:T(512)S(1)} %mul.140, f32[320]{0:T(512)S(1)} %sub.133, f32[1,1,512,320]{3,2,1,0:T(8,128)S(1)} %copy.60, f32[1,4,512,320]{3,2,1,0:T(8,128)} %bitcast.51, f32[1,1,512,320]{3,2,1,0:T(8,128)S(1)} %copy.59, pred[6]{0:T(512)(128)(4,1)S(1)} %and_or_fusion), kind=kLoop, calls=%fused_computation.17 | loop fusion | flops 9830400 | bytes 5900806 | tf_op jit(solution)/shard_map/jit(_where)/select_n | solution.py:62
  154.6 4.8 %pad_maximum_fusion.1.x_ref = bf16[6,512,960]{2,1,0:T(8,128)(2,1)} fusion(bf16[6,512,320]{2,1,0:T(8,128)(2,1)S(1)} %get-tuple-element.10, bf16[6,512,320]{2,1,0:T(8,128)(2,1)S(1)} %get-tuple-element.11, bf16[6,512,320]{2,1,0:T(8,128)(2,1)S(1)} %get-tuple-element.9), kind=kLoop, calls=%fused_computation.3 | loop fusion | flops 17694720 | bytes 11796480 | tf_op jit(solution)/shard_map/concatenate | solution.py:68
  159.4 11.7 %shard_map.92 = bf16[4,512,320]{2,1,0:T(8,128)(2,1)} custom-call(bf16[6,512,960]{2,1,0:T(8,128)(2,1)} %pad_maximum_fusion.1.x_ref, bf16[3,960,320]{2,1,0:T(8,128)(2,1)} %bitcast.55, bf16[4,512,320]{2,1,0:T(8,128)(2,1)} %bitcast.52), custom_call_target="tpu_custom_call" | custom-call | flops 1258291200 | bytes 10362880 | tf_op jit(solution)/shard_map/pallas_call | solution.py:122
  171.0 2.5 %copy.64 = bf16[1,4,512,320]{2,3,1,0:T(8,128)(2,1)} copy(bf16[1,4,512,320]{3,2,1,0:T(8,128)(2,1)} %bitcast.53) | data formatting | bytes 2621440 | tf_op jit(solution)/shard_map/broadcast_in_dim | solution.py:191
  (94 shorter events, 33.0 us)
Async XLA Ops:
  0.0 29.4 %copy-start = (bf16[1280,320]{0,1:T(8,128)(2,1)S(1)}, bf16[1280,320]{0,1:T(8,128)(2,1)}, u32[]{:S(2)}) copy-start(bf16[1280,320]{0,1:T(8,128)(2,1)} %param.17) | copy-start | bytes 2457604
  0.0 26.0 %copy-start.5 = (bf16[1,64,320]{2,1,0:T(8,128)(2,1)S(1)}, bf16[1,64,320]{2,1,0:T(8,128)(2,1)}, u32[]{:S(2)}) copy-start(bf16[1,64,320]{2,1,0:T(8,128)(2,1)} %param.15) | copy-start | bytes 122884
  1.9 67.7 %copy-start.3 = (bf16[1,4,512,320]{3,2,1,0:T(8,128)(2,1)}, bf16[1,4,512,320]{3,2,1,0:T(8,128)(2,1)S(1)}, u32[]{:S(2)}) copy-start(bf16[1,4,512,320]{3,2,1,0:T(8,128)(2,1)S(1)} %copy.51) | copy-start | bytes 3932164
  3.0 66.6 %collective-permute-start.1 = (bf16[1,1,512,320]{3,2,1,0:T(8,128)(2,1)}, bf16[1,1,512,320]{3,2,1,0:T(8,128)(2,1)}, u32[]{:S(2)}, u32[]{:S(2)}) collective-permute-start(bf16[1,1,512,320]{3,2,1,0:T(8,128)(2,1)} %get-tuple-element.16), channel_id=1, source_target_pairs={{16,0},{32,16},{48,32},{64,48},{80,64},{96,80},{112,96},{128,112},... | collective-permute-start | bytes 983048 | tf_op jit(solution)/shard_map/ppermute | solution.py:18
  8.1 61.5 %collective-permute-start = (bf16[1,1,512,320]{3,2,1,0:T(8,128)(2,1)}, bf16[1,1,512,320]{3,2,1,0:T(8,128)(2,1)}, u32[]{:S(2)}, u32[]{:S(2)}) collective-permute-start(bf16[1,1,512,320]{3,2,1,0:T(8,128)(2,1)} %get-tuple-element.15), channel_id=1, source_target_pairs={{0,16},{16,32},{32,48},{48,64},{64,80},{80,96},{96,112},{112,128},... | collective-permute-start | bytes 983048 | tf_op jit(solution)/shard_map/ppermute | solution.py:17
  12.4 18.7 %all-to-all-start.1 = ((s32[16,1,1]{2,1,0:T(1,128)}), s32[16,1,1]{2,1,0:T(1,128)S(1)}, u32[]{:S(2)}, u32[]{:S(2)}) async-start(s32[16,1,1]{2,1,0:T(1,128)} %broadcast_in_dim.81), calls=%async_computation.1 | async-start | bytes 16384 | tf_op jit(solution)/shard_map/all_to_all | solution.py:26
  23.0 16.7 %copy-start.2 = (s32[256]{0:T(256)S(1)}, s32[256]{0:T(256)}, u32[]{:S(2)}) copy-start(s32[256]{0:T(256)} %param.12) | copy-start | bytes 3076
  31.7 15.0 %all-to-all-start = ((f32[16,2,1,32]{3,2,1,0:T(1,128)}), f32[16,2,1,32]{3,2,1,0:T(1,128)S(1)}, u32[]{:S(2)}, u32[]{:S(2)}) async-start(f32[16,2,1,32]{3,2,1,0:T(1,128)} %broadcast_in_dim.79), calls=%async_computation | async-start | bytes 32768 | tf_op jit(solution)/shard_map/all_to_all | solution.py:26
  46.7 14.5 %all-to-all-start.2 = ((bf16[16,112,128]{2,1,0:T(8,128)(2,1)}), bf16[16,112,128]{2,1,0:T(8,128)(2,1)S(1)}, u32[]{:S(2)}, u32[]{:S(2)}) async-start(bf16[16,112,128]{2,1,0:T(8,128)(2,1)} %bitcast.9), calls=%async_computation.2 | async-start | bytes 917504 | tf_op jit(solution)/shard_map/all_to_all | solution.py:146
  62.7 19.0 %all-to-all-start.3 = ((bf16[16,112,128]{2,1,0:T(8,128)(2,1)}), bf16[16,112,128]{2,1,0:T(8,128)(2,1)S(1)}, u32[]{:S(2)}, u32[]{:S(2)}) async-start(bf16[16,112,128]{2,1,0:T(8,128)(2,1)} %broadcast_select_fusion), calls=%async_computation.3 | async-start | bytes 917504 | tf_op jit(solution)/shard_map/all_to_all | solution.py:148
  82.5 17.5 %all-to-all-start.4 = ((bf16[16,112,128]{2,1,0:T(8,128)(2,1)}), bf16[16,112,128]{2,1,0:T(8,128)(2,1)S(1)}, u32[]{:S(2)}, u32[]{:S(2)}) async-start(bf16[16,112,128]{2,1,0:T(8,128)(2,1)} %broadcast_in_dim.85), calls=%async_computation.4 | async-start | bytes 917504 | tf_op jit(solution)/shard_map/all_to_all | solution.py:26
  90.6 10.5 %copy-start.4 = (bf16[3,3,320,320]{3,2,1,0:T(8,128)(2,1)S(1)}, bf16[3,3,320,320]{3,2,1,0:T(8,128)(2,1)}, u32[]{:S(2)}) copy-start(bf16[3,3,320,320]{3,2,1,0:T(8,128)(2,1)} %param.13) | copy-start | bytes 5529604
  121.4 13.4 %all-to-all-start.5 = ((f32[16,2,1,32]{3,2,1,0:T(1,128)}), f32[16,2,1,32]{3,2,1,0:T(1,128)S(1)}, u32[]{:S(2)}, u32[]{:S(2)}) async-start(f32[16,2,1,32]{3,2,1,0:T(1,128)} %broadcast_in_dim.89), calls=%async_computation.5 | async-start | bytes 32768 | tf_op jit(solution)/shard_map/all_to_all | solution.py:26
  127.4 13.4 %collective-permute-start.3 = (f32[1,1,512,320]{2,3,1,0:T(8,128)S(1)}, f32[1,1,512,320]{2,3,1,0:T(8,128)S(1)}, u32[]{:S(2)}, u32[]{:S(2)}) collective-permute-start(f32[1,1,512,320]{2,3,1,0:T(8,128)S(1)} %copy.58), channel_id=1, source_target_pairs={{16,0},{32,16},{48,32},{64,48},{80,64},{96,80},{112,96},{128,112},... | collective-permute-start | bytes 1966088 | tf_op jit(solution)/shard_map/ppermute | solution.py:18
  130.0 18.2 %collective-permute-start.2 = (f32[1,1,512,320]{2,3,1,0:T(8,128)S(1)}, f32[1,1,512,320]{2,3,1,0:T(8,128)}, u32[]{:S(2)}, u32[]{:S(2)}) collective-permute-start(f32[1,1,512,320]{2,3,1,0:T(8,128)S(1)} %copy.57), channel_id=1, source_target_pairs={{0,16},{16,32},{32,48},{48,64},{64,80},{80,96},{96,112},{112,128},... | collective-permute-start | bytes 1966088 | tf_op jit(solution)/shard_map/ppermute | solution.py:17
  159.4 14.2 %copy-start.1 = (bf16[1280,320]{0,1:T(8,128)(2,1)S(1)}, bf16[1280,320]{0,1:T(8,128)(2,1)}, u32[]{:S(2)}) copy-start(bf16[1280,320]{0,1:T(8,128)(2,1)} %param.17) | copy-start | bytes 2457604

commit v3 on v2

--- a/solution.py
+++ b/solution.py
@@ -53,14 +53,9 @@
 
 
 def conv_input(field, groups):
-    extended = with_halo(field, (("band", 1),), 1)
     mean, scale = norm_stats(field, groups)
-    normed = norm_silu(extended, mean, scale, groups)
-    band, bands = lax.axis_index("band"), lax.axis_size("band")
-    row = lax.broadcasted_iota(jnp.int32, (1, normed.shape[1], 1, 1), 1)
-    outside = ((row == 0) & (band == 0)) | ((row == normed.shape[1] - 1) & (band == bands - 1))
-    normed = jnp.where(outside, jnp.zeros((), normed.dtype), normed)
-    return jnp.pad(normed, ((0, 0), (0, 0), (1, 1), (0, 0)))
+    extended = with_halo(norm_silu(field, mean, scale, groups), (("band", 1),), 1)
+    return jnp.pad(extended, ((0, 0), (0, 0), (1, 1), (0, 0)))
 
 
 def taps_by_column(padded):

time: 175 us -> 171 us (0.977)
  blocking collectives: 0 us -> 10.8 us
  starting transfers between devices: 53.8 us -> 45.5 us
  waiting for transfers between devices: 39.8 us -> 33.7 us
  other arithmetic: 29.2 us -> 32.7 us
  local copies, waits for them, and re-layouts: 22.2 us -> 19 us
    all_to_all x0 -> x1, blocking collectives: none -> 10.8 us  [exchange(): return lax.all_to_all(spread, axis, 0, 0, tiled=True)]
    all_to_all x1, waiting for transfers between devices: 8.69 us -> 0.01 us  [fetch_adapter(): by_req = lax.all_to_all(wanted, 'req', 0, 0, tiled=True)]
    select_n x2 -> x0, other arithmetic: 5.6 us -> none  [conv_input(): normed = jnp.where(outside, jnp.zeros((), normed.dtype), normed)]
    convert_element_type x0 -> x2, other arithmetic: none -> 5 us  [norm_silu(): return jax.nn.silu(normed.reshape(field.shape)).astype(jnp.bfloat16)]
    squeeze x0 -> x2, other arithmetic: none -> 4.34 us  [the longest x1 2.82 us: shards(): conv_input(latents, G)[0]]
    ppermute x2, starting transfers between devices: 7.41 us -> 4.06 us  [with_halo(): after = lax.ppermute(initial, axis, down)]
    slice x3 -> x2, local copies, waits for them, and re-layouts: 2.8 us -> 0.16 us  [with_halo(): last = lax.slice_in_dim(x, length - width, length, axis=dim)]
    all_to_all x4 -> x3, starting transfers between devices: 27.9 us -> 25.4 us  [exchange(): return lax.all_to_all(spread, axis, 0, 0, tiled=True)]
  transfers between devices with their start and end apart: 10 -> 9, of which waited for: 6 -> 6; matrix products, arithmetic and copies ran while one was open for 15% -> 13% of each run, Pallas kernels for 0% -> 0%
where the time goes in v3:
time: 171 us; the launch traced here: 170 us
  starting transfers between devices  45.5 us (27%)
  waiting for transfers between devices  33.7 us (20%)
  other arithmetic  32.7 us (19%)
  Pallas kernels  23.9 us (14%)
  local copies, waits for them, and re-layouts  19 us (11%)
  blocking collectives  10.8 us (6%)
  between operations  3.13 us (2%)
    all_to_all x3, starting transfers between devices, exchange(): return lax.all_to_all(spread, axis, 0, 0, tiled=True)  25.4 us
    pallas_call x1, Pallas kernels, first_conv(): pl.pallas_call(first_conv_kernel, grid=(rows,), in_specs=[pl.BlockSpec(co...  12.3 us
    pallas_call x1, Pallas kernels, second_conv(): pl.pallas_call(second_conv_kernel, grid=(rows,), in_specs=[pl.BlockSpec(c...  11.6 us
    all_to_all x1, blocking collectives, exchange(): return lax.all_to_all(spread, axis, 0, 0, tiled=True)  10.8 us
    all_to_all x3, waiting for transfers between devices, exchange(): return lax.all_to_all(spread, axis, 0, 0, tiled=True)  10.2 us
    concatenate x2, other arithmetic, taps_by_column(): jnp.concatenate([padded[:, tap:tap + width] for tap in range(3)], axis=-1)  9.63 us
    ppermute x2, waiting for transfers between devices, with_halo(): before = lax.ppermute(last, axis, up)  9.51 us
    all_to_all x1, waiting for transfers between devices, fetch_adapter(): by_band = lax.all_to_all(pieces, 'band', 0, 0, tiled=True)  8.15 us
  transfers between devices with their start and end apart: 9, of which 6 were waited for; matrix products, arithmetic and copies ran while one was open for 13% of the time, Pallas kernels for 0%

profile of v3, /device:TPU:1, one launch (start us, length us, event | category | flops | bytes accessed | tf_op | source)
XLA Modules:
  0.0 169.6 jit_solution(5082122797093176228)
XLA Ops:
  1.3 10.2 %all-to-all-start.1 = ((s32[16,1,1]{2,1,0:T(1,128)}), s32[16,1,1]{2,1,0:T(1,128)}, u32[]{:S(2)}, u32[]{:S(2)}) async-start(s32[16,1,1]{2,1,0:T(1,128)} %broadcast_in_dim.60), calls=%async_computation.1 | async-start | bytes 16384 | tf_op jit(solution)/shard_map/all_to_all | solution.py:26
  19.4 8.7 %all-to-all-start = ((f32[16,2,1,32]{3,2,1,0:T(1,128)}), f32[16,2,1,32]{3,2,1,0:T(1,128)S(1)}, u32[]{:S(2)}, u32[]{:S(2)}) async-start(f32[16,2,1,32]{3,2,1,0:T(1,128)} %broadcast_in_dim.58), calls=%async_computation | async-start | bytes 32768 | tf_op jit(solution)/shard_map/all_to_all | solution.py:26
  29.9 5.5 %all-to-all-done = f32[16,2,1,32]{3,2,1,0:T(1,128)S(1)} async-done(((f32[16,2,1,32]{3,2,1,0:T(1,128)}), f32[16,2,1,32]{3,2,1,0:T(1,128)S(1)}, u32[]{:S(2)}, u32[]{:S(2)}) %all-to-all-start) | async-done | bytes 4128 | tf_op jit(solution)/shard_map/all_to_all | solution.py:26
  35.4 3.7 %all-to-all-start.2 = ((bf16[16,112,128]{2,1,0:T(8,128)(2,1)}), bf16[16,112,128]{2,1,0:T(8,128)(2,1)S(1)}, u32[]{:S(2)}, u32[]{:S(2)}) async-start(bf16[16,112,128]{2,1,0:T(8,128)(2,1)} %bitcast.9), calls=%async_computation.2 | async-start | bytes 917504 | tf_op jit(solution)/shard_map/all_to_all | solution.py:141
  41.7 8.2 %all-to-all-done.2 = bf16[16,112,128]{2,1,0:T(8,128)(2,1)S(1)} async-done(((bf16[16,112,128]{2,1,0:T(8,128)(2,1)}), bf16[16,112,128]{2,1,0:T(8,128)(2,1)S(1)}, u32[]{:S(2)}, u32[]{:S(2)}) %all-to-all-start.2) | async-done | bytes 458784 | tf_op jit(solution)/shard_map/all_to_all | solution.py:141
  51.4 6.1 %all-to-all-start.3 = ((bf16[16,112,128]{2,1,0:T(8,128)(2,1)}), bf16[16,112,128]{2,1,0:T(8,128)(2,1)}, u32[]{:S(2)}, u32[]{:S(2)}) async-start(bf16[16,112,128]{2,1,0:T(8,128)(2,1)} %broadcast_select_fusion), calls=%async_computation.3 | async-start | bytes 917504 | tf_op jit(solution)/shard_map/all_to_all | solution.py:143
  57.6 3.7 %collective-permute-start = (bf16[1,1,512,320]{3,2,1,0:T(8,128)(2,1)S(1)}, bf16[1,1,512,320]{3,2,1,0:T(8,128)(2,1)S(1)}, u32[]{:S(2)}, u32[]{:S(2)}) collective-permute-start(bf16[1,1,512,320]{3,2,1,0:T(8,128)(2,1)S(1)} %get-tuple-element.15), channel_id=1, source_target_pairs={{0,16},{16,32},{32,48},{48,64},{64,80},{80,96},{96,112},{112,128},... | collective-permute-start | bytes 983048 | tf_op jit(solution)/shard_map/ppermute | solution.py:17
  67.0 7.0 %collective-permute-done = bf16[1,1,512,320]{3,2,1,0:T(8,128)(2,1)S(1)} collective-permute-done((bf16[1,1,512,320]{3,2,1,0:T(8,128)(2,1)S(1)}, bf16[1,1,512,320]{3,2,1,0:T(8,128)(2,1)S(1)}, u32[]{:S(2)}, u32[]{:S(2)}) %collective-permute-start) | collective-permute-done | bytes 327712 | tf_op jit(solution)/shard_map/ppermute | solution.py:17
  74.7 2.8 %fusion.16 = bf16[6,514,320]{2,1,0:T(8,128)(2,1)S(1)} fusion(bf16[1,1,512,320]{3,2,1,0:T(8,128)(2,1)} %collective-permute-done.1, bf16[1,4,512,320]{3,2,1,0:T(8,128)(2,1)} %fusion.9, bf16[1,1,512,320]{3,2,1,0:T(8,128)(2,1)} %copy-done.4), kind=kLoop, calls=%fused_computation.30 | loop fusion | flops 11842560 | bytes 3939840 | tf_op jit(solution)/shard_map/squeeze | solution.py:175
  79.1 6.5 %all-to-all-start.4 = ((bf16[16,112,128]{2,1,0:T(8,128)(2,1)}), bf16[16,112,128]{2,1,0:T(8,128)(2,1)}, u32[]{:S(2)}, u32[]{:S(2)}) async-start(bf16[16,112,128]{2,1,0:T(8,128)(2,1)} %broadcast_in_dim.64), calls=%async_computation.4 | async-start | bytes 917504 | tf_op jit(solution)/shard_map/all_to_all | solution.py:26
  86.9 4.8 %pad_maximum_fusion.x_ref = bf16[6,512,960]{2,1,0:T(8,128)(2,1)} fusion(bf16[6,512,320]{2,1,0:T(8,128)(2,1)S(1)} %get-tuple-element.11, bf16[6,512,320]{2,1,0:T(8,128)(2,1)S(1)} %get-tuple-element.12, bf16[6,512,320]{2,1,0:T(8,128)(2,1)S(1)} %get-tuple-element.10), kind=kLoop, calls=%fused_computation.4 | loop fusion | flops 17694720 | bytes 11796480 | tf_op jit(solution)/shard_map/concatenate | solution.py:63
  91.7 4.7 %all-to-all-done.4 = bf16[16,112,128]{2,1,0:T(8,128)(2,1)} async-done(((bf16[16,112,128]{2,1,0:T(8,128)(2,1)}), bf16[16,112,128]{2,1,0:T(8,128)(2,1)}, u32[]{:S(2)}, u32[]{:S(2)}) %all-to-all-start.4) | async-done | bytes 458784 | tf_op jit(solution)/shard_map/all_to_all | solution.py:26
  99.2 3.8 %pad_maximum_fusion.2.w_ref = bf16[3,960,448]{2,1,0:T(8,128)(2,1)} fusion(bf16[3,960,320]{2,1,0:T(8,128)(2,1)} %bitcast.53, bf16[3,960,64]{2,1,0:T(8,128)(2,1)S(1)} %reshape_reshape.3, bf16[448]{0:T(512)(128)(2,1)S(1)} %pad.23.clone), kind=kLoop, calls=%fused_computation.21 | loop fusion | flops 7741440 | bytes 4793216 | tf_op jit(solution)/shard_map/concatenate | solution.py:94
  103.0 12.3 %shard_map.91 = f32[4,512,320]{2,1,0:T(8,128)} custom-call(bf16[6,512,960]{2,1,0:T(8,128)(2,1)} %pad_maximum_fusion.x_ref, bf16[3,960,448]{2,1,0:T(8,128)(2,1)} %pad_maximum_fusion.2.w_ref, bf16[64,320]{1,0:T(8,128)(2,1)} %reshape.400.u_ref, f32[1,320]{1,0:T(1,128)} %fusion.21.s_ref), custom_call_target="tpu_custom_call" | custom-call | flops 1845493760 | bytes 11100160 | tf_op jit(solution)/shard_map/pallas_call | solution.py:96
  115.3 2.2 %reduce_sum.127 = f32[320]{0:T(512)S(1)} reduce(f32[4,512,320]{2,1,0:T(8,128)} %shard_map.91, f32[]{:T(128)} %constant.70.clone.1), dimensions={0,1}, to_apply=%region_7.8 | reduce | flops 655040 | bytes 2622724 | tf_op jit(solution)/shard_map/reduce_sum | solution.py:34
  117.9 2.3 %multiply_reduce_fusion = f32[320]{0:T(512)S(1)} fusion(f32[4,512,320]{2,1,0:T(8,128)} %shard_map.91, f32[320]{0:T(512)S(1)} %sub.115), kind=kLoop, calls=%fused_computation.20 | loop fusion | flops 1965760 | bytes 2624000 | tf_op jit(solution)/shard_map/reduce_sum | solution.py:36
  120.5 10.8 %all_to_all.37 = f32[16,2,1,32]{3,2,1,0:T(1,128)S(1)} all-to-all(f32[16,2,1,32]{3,2,1,0:T(1,128)S(1)} %broadcast_in_dim.67), channel_id=1, replica_groups=mesh['band'=16,'req'=16] {'band'}, dimensions={0} | all-to-all | bytes 8192 | tf_op jit(solution)/shard_map/all_to_all | solution.py:26
  131.7 2.9 %fusion.17 = bf16[1,4,512,320]{3,2,1,0:T(8,128)(2,1)S(1)} fusion(f32[320]{0:T(512)S(1)} %mul.113, f32[4,512,320]{2,1,0:T(8,128)} %shard_map.91, f32[320]{0:T(512)S(1)} %sub.119), kind=kLoop, calls=%fused_computation.31 | loop fusion | flops 4587520 | bytes 3934720 | tf_op jit(solution)/shard_map/convert_element_type | solution.py:52
  134.8 2.5 %collective-permute-start.2 = (bf16[1,1,512,320]{3,2,1,0:T(8,128)(2,1)S(1)}, bf16[1,1,512,320]{3,2,1,0:T(8,128)(2,1)S(1)}, u32[]{:S(2)}, u32[]{:S(2)}) collective-permute-start(bf16[1,1,512,320]{3,2,1,0:T(8,128)(2,1)S(1)} %get-tuple-element.13), channel_id=1, source_target_pairs={{0,16},{16,32},{32,48},{48,64},{64,80},{80,96},{96,112},{112,128},... | collective-permute-start | bytes 983048 | tf_op jit(solution)/shard_map/ppermute | solution.py:17
  139.4 2.6 %collective-permute-done.2 = bf16[1,1,512,320]{3,2,1,0:T(8,128)(2,1)S(1)} collective-permute-done((bf16[1,1,512,320]{3,2,1,0:T(8,128)(2,1)S(1)}, bf16[1,1,512,320]{3,2,1,0:T(8,128)(2,1)S(1)}, u32[]{:S(2)}, u32[]{:S(2)}) %collective-permute-start.2) | collective-permute-done | bytes 327712 | tf_op jit(solution)/shard_map/ppermute | solution.py:17
  141.9 5.9 %collective-permute-done.3 = bf16[1,1,512,320]{3,2,1,0:T(8,128)(2,1)S(1)} collective-permute-done((bf16[1,1,512,320]{3,2,1,0:T(8,128)(2,1)S(1)}, bf16[1,1,512,320]{3,2,1,0:T(8,128)(2,1)S(1)}, u32[]{:S(2)}, u32[]{:S(2)}) %collective-permute-start.3) | collective-permute-done | bytes 327712 | tf_op jit(solution)/shard_map/ppermute | solution.py:18
  150.7 4.8 %pad_maximum_fusion.1.x_ref = bf16[6,512,960]{2,1,0:T(8,128)(2,1)} fusion(bf16[6,512,320]{2,1,0:T(8,128)(2,1)S(1)} %get-tuple-element.8, bf16[6,512,320]{2,1,0:T(8,128)(2,1)S(1)} %get-tuple-element.9, bf16[6,512,320]{2,1,0:T(8,128)(2,1)S(1)} %get-tuple-element.7), kind=kLoop, calls=%fused_computation.5 | loop fusion | flops 17694720 | bytes 11796480 | tf_op jit(solution)/shard_map/concatenate | solution.py:63
  155.5 11.6 %shard_map.92 = bf16[4,512,320]{2,1,0:T(8,128)(2,1)} custom-call(bf16[6,512,960]{2,1,0:T(8,128)(2,1)} %pad_maximum_fusion.1.x_ref, bf16[3,960,320]{2,1,0:T(8,128)(2,1)} %bitcast.54, bf16[4,512,320]{2,1,0:T(8,128)(2,1)} %bitcast.51), custom_call_target="tpu_custom_call" | custom-call | flops 1258291200 | bytes 10362880 | tf_op jit(solution)/shard_map/pallas_call | solution.py:117
  167.2 2.5 %copy.36 = bf16[1,4,512,320]{2,3,1,0:T(8,128)(2,1)} copy(bf16[1,4,512,320]{3,2,1,0:T(8,128)(2,1)} %bitcast.52) | data formatting | bytes 2621440 | tf_op jit(solution)/shard_map/broadcast_in_dim | solution.py:186
  (90 shorter events, 30.5 us)
Async XLA Ops:
  0.0 63.4 %copy-start = (bf16[1280,320]{0,1:T(8,128)(2,1)S(1)}, bf16[1280,320]{0,1:T(8,128)(2,1)}, u32[]{:S(2)}) copy-start(bf16[1280,320]{0,1:T(8,128)(2,1)} %param.17) | copy-start | bytes 2457604
  1.3 17.4 %all-to-all-start.1 = ((s32[16,1,1]{2,1,0:T(1,128)}), s32[16,1,1]{2,1,0:T(1,128)}, u32[]{:S(2)}, u32[]{:S(2)}) async-start(s32[16,1,1]{2,1,0:T(1,128)} %broadcast_in_dim.60), calls=%async_computation.1 | async-start | bytes 16384 | tf_op jit(solution)/shard_map/all_to_all | solution.py:26
  13.4 26.3 %copy-start.2 = (bf16[1,4,512,320]{3,2,1,0:T(8,128)(2,1)}, bf16[1,4,512,320]{3,2,1,0:T(8,128)(2,1)S(1)}, u32[]{:S(2)}) copy-start(bf16[1,4,512,320]{3,2,1,0:T(8,128)(2,1)S(1)} %copy.29) | copy-start | bytes 3932164
  13.4 3.8 %copy-start.5 = (bf16[1,64,320]{2,1,0:T(8,128)(2,1)S(1)}, bf16[1,64,320]{2,1,0:T(8,128)(2,1)}, u32[]{:S(2)}) copy-start(bf16[1,64,320]{2,1,0:T(8,128)(2,1)} %param.15) | copy-start | bytes 122884
  13.4 15.8 %copy-start.1 = (s32[256]{0:T(256)S(1)}, s32[256]{0:T(256)}, u32[]{:S(2)}) copy-start(s32[256]{0:T(256)} %param.12) | copy-start | bytes 3076
  19.4 16.0 %all-to-all-start = ((f32[16,2,1,32]{3,2,1,0:T(1,128)}), f32[16,2,1,32]{3,2,1,0:T(1,128)S(1)}, u32[]{:S(2)}, u32[]{:S(2)}) async-start(f32[16,2,1,32]{3,2,1,0:T(1,128)} %broadcast_in_dim.58), calls=%async_computation | async-start | bytes 32768 | tf_op jit(solution)/shard_map/all_to_all | solution.py:26
  35.4 14.5 %all-to-all-start.2 = ((bf16[16,112,128]{2,1,0:T(8,128)(2,1)}), bf16[16,112,128]{2,1,0:T(8,128)(2,1)S(1)}, u32[]{:S(2)}, u32[]{:S(2)}) async-start(bf16[16,112,128]{2,1,0:T(8,128)(2,1)} %bitcast.9), calls=%async_computation.2 | async-start | bytes 917504 | tf_op jit(solution)/shard_map/all_to_all | solution.py:141
  39.6 23.7 %copy-start.6 = (bf16[1,1280]{1,0:T(2,128)(2,1)S(1)}, bf16[1,1280]{1,0:T(2,128)(2,1)}, u32[]{:S(2)}) copy-start(bf16[1,1280]{1,0:T(2,128)(2,1)} %param.10) | copy-start | bytes 7684
  41.7 15.8 %copy-start.3 = (bf16[1,4,512,320]{3,2,1,0:T(8,128)(2,1)S(1)}, bf16[1,4,512,320]{3,2,1,0:T(8,128)(2,1)}, u32[]{:S(2)}) copy-start(bf16[1,4,512,320]{3,2,1,0:T(8,128)(2,1)} %fusion.9) | copy-start | bytes 3932164
  51.4 26.1 %all-to-all-start.3 = ((bf16[16,112,128]{2,1,0:T(8,128)(2,1)}), bf16[16,112,128]{2,1,0:T(8,128)(2,1)}, u32[]{:S(2)}, u32[]{:S(2)}) async-start(bf16[16,112,128]{2,1,0:T(8,128)(2,1)} %broadcast_select_fusion), calls=%async_computation.3 | async-start | bytes 917504 | tf_op jit(solution)/shard_map/all_to_all | solution.py:143
  57.6 16.3 %collective-permute-start = (bf16[1,1,512,320]{3,2,1,0:T(8,128)(2,1)S(1)}, bf16[1,1,512,320]{3,2,1,0:T(8,128)(2,1)S(1)}, u32[]{:S(2)}, u32[]{:S(2)}) collective-permute-start(bf16[1,1,512,320]{3,2,1,0:T(8,128)(2,1)S(1)} %get-tuple-element.15), channel_id=1, source_target_pairs={{0,16},{16,32},{32,48},{48,64},{64,80},{80,96},{96,112},{112,128},... | collective-permute-start | bytes 983048 | tf_op jit(solution)/shard_map/ppermute | solution.py:17
  61.3 13.3 %collective-permute-start.1 = (bf16[1,1,512,320]{3,2,1,0:T(8,128)(2,1)S(1)}, bf16[1,1,512,320]{3,2,1,0:T(8,128)(2,1)}, u32[]{:S(2)}, u32[]{:S(2)}) collective-permute-start(bf16[1,1,512,320]{3,2,1,0:T(8,128)(2,1)S(1)} %get-tuple-element.16), channel_id=1, source_target_pairs={{16,0},{32,16},{48,32},{64,48},{80,64},{96,80},{112,96},{128,112},... | collective-permute-start | bytes 983048 | tf_op jit(solution)/shard_map/ppermute | solution.py:18
  73.9 0.7 copy-start.4
  79.1 17.3 %all-to-all-start.4 = ((bf16[16,112,128]{2,1,0:T(8,128)(2,1)}), bf16[16,112,128]{2,1,0:T(8,128)(2,1)}, u32[]{:S(2)}, u32[]{:S(2)}) async-start(bf16[16,112,128]{2,1,0:T(8,128)(2,1)} %broadcast_in_dim.64), calls=%async_computation.4 | async-start | bytes 917504 | tf_op jit(solution)/shard_map/all_to_all | solution.py:26
  134.8 7.2 %collective-permute-start.2 = (bf16[1,1,512,320]{3,2,1,0:T(8,128)(2,1)S(1)}, bf16[1,1,512,320]{3,2,1,0:T(8,128)(2,1)S(1)}, u32[]{:S(2)}, u32[]{:S(2)}) collective-permute-start(bf16[1,1,512,320]{3,2,1,0:T(8,128)(2,1)S(1)} %get-tuple-element.13), channel_id=1, source_target_pairs={{0,16},{16,32},{32,48},{48,64},{64,80},{80,96},{96,112},{112,128},... | collective-permute-start | bytes 983048 | tf_op jit(solution)/shard_map/ppermute | solution.py:17
  137.2 10.6 %collective-permute-start.3 = (bf16[1,1,512,320]{3,2,1,0:T(8,128)(2,1)S(1)}, bf16[1,1,512,320]{3,2,1,0:T(8,128)(2,1)S(1)}, u32[]{:S(2)}, u32[]{:S(2)}) collective-permute-start(bf16[1,1,512,320]{3,2,1,0:T(8,128)(2,1)S(1)} %get-tuple-element.14), channel_id=1, source_target_pairs={{16,0},{32,16},{48,32},{64,48},{80,64},{96,80},{112,96},{128,112},... | collective-permute-start | bytes 983048 | tf_op jit(solution)/shard_map/ppermute | solution.py:18

commit v4 on v3

--- a/solution.py
+++ b/solution.py
@@ -54,13 +54,14 @@
 
 def conv_input(field, groups):
     mean, scale = norm_stats(field, groups)
-    extended = with_halo(norm_silu(field, mean, scale, groups), (("band", 1),), 1)
-    return jnp.pad(extended, ((0, 0), (0, 0), (1, 1), (0, 0)))
-
-
-def taps_by_column(padded):
-    width = padded.shape[1] - 2
-    return jnp.concatenate([padded[:, tap : tap + width] for tap in range(3)], axis=-1)
+    return with_halo(norm_silu(field, mean, scale, groups), (("band", 1),), 1)
+
+
+def taps_by_column(field):
+    none = (0, 0)
+    left = jnp.pad(field[:, :-1], (none, (1, 0), none))
+    right = jnp.pad(field[:, 1:], (none, (0, 1), none))
+    return jnp.concatenate([left, field, right], axis=-1)
 
 
 def first_conv_kernel(x_ref, w_ref, u_ref, s_ref, o_ref):

time: 171 us -> 163 us (0.953)
  waiting for transfers between devices: 33.7 us -> 21.5 us
  local copies, waits for them, and re-layouts: 19 us -> 21.3 us
  starting transfers between devices: 45.5 us -> 47.7 us
    all_to_all x1, waiting for transfers between devices: 8.15 us -> 1.08 us  [fetch_adapter(): by_band = lax.all_to_all(pieces, 'band', 0, 0, tiled=True)]
    ppermute x2, waiting for transfers between devices: 9.51 us -> 2.77 us  [with_halo(): before = lax.ppermute(last, axis, up)]
    all_to_all x1, waiting for transfers between devices: 0.01 us -> 2.76 us  [fetch_adapter(): by_req = lax.all_to_all(wanted, 'req', 0, 0, tiled=True)]
    concatenate x2, other arithmetic: 9.63 us -> 12.2 us  [taps_by_column(): return jnp.concatenate([left, field, right], axis=-1)]
  transfers between devices with their start and end apart: 9 -> 9, of which waited for: 6 -> 6; matrix products, arithmetic and copies ran while one was open for 13% -> 16% of each run, Pallas kernels for 0% -> 0%
where the time goes in v4:
time: 163 us; the launch traced here: 161 us
  starting transfers between devices  47.7 us (29%)
  other arithmetic  32.4 us (20%)
  Pallas kernels  23.9 us (15%)
  waiting for transfers between devices  21.5 us (13%)
  local copies, waits for them, and re-layouts  21.3 us (13%)
  blocking collectives  10.8 us (7%)
  between operations  2.95 us (2%)
    all_to_all x3, starting transfers between devices, exchange(): return lax.all_to_all(spread, axis, 0, 0, tiled=True)  26.5 us
    pallas_call x1, Pallas kernels, first_conv(): pl.pallas_call(first_conv_kernel, grid=(rows,), in_specs=[pl.BlockSpec(co...  12.3 us
    concatenate x2, other arithmetic, taps_by_column(): return jnp.concatenate([left, field, right], axis=-1)  12.2 us
    pallas_call x1, Pallas kernels, second_conv(): pl.pallas_call(second_conv_kernel, grid=(rows,), in_specs=[pl.BlockSpec(c...  11.6 us
    all_to_all x1, blocking collectives, exchange(): return lax.all_to_all(spread, axis, 0, 0, tiled=True)  10.8 us
    all_to_all x3, waiting for transfers between devices, exchange(): return lax.all_to_all(spread, axis, 0, 0, tiled=True)  9.02 us
    ppermute x2, starting transfers between devices, with_halo(): before = lax.ppermute(last, axis, up)  7.53 us
    all_to_all x1, starting transfers between devices, fetch_adapter(): by_req = lax.all_to_all(wanted, 'req', 0, 0, tiled=True)  6.09 us
  transfers between devices with their start and end apart: 9, of which 6 were waited for; matrix products, arithmetic and copies ran while one was open for 16% of the time, Pallas kernels for 0%

profile of v4, /device:TPU:1, one launch (start us, length us, event | category | flops | bytes accessed | tf_op | source)
XLA Modules:
  0.0 161.5 jit_solution(9768969532546793966)
XLA Ops:
  1.3 10.2 %all-to-all-start.1 = ((s32[16,1,1]{2,1,0:T(1,128)}), s32[16,1,1]{2,1,0:T(1,128)}, u32[]{:S(2)}, u32[]{:S(2)}) async-start(s32[16,1,1]{2,1,0:T(1,128)} %broadcast_in_dim.60), calls=%async_computation.1 | async-start | bytes 16384 | tf_op jit(solution)/shard_map/all_to_all | solution.py:26
  19.4 8.7 %all-to-all-start = ((f32[16,2,1,32]{3,2,1,0:T(1,128)}), f32[16,2,1,32]{3,2,1,0:T(1,128)S(1)}, u32[]{:S(2)}, u32[]{:S(2)}) async-start(f32[16,2,1,32]{3,2,1,0:T(1,128)} %broadcast_in_dim.58), calls=%async_computation | async-start | bytes 32768 | tf_op jit(solution)/shard_map/all_to_all | solution.py:26
  29.9 5.5 %all-to-all-done = f32[16,2,1,32]{3,2,1,0:T(1,128)S(1)} async-done(((f32[16,2,1,32]{3,2,1,0:T(1,128)}), f32[16,2,1,32]{3,2,1,0:T(1,128)S(1)}, u32[]{:S(2)}, u32[]{:S(2)}) %all-to-all-start) | async-done | bytes 4128 | tf_op jit(solution)/shard_map/all_to_all | solution.py:26
  35.4 3.7 %all-to-all-start.2 = ((bf16[16,112,128]{2,1,0:T(8,128)(2,1)}), bf16[16,112,128]{2,1,0:T(8,128)(2,1)S(1)}, u32[]{:S(2)}, u32[]{:S(2)}) async-start(bf16[16,112,128]{2,1,0:T(8,128)(2,1)} %bitcast.9), calls=%async_computation.2 | async-start | bytes 917504 | tf_op jit(solution)/shard_map/all_to_all | solution.py:142
  41.8 5.1 %collective-permute-start = (bf16[1,1,512,320]{3,2,1,0:T(8,128)(2,1)S(1)}, bf16[1,1,512,320]{3,2,1,0:T(8,128)(2,1)S(1)}, u32[]{:S(2)}, u32[]{:S(2)}) collective-permute-start(bf16[1,1,512,320]{3,2,1,0:T(8,128)(2,1)S(1)} %get-tuple-element.13), channel_id=1, source_target_pairs={{0,16},{16,32},{32,48},{48,64},{64,80},{80,96},{96,112},{112,128},... | collective-permute-start | bytes 983048 | tf_op jit(solution)/shard_map/ppermute | solution.py:17
  51.4 6.1 %all-to-all-start.3 = ((bf16[16,112,128]{2,1,0:T(8,128)(2,1)}), bf16[16,112,128]{2,1,0:T(8,128)(2,1)}, u32[]{:S(2)}, u32[]{:S(2)}) async-start(bf16[16,112,128]{2,1,0:T(8,128)(2,1)} %broadcast_select_fusion), calls=%async_computation.3 | async-start | bytes 917504 | tf_op jit(solution)/shard_map/all_to_all | solution.py:144
  61.8 2.1 %maximum_bitcast_fusion = bf16[6,512,320]{2,1,0:T(8,128)(2,1)S(1)} fusion(bf16[1,1,512,320]{3,2,1,0:T(8,128)(2,1)} %collective-permute-done.1, bf16[1,4,512,320]{3,2,1,0:T(8,128)(2,1)} %copy-done.3, bf16[1,1,512,320]{3,2,1,0:T(8,128)(2,1)} %copy-done.4), kind=kLoop, calls=%fused_computation.27 | loop fusion | flops 1966080 | bytes 3932160 | tf_op jit(solution)/shard_map/squeeze | solution.py:176
  63.8 3.0 %fusion.34 = (bf16[6,511,320]{2,1,0:T(8,128)(2,1)}, bf16[6,511,320]{2,1,0:T(8,128)(2,1)}) fusion(bf16[6,512,320]{2,1,0:T(8,128)(2,1)S(1)} %maximum_bitcast_fusion), kind=kLoop, calls=%fused_computation.77 | loop fusion | bytes 7848960 | tf_op jit(solution)/shard_map/slice | solution.py:62
  66.8 2.8 %all-to-all-done.3 = bf16[16,112,128]{2,1,0:T(8,128)(2,1)} async-done(((bf16[16,112,128]{2,1,0:T(8,128)(2,1)}), bf16[16,112,128]{2,1,0:T(8,128)(2,1)}, u32[]{:S(2)}, u32[]{:S(2)}) %all-to-all-start.3) | async-done | bytes 458784 | tf_op jit(solution)/shard_map/all_to_all | solution.py:144
  71.2 7.6 %all-to-all-start.4 = ((bf16[16,112,128]{2,1,0:T(8,128)(2,1)}), bf16[16,112,128]{2,1,0:T(8,128)(2,1)}, u32[]{:S(2)}, u32[]{:S(2)}) async-start(bf16[16,112,128]{2,1,0:T(8,128)(2,1)} %broadcast_in_dim.64), calls=%async_computation.4 | async-start | bytes 917504 | tf_op jit(solution)/shard_map/all_to_all | solution.py:26
  78.7 7.2 %fusion.5.x_ref = bf16[6,512,960]{2,1,0:T(8,128)(2,1)} fusion(bf16[6,511,320]{2,1,0:T(8,128)(2,1)} %get-tuple-element.10, bf16[6,511,320]{2,1,0:T(8,128)(2,1)} %get-tuple-element.9, bf16[6,512,320]{2,1,0:T(8,128)(2,1)S(1)} %maximum_bitcast_fusion), kind=kLoop, calls=%fused_computation.9 | loop fusion | flops 29491200 | bytes 11788800 | tf_op jit(solution)/shard_map/concatenate | solution.py:64
  86.0 3.5 %all-to-all-done.4 = bf16[16,112,128]{2,1,0:T(8,128)(2,1)} async-done(((bf16[16,112,128]{2,1,0:T(8,128)(2,1)}), bf16[16,112,128]{2,1,0:T(8,128)(2,1)}, u32[]{:S(2)}, u32[]{:S(2)}) %all-to-all-start.4) | async-done | bytes 458784 | tf_op jit(solution)/shard_map/all_to_all | solution.py:26
  92.4 3.8 %pad_maximum_fusion.w_ref = bf16[3,960,448]{2,1,0:T(8,128)(2,1)} fusion(bf16[3,960,320]{2,1,0:T(8,128)(2,1)} %bitcast.53, bf16[3,960,64]{2,1,0:T(8,128)(2,1)S(1)} %reshape_reshape.3, bf16[448]{0:T(512)(128)(2,1)S(1)} %pad.32.clone), kind=kLoop, calls=%fused_computation.26 | loop fusion | flops 7741440 | bytes 4793216 | tf_op jit(solution)/shard_map/concatenate | solution.py:95
  96.2 12.3 %shard_map.91 = f32[4,512,320]{2,1,0:T(8,128)} custom-call(bf16[6,512,960]{2,1,0:T(8,128)(2,1)} %fusion.5.x_ref, bf16[3,960,448]{2,1,0:T(8,128)(2,1)} %pad_maximum_fusion.w_ref, bf16[64,320]{1,0:T(8,128)(2,1)} %reshape.400.u_ref, f32[1,320]{1,0:T(1,128)} %fusion.21.s_ref), custom_call_target="tpu_custom_call" | custom-call | flops 1845493760 | bytes 11100160 | tf_op jit(solution)/shard_map/pallas_call | solution.py:97
  108.4 2.2 %reduce_sum.127 = f32[320]{0:T(512)S(1)} reduce(f32[4,512,320]{2,1,0:T(8,128)} %shard_map.91, f32[]{:T(128)} %constant.70.clone.1), dimensions={0,1}, to_apply=%region_7.8 | reduce | flops 655040 | bytes 2622724 | tf_op jit(solution)/shard_map/reduce_sum | solution.py:34
  111.0 2.3 %multiply_reduce_fusion = f32[320]{0:T(512)S(1)} fusion(f32[4,512,320]{2,1,0:T(8,128)} %shard_map.91, f32[320]{0:T(512)S(1)} %sub.115), kind=kLoop, calls=%fused_computation.25 | loop fusion | flops 1965760 | bytes 2624000 | tf_op jit(solution)/shard_map/reduce_sum | solution.py:36
  113.6 10.8 %all_to_all.37 = f32[16,2,1,32]{3,2,1,0:T(1,128)S(1)} all-to-all(f32[16,2,1,32]{3,2,1,0:T(1,128)S(1)} %broadcast_in_dim.67), channel_id=1, replica_groups=mesh['band'=16,'req'=16] {'band'}, dimensions={0} | all-to-all | bytes 8192 | tf_op jit(solution)/shard_map/all_to_all | solution.py:26
  124.9 2.9 %fusion.17 = bf16[1,4,512,320]{3,2,1,0:T(8,128)(2,1)S(1)} fusion(f32[320]{0:T(512)S(1)} %mul.113, f32[4,512,320]{2,1,0:T(8,128)} %shard_map.91, f32[320]{0:T(512)S(1)} %sub.119), kind=kLoop, calls=%fused_computation.29 | loop fusion | flops 4587520 | bytes 3934720 | tf_op jit(solution)/shard_map/convert_element_type | solution.py:52
  127.9 2.5 %collective-permute-start.2 = (bf16[1,1,512,320]{3,2,1,0:T(8,128)(2,1)S(1)}, bf16[1,1,512,320]{3,2,1,0:T(8,128)(2,1)S(1)}, u32[]{:S(2)}, u32[]{:S(2)}) collective-permute-start(bf16[1,1,512,320]{3,2,1,0:T(8,128)(2,1)S(1)} %get-tuple-element.11), channel_id=1, source_target_pairs={{0,16},{16,32},{32,48},{48,64},{64,80},{80,96},{96,112},{112,128},... | collective-permute-start | bytes 983048 | tf_op jit(solution)/shard_map/ppermute | solution.py:17
  132.3 2.8 %collective-permute-done.2 = bf16[1,1,512,320]{3,2,1,0:T(8,128)(2,1)S(1)} collective-permute-done((bf16[1,1,512,320]{3,2,1,0:T(8,128)(2,1)S(1)}, bf16[1,1,512,320]{3,2,1,0:T(8,128)(2,1)S(1)}, u32[]{:S(2)}, u32[]{:S(2)}) %collective-permute-start.2) | collective-permute-done | bytes 327712 | tf_op jit(solution)/shard_map/ppermute | solution.py:17
  135.1 5.9 %collective-permute-done.3 = bf16[1,1,512,320]{3,2,1,0:T(8,128)(2,1)S(1)} collective-permute-done((bf16[1,1,512,320]{3,2,1,0:T(8,128)(2,1)S(1)}, bf16[1,1,512,320]{3,2,1,0:T(8,128)(2,1)S(1)}, u32[]{:S(2)}, u32[]{:S(2)}) %collective-permute-start.3) | collective-permute-done | bytes 327712 | tf_op jit(solution)/shard_map/ppermute | solution.py:18
  142.4 5.0 %fusion.7.x_ref = bf16[6,512,960]{2,1,0:T(8,128)(2,1)} fusion(bf16[6,511,320]{2,1,0:T(8,128)(2,1)S(1)} %get-tuple-element.8, bf16[6,511,320]{2,1,0:T(8,128)(2,1)S(1)} %get-tuple-element.7, bf16[6,512,320]{2,1,0:T(8,128)(2,1)S(1)} %maximum_bitcast_fusion.1), kind=kLoop, calls=%fused_computation.11 | loop fusion | flops 29491200 | bytes 11788800 | tf_op jit(solution)/shard_map/concatenate | solution.py:64
  147.3 11.6 %shard_map.92 = bf16[4,512,320]{2,1,0:T(8,128)(2,1)} custom-call(bf16[6,512,960]{2,1,0:T(8,128)(2,1)} %fusion.7.x_ref, bf16[3,960,320]{2,1,0:T(8,128)(2,1)} %bitcast.54, bf16[4,512,320]{2,1,0:T(8,128)(2,1)} %bitcast.51), custom_call_target="tpu_custom_call" | custom-call | flops 1258291200 | bytes 10362880 | tf_op jit(solution)/shard_map/pallas_call | solution.py:118
  159.0 2.5 %copy.36 = bf16[1,4,512,320]{2,3,1,0:T(8,128)(2,1)} copy(bf16[1,4,512,320]{3,2,1,0:T(8,128)(2,1)} %bitcast.52) | data formatting | bytes 2621440 | tf_op jit(solution)/shard_map/broadcast_in_dim | solution.py:187
  (90 shorter events, 28.5 us)
Async XLA Ops:
  0.0 57.6 %copy-start = (bf16[1280,320]{0,1:T(8,128)(2,1)S(1)}, bf16[1280,320]{0,1:T(8,128)(2,1)}, u32[]{:S(2)}) copy-start(bf16[1280,320]{0,1:T(8,128)(2,1)} %param.17) | copy-start | bytes 2457604
  1.3 17.4 %all-to-all-start.1 = ((s32[16,1,1]{2,1,0:T(1,128)}), s32[16,1,1]{2,1,0:T(1,128)}, u32[]{:S(2)}, u32[]{:S(2)}) async-start(s32[16,1,1]{2,1,0:T(1,128)} %broadcast_in_dim.60), calls=%async_computation.1 | async-start | bytes 16384 | tf_op jit(solution)/shard_map/all_to_all | solution.py:26
  13.4 26.3 %copy-start.2 = (bf16[1,4,512,320]{3,2,1,0:T(8,128)(2,1)}, bf16[1,4,512,320]{3,2,1,0:T(8,128)(2,1)S(1)}, u32[]{:S(2)}) copy-start(bf16[1,4,512,320]{3,2,1,0:T(8,128)(2,1)S(1)} %copy.29) | copy-start | bytes 3932164
  13.4 3.8 %copy-start.5 = (bf16[1,64,320]{2,1,0:T(8,128)(2,1)S(1)}, bf16[1,64,320]{2,1,0:T(8,128)(2,1)}, u32[]{:S(2)}) copy-start(bf16[1,64,320]{2,1,0:T(8,128)(2,1)} %param.15) | copy-start | bytes 122884
  13.4 15.8 %copy-start.1 = (s32[256]{0:T(256)S(1)}, s32[256]{0:T(256)}, u32[]{:S(2)}) copy-start(s32[256]{0:T(256)} %param.12) | copy-start | bytes 3076
  19.4 16.0 %all-to-all-start = ((f32[16,2,1,32]{3,2,1,0:T(1,128)}), f32[16,2,1,32]{3,2,1,0:T(1,128)S(1)}, u32[]{:S(2)}, u32[]{:S(2)}) async-start(f32[16,2,1,32]{3,2,1,0:T(1,128)} %broadcast_in_dim.58), calls=%async_computation | async-start | bytes 32768 | tf_op jit(solution)/shard_map/all_to_all | solution.py:26
  35.4 14.5 %all-to-all-start.2 = ((bf16[16,112,128]{2,1,0:T(8,128)(2,1)}), bf16[16,112,128]{2,1,0:T(8,128)(2,1)S(1)}, u32[]{:S(2)}, u32[]{:S(2)}) async-start(bf16[16,112,128]{2,1,0:T(8,128)(2,1)} %bitcast.9), calls=%async_computation.2 | async-start | bytes 917504 | tf_op jit(solution)/shard_map/all_to_all | solution.py:142
  39.6 18.0 %copy-start.6 = (bf16[1,1280]{1,0:T(2,128)(2,1)S(1)}, bf16[1,1280]{1,0:T(2,128)(2,1)}, u32[]{:S(2)}) copy-start(bf16[1,1280]{1,0:T(2,128)(2,1)} %param.10) | copy-start | bytes 7684
  40.6 1.2 copy-start.3
  41.8 19.2 %collective-permute-start = (bf16[1,1,512,320]{3,2,1,0:T(8,128)(2,1)S(1)}, bf16[1,1,512,320]{3,2,1,0:T(8,128)(2,1)S(1)}, u32[]{:S(2)}, u32[]{:S(2)}) collective-permute-start(bf16[1,1,512,320]{3,2,1,0:T(8,128)(2,1)S(1)} %get-tuple-element.13), channel_id=1, source_target_pairs={{0,16},{16,32},{32,48},{48,64},{64,80},{80,96},{96,112},{112,128},... | collective-permute-start | bytes 983048 | tf_op jit(solution)/shard_map/ppermute | solution.py:17
  46.9 14.9 %collective-permute-start.1 = (bf16[1,1,512,320]{3,2,1,0:T(8,128)(2,1)S(1)}, bf16[1,1,512,320]{3,2,1,0:T(8,128)(2,1)}, u32[]{:S(2)}, u32[]{:S(2)}) collective-permute-start(bf16[1,1,512,320]{3,2,1,0:T(8,128)(2,1)S(1)} %get-tuple-element.14), channel_id=1, source_target_pairs={{16,0},{32,16},{48,32},{64,48},{80,64},{96,80},{112,96},{128,112},... | collective-permute-start | bytes 983048 | tf_op jit(solution)/shard_map/ppermute | solution.py:18
  51.4 18.2 %all-to-all-start.3 = ((bf16[16,112,128]{2,1,0:T(8,128)(2,1)}), bf16[16,112,128]{2,1,0:T(8,128)(2,1)}, u32[]{:S(2)}, u32[]{:S(2)}) async-start(bf16[16,112,128]{2,1,0:T(8,128)(2,1)} %broadcast_select_fusion), calls=%async_computation.3 | async-start | bytes 917504 | tf_op jit(solution)/shard_map/all_to_all | solution.py:144
  61.0 0.8 copy-start.4
  71.2 18.3 %all-to-all-start.4 = ((bf16[16,112,128]{2,1,0:T(8,128)(2,1)}), bf16[16,112,128]{2,1,0:T(8,128)(2,1)}, u32[]{:S(2)}, u32[]{:S(2)}) async-start(bf16[16,112,128]{2,1,0:T(8,128)(2,1)} %broadcast_in_dim.64), calls=%async_computation.4 | async-start | bytes 917504 | tf_op jit(solution)/shard_map/all_to_all | solution.py:26
  127.9 7.2 %collective-permute-start.2 = (bf16[1,1,512,320]{3,2,1,0:T(8,128)(2,1)S(1)}, bf16[1,1,512,320]{3,2,1,0:T(8,128)(2,1)S(1)}, u32[]{:S(2)}, u32[]{:S(2)}) collective-permute-start(bf16[1,1,512,320]{3,2,1,0:T(8,128)(2,1)S(1)} %get-tuple-element.11), channel_id=1, source_target_pairs={{0,16},{16,32},{32,48},{48,64},{64,80},{80,96},{96,112},{112,128},... | collective-permute-start | bytes 983048 | tf_op jit(solution)/shard_map/ppermute | solution.py:17
  130.4 10.6 %collective-permute-start.3 = (bf16[1,1,512,320]{3,2,1,0:T(8,128)(2,1)S(1)}, bf16[1,1,512,320]{3,2,1,0:T(8,128)(2,1)S(1)}, u32[]{:S(2)}, u32[]{:S(2)}) collective-permute-start(bf16[1,1,512,320]{3,2,1,0:T(8,128)(2,1)S(1)} %get-tuple-element.12), channel_id=1, source_target_pairs={{16,0},{32,16},{48,32},{64,48},{80,64},{96,80},{112,96},{128,112},... | collective-permute-start | bytes 983048 | tf_op jit(solution)/shard_map/ppermute | solution.py:18

commit v5 on v4

--- a/solution.py
+++ b/solution.py
@@ -28,12 +28,12 @@
 
 def norm_stats(field, groups):
     field = field.astype(jnp.float32)
-    requests, rows, width, channels = field.shape
-    grouped = field.reshape(requests, rows, width, groups, channels // groups)
+    requests, rows, channels, width = field.shape
+    grouped = field.reshape(requests, rows, groups, channels // groups, width)
     count = rows * width * (channels // groups)
-    local_mean = jnp.sum(grouped, axis=(1, 2, 4)) / count
-    deviation = grouped - local_mean[:, None, None, :, None]
-    local_m2 = jnp.sum(deviation * deviation, axis=(1, 2, 4))
+    local_mean = jnp.sum(grouped, axis=(1, 3, 4)) / count
+    deviation = grouped - local_mean[:, None, :, None, None]
+    local_m2 = jnp.sum(deviation * deviation, axis=(1, 3, 4))
     stats = exchange(jnp.stack([local_mean, local_m2]), "band")
     means, m2s = stats[:, 0], stats[:, 1]
     bands = means.shape[0]
@@ -46,9 +46,9 @@
 
 def norm_silu(field, mean, scale, groups):
     field = field.astype(jnp.float32)
-    requests, rows, width, channels = field.shape
-    grouped = field.reshape(requests, rows, width, groups, channels // groups)
-    normed = (grouped - mean[:, None, None, :, None]) * scale[:, None, None, :, None]
+    requests, rows, channels, width = field.shape
+    grouped = field.reshape(requests, rows, groups, channels // groups, width)
+    normed = (grouped - mean[:, None, :, None, None]) * scale[:, None, :, None, None]
     return jax.nn.silu(normed.reshape(field.shape)).astype(jnp.bfloat16)
 
 
@@ -59,21 +59,26 @@
 
 def taps_by_column(field):
     none = (0, 0)
-    left = jnp.pad(field[:, :-1], (none, (1, 0), none))
-    right = jnp.pad(field[:, 1:], (none, (0, 1), none))
-    return jnp.concatenate([left, field, right], axis=-1)
+    left = jnp.pad(field[:, :, :-1], (none, none, (1, 0)))
+    right = jnp.pad(field[:, :, 1:], (none, none, (0, 1)))
+    return jnp.concatenate([left, field, right], axis=1)
+
+
+def tap_weights(kernel):
+    taps, cols, inner, outer = kernel.shape
+    return jnp.transpose(kernel, (0, 3, 1, 2)).reshape(taps, outer, cols * inner)
 
 
 def first_conv_kernel(x_ref, w_ref, u_ref, s_ref, o_ref):
     row = pl.program_id(0)
     total = None
     for tap in range(3):
-        t = jnp.dot(x_ref[row + tap], w_ref[tap], preferred_element_type=jnp.float32)
+        t = jnp.dot(w_ref[tap], x_ref[row + tap], preferred_element_type=jnp.float32)
         total = t if total is None else total + t
-    rank = u_ref.shape[0]
-    low = total[:, :rank]
-    main = total[:, w_ref.shape[-1] - o_ref.shape[-1] :]
-    lifted = jnp.dot(low.astype(jnp.bfloat16), u_ref[...], preferred_element_type=jnp.float32)
+    rank = u_ref.shape[1]
+    low = total[:rank]
+    main = total[w_ref.shape[1] - o_ref.shape[1] :]
+    lifted = jnp.dot(u_ref[...], low.astype(jnp.bfloat16), preferred_element_type=jnp.float32)
     o_ref[0] = main + lifted + s_ref[...]
 
 
@@ -81,18 +86,18 @@
     row = pl.program_id(0)
     total = None
     for tap in range(3):
-        t = jnp.dot(x_ref[row + tap], w_ref[tap], preferred_element_type=jnp.float32)
+        t = jnp.dot(w_ref[tap], x_ref[row + tap], preferred_element_type=jnp.float32)
         total = t if total is None else total + t
     o_ref[0] = (r_ref[0].astype(jnp.float32) + total).astype(o_ref.dtype)
 
 
-def first_conv(cols, weight, down, up, shift):
-    rows, width, wide = cols.shape[0] - 2, cols.shape[1], cols.shape[2]
-    out = weight.shape[-1]
-    rank = down.shape[-1]
+def first_conv(cols, weight, down, up_t, shift):
+    rows, wide, width = cols.shape[0] - 2, cols.shape[1], cols.shape[2]
+    out = weight.shape[1]
+    rank = down.shape[1]
     lead = -(-rank // 128) * 128
-    gap = jnp.zeros(down.shape[:-1] + (lead - rank,), down.dtype)
-    weight = jnp.concatenate([down, gap, weight], axis=-1)
+    base = jnp.concatenate([jnp.zeros((3, lead, wide), weight.dtype), weight], axis=1)
+    weight = lax.dynamic_update_slice(base, down, (0, 0, 0))
     flops = 2 * rows * width * wide * (out + lead) + 2 * rows * width * rank * out
     return pl.pallas_call(
         first_conv_kernel,
@@ -100,31 +105,31 @@
         in_specs=[
             pl.BlockSpec(cols.shape, lambda h: (0, 0, 0)),
             pl.BlockSpec(weight.shape, lambda h: (0, 0, 0)),
-            pl.BlockSpec(up.shape, lambda h: (0, 0)),
+            pl.BlockSpec(up_t.shape, lambda h: (0, 0)),
             pl.BlockSpec(shift.shape, lambda h: (0, 0)),
         ],
-        out_specs=pl.BlockSpec((1, width, out), lambda h: (h, 0, 0)),
-        out_shape=jax.ShapeDtypeStruct((rows, width, out), jnp.float32),
+        out_specs=pl.BlockSpec((1, out, width), lambda h: (h, 0, 0)),
+        out_shape=jax.ShapeDtypeStruct((rows, out, width), jnp.float32),
         cost_estimate=pl.CostEstimate(
             flops=flops, transcendentals=0,
             bytes_accessed=cols.size * 2 + weight.size * 2 + rows * width * out * 4,
         ),
-    )(cols, weight, up, shift)
+    )(cols, weight, up_t, shift)
 
 
 def second_conv(cols, weight, residual):
-    rows, width, wide = cols.shape[0] - 2, cols.shape[1], cols.shape[2]
-    out = weight.shape[-1]
+    rows, wide, width = cols.shape[0] - 2, cols.shape[1], cols.shape[2]
+    out = weight.shape[1]
     return pl.pallas_call(
         second_conv_kernel,
         grid=(rows,),
         in_specs=[
             pl.BlockSpec(cols.shape, lambda h: (0, 0, 0)),
             pl.BlockSpec(weight.shape, lambda h: (0, 0, 0)),
-            pl.BlockSpec((1, width, out), lambda h: (h, 0, 0)),
+            pl.BlockSpec((1, out, width), lambda h: (h, 0, 0)),
         ],
-        out_specs=pl.BlockSpec((1, width, out), lambda h: (h, 0, 0)),
-        out_shape=jax.ShapeDtypeStruct((rows, width, out), residual.dtype),
+        out_specs=pl.BlockSpec((1, out, width), lambda h: (h, 0, 0)),
+        out_shape=jax.ShapeDtypeStruct((rows, out, width), residual.dtype),
         cost_estimate=pl.CostEstimate(
             flops=2 * rows * width * wide * out, transcendentals=0,
             bytes_accessed=cols.size * 2 + weight.size * 2 + rows * width * out * 4,
@@ -171,20 +176,20 @@
         time_projection_weight,
         preferred_element_type=jnp.float32,
     )
-    wide = 3 * channels
+    field = jnp.swapaxes(latents, 2, 3)
     hidden = first_conv(
-        taps_by_column(conv_input(latents, G)[0]),
-        first_conv_weight.reshape(3, wide, channels),
-        chosen_down.reshape(3, wide, chosen_down.shape[-1]),
-        chosen_up,
-        shift,
+        taps_by_column(conv_input(field, G)[0]),
+        tap_weights(first_conv_weight),
+        tap_weights(chosen_down),
+        chosen_up.T,
+        shift.reshape(channels, 1),
     )[None]
     result = second_conv(
         taps_by_column(conv_input(hidden, G)[0]),
-        second_conv_weight.reshape(3, wide, channels),
-        latents[0],
+        tap_weights(second_conv_weight),
+        field[0],
     )
-    return result[None]
+    return jnp.swapaxes(result[None], 2, 3)
 
 
 def solution(mesh):

time: 163 us -> 146 us (0.90)
  other arithmetic: 32.4 us -> 21.7 us
  waiting for transfers between devices: 21.5 us -> 13 us
  local copies, waits for them, and re-layouts: 21.3 us -> 25.3 us
  Pallas kernels: 23.9 us -> 20.1 us
  starting transfers between devices: 47.7 us -> 49.9 us
    reshape x0 -> x5, local copies, waits for them, and re-layouts: none -> 8.22 us  [the longest x3 7.1 us: tap_weights(): jnp.transpose(kernel, (0, 3, 1, 2)).reshape(taps, outer, cols * inner)]
    concatenate x3 -> x2, other arithmetic: 16 us -> 9.21 us  [taps_by_column(): return jnp.concatenate([left, field, right], axis=1)]
    ppermute x2, waiting for transfers between devices: 5.9 us -> 0.01 us  [with_halo(): after = lax.ppermute(initial, axis, down)]
    all_to_all x3, waiting for transfers between devices: 9.02 us -> 12.6 us  [exchange(): return lax.all_to_all(spread, axis, 0, 0, tiled=True)]
    ppermute x2, waiting for transfers between devices: 2.77 us -> 0.01 us  [with_halo(): before = lax.ppermute(last, axis, up)]
    all_to_all x1, waiting for transfers between devices: 2.76 us -> 0.01 us  [fetch_adapter(): by_req = lax.all_to_all(wanted, 'req', 0, 0, tiled=True)]
    pallas_call x1, Pallas kernels: 11.6 us -> 8.89 us  [second_conv(): pl.pallas_call(second_conv_kernel, grid=(rows,), in_specs=[pl.BlockSpec(c...]
    unnamed x16 -> x21, local copies, waits for them, and re-layouts: 5.2 us -> 2.54 us
  transfers between devices with their start and end apart: 9 -> 9, of which waited for: 6 -> 4; matrix products, arithmetic and copies ran while one was open for 16% -> 22% of each run, Pallas kernels for 0% -> 0%
where the time goes in v5:
time: 146 us; the launch traced here: 144 us
  starting transfers between devices  49.9 us (34%)
  local copies, waits for them, and re-layouts  25.3 us (17%)
  other arithmetic  21.7 us (15%)
  Pallas kernels  20.1 us (14%)
  waiting for transfers between devices  13 us (9%)
  blocking collectives  10.8 us (7%)
  between operations  3.03 us (2%)
    all_to_all x3, starting transfers between devices, exchange(): return lax.all_to_all(spread, axis, 0, 0, tiled=True)  27 us
    all_to_all x3, waiting for transfers between devices, exchange(): return lax.all_to_all(spread, axis, 0, 0, tiled=True)  12.6 us
    pallas_call x1, Pallas kernels, first_conv(): pl.pallas_call(first_conv_kernel, grid=(rows,), in_specs=[pl.BlockSpec(co...  11.2 us
    all_to_all x1, blocking collectives, exchange(): return lax.all_to_all(spread, axis, 0, 0, tiled=True)  10.8 us
    ppermute x2, starting transfers between devices, with_halo(): before = lax.ppermute(last, axis, up)  9.88 us
    concatenate x2, other arithmetic, taps_by_column(): return jnp.concatenate([left, field, right], axis=1)  9.21 us
    pallas_call x1, Pallas kernels, second_conv(): pl.pallas_call(second_conv_kernel, grid=(rows,), in_specs=[pl.BlockSpec(c...  8.89 us
    reshape x3, local copies, waits for them, and re-layouts, tap_weights(): jnp.transpose(kernel, (0, 3, 1, 2)).reshape(taps, outer, cols * inner)  7.1 us
  transfers between devices with their start and end apart: 9, of which 4 were waited for; matrix products, arithmetic and copies ran while one was open for 22% of the time, Pallas kernels for 0%

profile of v5, /device:TPU:1, one launch (start us, length us, event | category | flops | bytes accessed | tf_op | source)
XLA Modules:
  0.0 144.2 jit_solution(5953083294362894406)
XLA Ops:
  1.4 10.1 %all-to-all-start.1 = ((s32[16,1,1]{2,1,0:T(1,128)}), s32[16,1,1]{2,1,0:T(1,128)S(1)}, u32[]{:S(2)}, u32[]{:S(2)}) async-start(s32[16,1,1]{2,1,0:T(1,128)} %broadcast_in_dim.58), calls=%async_computation.1 | async-start | bytes 16384 | tf_op jit(solution)/shard_map/all_to_all | solution.py:26
  11.5 1.6 %convert_reduce_fusion = f32[320]{0:T(512)S(1)} fusion(bf16[1,4,512,320]{2,3,1,0:T(8,128)(2,1)} %param.9), kind=kLoop, calls=%fused_computation.14 | loop fusion | flops 1310400 | bytes 1312000 | tf_op jit(solution)/shard_map/reduce_sum | solution.py:34
  13.5 1.8 %fusion.9 = f32[320]{0:T(512)S(1)} fusion(bf16[1,4,512,320]{2,3,1,0:T(8,128)(2,1)} %param.9, f32[320]{0:T(512)S(1)} %sub.103), kind=kLoop, calls=%fused_computation.16 | loop fusion | flops 2621120 | bytes 1313280 | tf_op jit(solution)/shard_map/reduce_sum | solution.py:36
  19.4 8.8 %all-to-all-start = ((f32[16,2,1,32]{3,2,1,0:T(1,128)}), f32[16,2,1,32]{3,2,1,0:T(1,128)S(1)}, u32[]{:S(2)}, u32[]{:S(2)}) async-start(f32[16,2,1,32]{3,2,1,0:T(1,128)} %broadcast_in_dim.31), calls=%async_computation | async-start | bytes 32768 | tf_op jit(solution)/shard_map/all_to_all | solution.py:26
  29.2 6.2 %all-to-all-done = f32[16,2,1,32]{3,2,1,0:T(1,128)S(1)} async-done(((f32[16,2,1,32]{3,2,1,0:T(1,128)}), f32[16,2,1,32]{3,2,1,0:T(1,128)S(1)}, u32[]{:S(2)}, u32[]{:S(2)}) %all-to-all-start) | async-done | bytes 4128 | tf_op jit(solution)/shard_map/all_to_all | solution.py:26
  35.4 3.7 %all-to-all-start.2 = ((bf16[16,112,128]{2,1,0:T(8,128)(2,1)}), bf16[16,112,128]{2,1,0:T(8,128)(2,1)S(1)}, u32[]{:S(2)}, u32[]{:S(2)}) async-start(bf16[16,112,128]{2,1,0:T(8,128)(2,1)} %bitcast.12), calls=%async_computation.2 | async-start | bytes 917504 | tf_op jit(solution)/shard_map/all_to_all | solution.py:147
  42.6 2.1 %collective-permute-start.1 = (bf16[1,1,320,512]{3,2,1,0:T(8,128)(2,1)}, bf16[1,1,320,512]{3,2,1,0:T(8,128)(2,1)}, u32[]{:S(2)}, u32[]{:S(2)}) collective-permute-start(bf16[1,1,320,512]{3,2,1,0:T(8,128)(2,1)} %get-tuple-element.14), channel_id=1, source_target_pairs={{16,0},{32,16},{48,32},{64,48},{80,64},{96,80},{112,96},{128,112},... | collective-permute-start | bytes 983048 | tf_op jit(solution)/shard_map/ppermute | solution.py:18
  44.7 4.9 %collective-permute-start = (bf16[1,1,320,512]{3,2,1,0:T(8,128)(2,1)}, bf16[1,1,320,512]{3,2,1,0:T(8,128)(2,1)}, u32[]{:S(2)}, u32[]{:S(2)}) collective-permute-start(bf16[1,1,320,512]{3,2,1,0:T(8,128)(2,1)} %get-tuple-element.13), channel_id=1, source_target_pairs={{0,16},{16,32},{32,48},{48,64},{64,80},{80,96},{96,112},{112,128},... | collective-permute-start | bytes 983048 | tf_op jit(solution)/shard_map/ppermute | solution.py:17
  51.5 4.7 %all-to-all-start.3 = ((bf16[16,112,128]{2,1,0:T(8,128)(2,1)}), bf16[16,112,128]{2,1,0:T(8,128)(2,1)S(1)}, u32[]{:S(2)}, u32[]{:S(2)}) async-start(bf16[16,112,128]{2,1,0:T(8,128)(2,1)} %broadcast_select_fusion), calls=%async_computation.3 | async-start | bytes 917504 | tf_op jit(solution)/shard_map/all_to_all | solution.py:149
  56.3 2.8 %copy.38 = bf16[3,320,960]{2,1,0:T(8,128)(2,1)S(1)} copy(bf16[3,320,960]{1,2,0:T(8,128)(2,1)} %bitcast.68) | data formatting | bytes 3686400 | tf_op jit(solution)/shard_map/reshape | solution.py:69
  60.2 1.9 %concatenate.20 = bf16[3,448,960]{2,1,0:T(8,128)(2,1)} pad(bf16[3,320,960]{2,1,0:T(8,128)(2,1)S(1)} %copy.38, bf16[]{:T(256)} %constant.77.clone.1), padding=0_0x128_0x0_0 | pad | bytes 4423682 | tf_op jit(solution)/shard_map/concatenate | solution.py:99
  64.6 1.7 %maximum_bitcast_fusion = bf16[6,320,512]{2,1,0:T(8,128)(2,1)S(1)} fusion(bf16[1,1,320,512]{3,2,1,0:T(8,128)(2,1)} %collective-permute-done.1, bf16[1,4,320,512]{3,2,1,0:T(8,128)(2,1)} %copy-done.4, bf16[1,1,320,512]{3,2,1,0:T(8,128)(2,1)} %collective-permute-done), kind=kLoop, calls=%fused_computation.26 | loop fusion | flops 1966080 | bytes 3932160 | tf_op jit(solution)/shard_map/squeeze | solution.py:181
  66.3 3.0 %fusion.33 = (bf16[6,320,511]{2,1,0:T(8,128)(2,1)}, bf16[6,320,511]{2,1,0:T(8,128)(2,1)}) fusion(bf16[6,320,512]{2,1,0:T(8,128)(2,1)S(1)} %maximum_bitcast_fusion), kind=kLoop, calls=%fused_computation.77 | loop fusion | bytes 7848960 | tf_op jit(solution)/shard_map/slice | solution.py:62
  70.1 8.2 %all-to-all-start.4 = ((bf16[16,112,128]{2,1,0:T(8,128)(2,1)}), bf16[16,112,128]{2,1,0:T(8,128)(2,1)S(1)}, u32[]{:S(2)}, u32[]{:S(2)}) async-start(bf16[16,112,128]{2,1,0:T(8,128)(2,1)} %broadcast_in_dim.62), calls=%async_computation.4 | async-start | bytes 917504 | tf_op jit(solution)/shard_map/all_to_all | solution.py:26
  78.3 5.7 %fusion.5.x_ref = bf16[6,960,512]{2,1,0:T(8,128)(2,1)} fusion(bf16[6,320,511]{2,1,0:T(8,128)(2,1)} %get-tuple-element.10, bf16[6,320,511]{2,1,0:T(8,128)(2,1)} %get-tuple-element.9, bf16[6,320,512]{2,1,0:T(8,128)(2,1)S(1)} %maximum_bitcast_fusion), kind=kLoop, calls=%fused_computation.9 | loop fusion | flops 29491200 | bytes 11788800 | tf_op jit(solution)/shard_map/concatenate | solution.py:64
  84.0 4.9 %all-to-all-done.4 = bf16[16,112,128]{2,1,0:T(8,128)(2,1)S(1)} async-done(((bf16[16,112,128]{2,1,0:T(8,128)(2,1)}), bf16[16,112,128]{2,1,0:T(8,128)(2,1)S(1)}, u32[]{:S(2)}, u32[]{:S(2)}) %all-to-all-start.4) | async-done | bytes 458784 | tf_op jit(solution)/shard_map/all_to_all | solution.py:26
  91.2 11.2 %shard_map.91 = f32[4,320,512]{2,1,0:T(8,128)} custom-call(bf16[6,960,512]{2,1,0:T(8,128)(2,1)} %fusion.5.x_ref, bf16[3,448,960]{2,1,0:T(8,128)(2,1)} %constant_dynamic-update-slice_fusion.w_ref, bf16[320,64]{1,0:T(8,128)(2,1)} %bitcast.72, f32[320,1]{1,0:T(8,128)} %reshape.436.s_ref), custom_call_target="tpu_custom_call" | custom-call | flops 1845493760 | bytes 11100160 | tf_op jit(solution)/shard_map/pallas_call | solution.py:102
  102.5 2.1 %reduce_sum.127 = f32[320]{0:T(512)S(1)} reduce(f32[4,320,512]{2,1,0:T(8,128)} %shard_map.91, f32[]{:T(128)} %constant.70.clone.1), dimensions={0,2}, to_apply=%region_7.8 | reduce | flops 655040 | bytes 2622724 | tf_op jit(solution)/shard_map/reduce_sum | solution.py:34
  105.7 10.8 %all_to_all.37 = f32[16,2,1,32]{3,2,1,0:T(1,128)S(1)} all-to-all(f32[16,2,1,32]{3,2,1,0:T(1,128)S(1)} %broadcast_in_dim.64), channel_id=1, replica_groups=mesh['band'=16,'req'=16] {'band'}, dimensions={0} | all-to-all | bytes 8192 | tf_op jit(solution)/shard_map/all_to_all | solution.py:26
  119.0 2.4 %collective-permute-start.3 = (bf16[1,1,320,512]{3,2,1,0:T(8,128)(2,1)S(1)}, bf16[1,1,320,512]{3,2,1,0:T(8,128)(2,1)S(1)}, u32[]{:S(2)}, u32[]{:S(2)}) collective-permute-start(bf16[1,1,320,512]{3,2,1,0:T(8,128)(2,1)S(1)} %get-tuple-element.12), channel_id=1, source_target_pairs={{16,0},{32,16},{48,32},{64,48},{80,64},{96,80},{112,96},{128,112},... | collective-permute-start | bytes 983048 | tf_op jit(solution)/shard_map/ppermute | solution.py:18
  121.5 4.9 %collective-permute-start.2 = (bf16[1,1,320,512]{3,2,1,0:T(8,128)(2,1)S(1)}, bf16[1,1,320,512]{3,2,1,0:T(8,128)(2,1)S(1)}, u32[]{:S(2)}, u32[]{:S(2)}) collective-permute-start(bf16[1,1,320,512]{3,2,1,0:T(8,128)(2,1)S(1)} %get-tuple-element.11), channel_id=1, source_target_pairs={{0,16},{16,32},{32,48},{48,64},{64,80},{80,96},{96,112},{112,128},... | collective-permute-start | bytes 983048 | tf_op jit(solution)/shard_map/ppermute | solution.py:17
  126.4 4.1 %copy.45.w_ref = bf16[3,320,960]{2,1,0:T(8,128)(2,1)} copy(bf16[3,320,960]{1,2,0:T(8,128)(2,1)} %bitcast.69) | data formatting | bytes 3686400 | tf_op jit(solution)/shard_map/reshape | solution.py:69
  131.8 3.5 %fusion.7.x_ref = bf16[6,960,512]{2,1,0:T(8,128)(2,1)} fusion(bf16[6,320,511]{2,1,0:T(8,128)(2,1)S(1)} %get-tuple-element.8, bf16[6,320,511]{2,1,0:T(8,128)(2,1)S(1)} %get-tuple-element.7, bf16[6,320,512]{2,1,0:T(8,128)(2,1)S(1)} %maximum_bitcast_fusion.1), kind=kLoop, calls=%fused_computation.11 | loop fusion | flops 29491200 | bytes 11788800 | tf_op jit(solution)/shard_map/concatenate | solution.py:64
  135.3 8.9 %shard_map.92 = bf16[4,320,512]{2,1,0:T(8,128)(2,1)} custom-call(bf16[6,960,512]{2,1,0:T(8,128)(2,1)} %fusion.7.x_ref, bf16[3,320,960]{2,1,0:T(8,128)(2,1)} %copy.45.w_ref, bf16[4,320,512]{2,1,0:T(8,128)(2,1)} %bitcast.66), custom_call_target="tpu_custom_call" | custom-call | flops 1258291200 | bytes 10362880 | tf_op jit(solution)/shard_map/pallas_call | solution.py:123
  (98 shorter events, 21.1 us)
Async XLA Ops:
  0.0 59.0 %copy-start = (bf16[1280,320]{0,1:T(8,128)(2,1)S(1)}, bf16[1280,320]{0,1:T(8,128)(2,1)}, u32[]{:S(2)}) copy-start(bf16[1280,320]{0,1:T(8,128)(2,1)} %param.17) | copy-start | bytes 2457604
  0.0 15.5 %copy-start.8 = (bf16[1,64,320]{2,1,0:T(8,128)(2,1)S(1)}, bf16[1,64,320]{2,1,0:T(8,128)(2,1)}, u32[]{:S(2)}) copy-start(bf16[1,64,320]{2,1,0:T(8,128)(2,1)} %param.15) | copy-start | bytes 122884
  0.0 15.7 %copy-start.7 = (bf16[1,3,3,320,64]{3,4,2,1,0:T(8,128)(2,1)S(1)}, bf16[1,3,3,320,64]{3,4,2,1,0:T(8,128)(2,1)}, u32[]{:S(2)}) copy-start(bf16[1,3,3,320,64]{3,4,2,1,0:T(8,128)(2,1)} %param.14) | copy-start | bytes 1105924
  1.4 17.4 %all-to-all-start.1 = ((s32[16,1,1]{2,1,0:T(1,128)}), s32[16,1,1]{2,1,0:T(1,128)S(1)}, u32[]{:S(2)}, u32[]{:S(2)}) async-start(s32[16,1,1]{2,1,0:T(1,128)} %broadcast_in_dim.58), calls=%async_computation.1 | async-start | bytes 16384 | tf_op jit(solution)/shard_map/all_to_all | solution.py:26
  13.1 15.4 %copy-start.1 = (s32[256]{0:T(256)S(1)}, s32[256]{0:T(256)}, u32[]{:S(2)}) copy-start(s32[256]{0:T(256)} %param.12) | copy-start | bytes 3076
  15.3 24.3 %copy-start.3 = (bf16[1,4,512,320]{2,3,1,0:T(8,128)(2,1)S(1)}, bf16[1,4,512,320]{2,3,1,0:T(8,128)(2,1)}, u32[]{:S(2)}) copy-start(bf16[1,4,512,320]{2,3,1,0:T(8,128)(2,1)} %param.9) | copy-start | bytes 3932164
  19.4 16.1 %all-to-all-start = ((f32[16,2,1,32]{3,2,1,0:T(1,128)}), f32[16,2,1,32]{3,2,1,0:T(1,128)S(1)}, u32[]{:S(2)}, u32[]{:S(2)}) async-start(f32[16,2,1,32]{3,2,1,0:T(1,128)} %broadcast_in_dim.31), calls=%async_computation | async-start | bytes 32768 | tf_op jit(solution)/shard_map/all_to_all | solution.py:26
  35.4 14.6 %all-to-all-start.2 = ((bf16[16,112,128]{2,1,0:T(8,128)(2,1)}), bf16[16,112,128]{2,1,0:T(8,128)(2,1)S(1)}, u32[]{:S(2)}, u32[]{:S(2)}) async-start(bf16[16,112,128]{2,1,0:T(8,128)(2,1)} %bitcast.12), calls=%async_computation.2 | async-start | bytes 917504 | tf_op jit(solution)/shard_map/all_to_all | solution.py:147
  40.6 1.1 copy-start.4
  42.6 22.1 %collective-permute-start.1 = (bf16[1,1,320,512]{3,2,1,0:T(8,128)(2,1)}, bf16[1,1,320,512]{3,2,1,0:T(8,128)(2,1)}, u32[]{:S(2)}, u32[]{:S(2)}) collective-permute-start(bf16[1,1,320,512]{3,2,1,0:T(8,128)(2,1)} %get-tuple-element.14), channel_id=1, source_target_pairs={{16,0},{32,16},{48,32},{64,48},{80,64},{96,80},{112,96},{128,112},... | collective-permute-start | bytes 983048 | tf_op jit(solution)/shard_map/ppermute | solution.py:18
  44.7 19.9 %collective-permute-start = (bf16[1,1,320,512]{3,2,1,0:T(8,128)(2,1)}, bf16[1,1,320,512]{3,2,1,0:T(8,128)(2,1)}, u32[]{:S(2)}, u32[]{:S(2)}) collective-permute-start(bf16[1,1,320,512]{3,2,1,0:T(8,128)(2,1)} %get-tuple-element.13), channel_id=1, source_target_pairs={{0,16},{16,32},{32,48},{48,64},{64,80},{80,96},{96,112},{112,128},... | collective-permute-start | bytes 983048 | tf_op jit(solution)/shard_map/ppermute | solution.py:17
  51.5 7.5 %copy-start.9 = (bf16[1,1280]{1,0:T(2,128)(2,1)S(1)}, bf16[1,1280]{1,0:T(2,128)(2,1)}, u32[]{:S(2)}) copy-start(bf16[1,1280]{1,0:T(2,128)(2,1)} %param.10) | copy-start | bytes 7684
  51.5 17.8 %all-to-all-start.3 = ((bf16[16,112,128]{2,1,0:T(8,128)(2,1)}), bf16[16,112,128]{2,1,0:T(8,128)(2,1)S(1)}, u32[]{:S(2)}, u32[]{:S(2)}) async-start(bf16[16,112,128]{2,1,0:T(8,128)(2,1)} %broadcast_select_fusion), calls=%async_computation.3 | async-start | bytes 917504 | tf_op jit(solution)/shard_map/all_to_all | solution.py:149
  70.1 18.8 %all-to-all-start.4 = ((bf16[16,112,128]{2,1,0:T(8,128)(2,1)}), bf16[16,112,128]{2,1,0:T(8,128)(2,1)S(1)}, u32[]{:S(2)}, u32[]{:S(2)}) async-start(bf16[16,112,128]{2,1,0:T(8,128)(2,1)} %broadcast_in_dim.62), calls=%async_computation.4 | async-start | bytes 917504 | tf_op jit(solution)/shard_map/all_to_all | solution.py:26
  102.5 2.5 %copy-start.2 = (f32[4,320,512]{2,1,0:T(8,128)S(1)}, f32[4,320,512]{2,1,0:T(8,128)}, u32[]{:S(2)}) copy-start(f32[4,320,512]{2,1,0:T(8,128)} %shard_map.91) | copy-start | bytes 7864324
  117.9 1.1 copy-start.5
  119.0 11.5 %copy-start.6 = (bf16[1,4,320,512]{3,2,1,0:T(8,128)(2,1)S(1)}, bf16[1,4,320,512]{3,2,1,0:T(8,128)(2,1)}, u32[]{:S(2)}) copy-start(bf16[1,4,320,512]{3,2,1,0:T(8,128)(2,1)} %copy-done.5) | copy-start | bytes 3932164
  119.0 11.5 %collective-permute-start.3 = (bf16[1,1,320,512]{3,2,1,0:T(8,128)(2,1)S(1)}, bf16[1,1,320,512]{3,2,1,0:T(8,128)(2,1)S(1)}, u32[]{:S(2)}, u32[]{:S(2)}) collective-permute-start(bf16[1,1,320,512]{3,2,1,0:T(8,128)(2,1)S(1)} %get-tuple-element.12), channel_id=1, source_target_pairs={{16,0},{32,16},{48,32},{64,48},{80,64},{96,80},{112,96},{128,112},... | collective-permute-start | bytes 983048 | tf_op jit(solution)/shard_map/ppermute | solution.py:18
  121.5 9.0 %collective-permute-start.2 = (bf16[1,1,320,512]{3,2,1,0:T(8,128)(2,1)S(1)}, bf16[1,1,320,512]{3,2,1,0:T(8,128)(2,1)S(1)}, u32[]{:S(2)}, u32[]{:S(2)}) collective-permute-start(bf16[1,1,320,512]{3,2,1,0:T(8,128)(2,1)S(1)} %get-tuple-element.11), channel_id=1, source_target_pairs={{0,16},{16,32},{32,48},{48,64},{64,80},{80,96},{96,112},{112,128},... | collective-permute-start | bytes 983048 | tf_op jit(solution)/shard_map/ppermute | solution.py:17

commit v6 on v5

--- a/solution.py
+++ b/solution.py
@@ -69,7 +69,7 @@
     return jnp.transpose(kernel, (0, 3, 1, 2)).reshape(taps, outer, cols * inner)
 
 
-def first_conv_kernel(x_ref, w_ref, u_ref, s_ref, o_ref):
+def first_conv_kernel(x_ref, w_ref, u_ref, s_ref, k_ref, o_ref):
     row = pl.program_id(0)
     total = None
     for tap in range(3):
@@ -91,12 +91,15 @@
     o_ref[0] = (r_ref[0].astype(jnp.float32) + total).astype(o_ref.dtype)
 
 
-def first_conv(cols, weight, down, up_t, shift):
+def merged_base(weight, rank):
+    lead = -(-rank // 128) * 128
+    return jnp.concatenate([jnp.zeros((3, lead, weight.shape[2]), weight.dtype), weight], axis=1)
+
+
+def first_conv(cols, base, down, up_t, shift, out, keep):
     rows, wide, width = cols.shape[0] - 2, cols.shape[1], cols.shape[2]
-    out = weight.shape[1]
     rank = down.shape[1]
-    lead = -(-rank // 128) * 128
-    base = jnp.concatenate([jnp.zeros((3, lead, wide), weight.dtype), weight], axis=1)
+    lead = base.shape[1] - out
     weight = lax.dynamic_update_slice(base, down, (0, 0, 0))
     flops = 2 * rows * width * wide * (out + lead) + 2 * rows * width * rank * out
     return pl.pallas_call(
@@ -107,6 +110,7 @@
             pl.BlockSpec(weight.shape, lambda h: (0, 0, 0)),
             pl.BlockSpec(up_t.shape, lambda h: (0, 0)),
             pl.BlockSpec(shift.shape, lambda h: (0, 0)),
+            pl.BlockSpec(memory_space=pl.ANY),
         ],
         out_specs=pl.BlockSpec((1, out, width), lambda h: (h, 0, 0)),
         out_shape=jax.ShapeDtypeStruct((rows, out, width), jnp.float32),
@@ -114,7 +118,7 @@
             flops=flops, transcendentals=0,
             bytes_accessed=cols.size * 2 + weight.size * 2 + rows * width * out * 4,
         ),
-    )(cols, weight, up_t, shift)
+    )(cols, weight, up_t, shift, keep)
 
 
 def second_conv(cols, weight, residual):
@@ -177,18 +181,18 @@
         preferred_element_type=jnp.float32,
     )
     field = jnp.swapaxes(latents, 2, 3)
+    base = merged_base(tap_weights(first_conv_weight), chosen_down.shape[-1])
+    second_weight = tap_weights(second_conv_weight)
     hidden = first_conv(
         taps_by_column(conv_input(field, G)[0]),
-        tap_weights(first_conv_weight),
+        base,
         tap_weights(chosen_down),
         chosen_up.T,
         shift.reshape(channels, 1),
+        channels,
+        second_weight,
     )[None]
-    result = second_conv(
-        taps_by_column(conv_input(hidden, G)[0]),
-        tap_weights(second_conv_weight),
-        field[0],
-    )
+    result = second_conv(taps_by_column(conv_input(hidden, G)[0]), second_weight, field[0])
     return jnp.swapaxes(result[None], 2, 3)
 
 

time: 146 us -> 148 us (1.014)
  waiting for transfers between devices: 13 us -> 17 us
    ppermute x2, waiting for transfers between devices: 0.01 us -> 2.82 us  [with_halo(): after = lax.ppermute(initial, axis, down)]
  transfers between devices with their start and end apart: 9 -> 9, of which waited for: 4 -> 6; matrix products, arithmetic and copies ran while one was open for 22% -> 22% of each run, Pallas kernels for 0% -> 0%
where the time goes in v6:
time: 148 us; the launch traced here: 147 us
  starting transfers between devices  49.6 us (34%)
  local copies, waits for them, and re-layouts  24.2 us (16%)
  other arithmetic  21.8 us (15%)
  Pallas kernels  20.1 us (14%)
  waiting for transfers between devices  17 us (11%)
  blocking collectives  10.8 us (7%)
  between operations  2.84 us (2%)
    all_to_all x3, starting transfers between devices, exchange(): return lax.all_to_all(spread, axis, 0, 0, tiled=True)  27.1 us
    all_to_all x3, waiting for transfers between devices, exchange(): return lax.all_to_all(spread, axis, 0, 0, tiled=True)  12.6 us
    pallas_call x1, Pallas kernels, first_conv(): pl.pallas_call(first_conv_kernel, grid=(rows,), in_specs=[pl.BlockSpec(co...  11.2 us
    all_to_all x1, blocking collectives, exchange(): return lax.all_to_all(spread, axis, 0, 0, tiled=True)  10.8 us
    ppermute x2, starting transfers between devices, with_halo(): before = lax.ppermute(last, axis, up)  9.7 us
    concatenate x2, other arithmetic, taps_by_column(): return jnp.concatenate([left, field, right], axis=1)  9.24 us
    pallas_call x1, Pallas kernels, second_conv(): pl.pallas_call(second_conv_kernel, grid=(rows,), in_specs=[pl.BlockSpec(c...  8.89 us
    reshape x3, local copies, waits for them, and re-layouts, tap_weights(): jnp.transpose(kernel, (0, 3, 1, 2)).reshape(taps, outer, cols * inner)  7.12 us
  transfers between devices with their start and end apart: 9, of which 6 were waited for; matrix products, arithmetic and copies ran while one was open for 22% of the time, Pallas kernels for 0%

profile of v6, /device:TPU:1, one launch (start us, length us, event | category | flops | bytes accessed | tf_op | source)
XLA Modules:
  0.0 146.8 jit_solution(6422248851365359792)
XLA Ops:
  1.4 10.1 %all-to-all-start.1 = ((s32[16,1,1]{2,1,0:T(1,128)}), s32[16,1,1]{2,1,0:T(1,128)S(1)}, u32[]{:S(2)}, u32[]{:S(2)}) async-start(s32[16,1,1]{2,1,0:T(1,128)} %broadcast_in_dim.58), calls=%async_computation.1 | async-start | bytes 16384 | tf_op jit(solution)/shard_map/all_to_all | solution.py:26
  13.5 1.8 %fusion.9 = f32[320]{0:T(512)S(1)} fusion(bf16[1,4,512,320]{2,3,1,0:T(8,128)(2,1)} %param.9, f32[320]{0:T(512)S(1)} %sub.103), kind=kLoop, calls=%fused_computation.16 | loop fusion | flops 2621120 | bytes 1313280 | tf_op jit(solution)/shard_map/reduce_sum | solution.py:36
  19.4 8.8 %all-to-all-start = ((f32[16,2,1,32]{3,2,1,0:T(1,128)}), f32[16,2,1,32]{3,2,1,0:T(1,128)S(1)}, u32[]{:S(2)}, u32[]{:S(2)}) async-start(f32[16,2,1,32]{3,2,1,0:T(1,128)} %broadcast_in_dim.31), calls=%async_computation | async-start | bytes 32768 | tf_op jit(solution)/shard_map/all_to_all | solution.py:26
  29.2 6.2 %all-to-all-done = f32[16,2,1,32]{3,2,1,0:T(1,128)S(1)} async-done(((f32[16,2,1,32]{3,2,1,0:T(1,128)}), f32[16,2,1,32]{3,2,1,0:T(1,128)S(1)}, u32[]{:S(2)}, u32[]{:S(2)}) %all-to-all-start) | async-done | bytes 4128 | tf_op jit(solution)/shard_map/all_to_all | solution.py:26
  35.4 3.7 %all-to-all-start.2 = ((bf16[16,112,128]{2,1,0:T(8,128)(2,1)}), bf16[16,112,128]{2,1,0:T(8,128)(2,1)S(1)}, u32[]{:S(2)}, u32[]{:S(2)}) async-start(bf16[16,112,128]{2,1,0:T(8,128)(2,1)} %bitcast.12), calls=%async_computation.2 | async-start | bytes 917504 | tf_op jit(solution)/shard_map/all_to_all | solution.py:151
  42.6 2.1 %collective-permute-start.1 = (bf16[1,1,320,512]{3,2,1,0:T(8,128)(2,1)}, bf16[1,1,320,512]{3,2,1,0:T(8,128)(2,1)}, u32[]{:S(2)}, u32[]{:S(2)}) collective-permute-start(bf16[1,1,320,512]{3,2,1,0:T(8,128)(2,1)} %get-tuple-element.14), channel_id=1, source_target_pairs={{16,0},{32,16},{48,32},{64,48},{80,64},{96,80},{112,96},{128,112},... | collective-permute-start | bytes 983048 | tf_op jit(solution)/shard_map/ppermute | solution.py:18
  44.7 4.9 %collective-permute-start = (bf16[1,1,320,512]{3,2,1,0:T(8,128)(2,1)}, bf16[1,1,320,512]{3,2,1,0:T(8,128)(2,1)}, u32[]{:S(2)}, u32[]{:S(2)}) collective-permute-start(bf16[1,1,320,512]{3,2,1,0:T(8,128)(2,1)} %get-tuple-element.13), channel_id=1, source_target_pairs={{0,16},{16,32},{32,48},{48,64},{64,80},{80,96},{96,112},{112,128},... | collective-permute-start | bytes 983048 | tf_op jit(solution)/shard_map/ppermute | solution.py:17
  51.5 4.7 %all-to-all-start.3 = ((bf16[16,112,128]{2,1,0:T(8,128)(2,1)}), bf16[16,112,128]{2,1,0:T(8,128)(2,1)S(1)}, u32[]{:S(2)}, u32[]{:S(2)}) async-start(bf16[16,112,128]{2,1,0:T(8,128)(2,1)} %broadcast_select_fusion), calls=%async_computation.3 | async-start | bytes 917504 | tf_op jit(solution)/shard_map/all_to_all | solution.py:153
  56.3 2.8 %copy.42 = bf16[3,320,960]{2,1,0:T(8,128)(2,1)S(1)} copy(bf16[3,320,960]{1,2,0:T(8,128)(2,1)} %bitcast.68) | data formatting | bytes 3686400 | tf_op jit(solution)/shard_map/reshape | solution.py:69
  60.2 4.1 %copy.47.k_ref.w_ref = bf16[3,320,960]{2,1,0:T(8,128)(2,1)} copy(bf16[3,320,960]{1,2,0:T(8,128)(2,1)} %bitcast.69) | data formatting | bytes 3686400 | tf_op jit(solution)/shard_map/reshape | solution.py:69
  64.3 1.9 %concatenate.20 = bf16[3,448,960]{2,1,0:T(8,128)(2,1)} pad(bf16[3,320,960]{2,1,0:T(8,128)(2,1)S(1)} %copy.42, bf16[]{:T(256)} %constant.77.clone.1), padding=0_0x128_0x0_0 | pad | bytes 4423682 | tf_op jit(solution)/shard_map/concatenate | solution.py:96
  68.5 1.7 %maximum_bitcast_fusion = bf16[6,320,512]{2,1,0:T(8,128)(2,1)S(1)} fusion(bf16[1,1,320,512]{3,2,1,0:T(8,128)(2,1)} %collective-permute-done.1, bf16[1,4,320,512]{3,2,1,0:T(8,128)(2,1)} %copy-done.4, bf16[1,1,320,512]{3,2,1,0:T(8,128)(2,1)} %collective-permute-done), kind=kLoop, calls=%fused_computation.26 | loop fusion | flops 1966080 | bytes 3932160 | tf_op jit(solution)/shard_map/squeeze | solution.py:187
  70.2 3.0 %fusion.33 = (bf16[6,320,511]{2,1,0:T(8,128)(2,1)}, bf16[6,320,511]{2,1,0:T(8,128)(2,1)}) fusion(bf16[6,320,512]{2,1,0:T(8,128)(2,1)S(1)} %maximum_bitcast_fusion), kind=kLoop, calls=%fused_computation.77 | loop fusion | bytes 7848960 | tf_op jit(solution)/shard_map/slice | solution.py:62
  74.1 8.2 %all-to-all-start.4 = ((bf16[16,112,128]{2,1,0:T(8,128)(2,1)}), bf16[16,112,128]{2,1,0:T(8,128)(2,1)S(1)}, u32[]{:S(2)}, u32[]{:S(2)}) async-start(bf16[16,112,128]{2,1,0:T(8,128)(2,1)} %broadcast_in_dim.62), calls=%async_computation.4 | async-start | bytes 917504 | tf_op jit(solution)/shard_map/all_to_all | solution.py:26
  82.2 5.8 %fusion.5.x_ref = bf16[6,960,512]{2,1,0:T(8,128)(2,1)} fusion(bf16[6,320,511]{2,1,0:T(8,128)(2,1)} %get-tuple-element.10, bf16[6,320,511]{2,1,0:T(8,128)(2,1)} %get-tuple-element.9, bf16[6,320,512]{2,1,0:T(8,128)(2,1)S(1)} %maximum_bitcast_fusion), kind=kLoop, calls=%fused_computation.9 | loop fusion | flops 29491200 | bytes 11788800 | tf_op jit(solution)/shard_map/concatenate | solution.py:64
  88.0 4.9 %all-to-all-done.4 = bf16[16,112,128]{2,1,0:T(8,128)(2,1)S(1)} async-done(((bf16[16,112,128]{2,1,0:T(8,128)(2,1)}), bf16[16,112,128]{2,1,0:T(8,128)(2,1)S(1)}, u32[]{:S(2)}, u32[]{:S(2)}) %all-to-all-start.4) | async-done | bytes 458784 | tf_op jit(solution)/shard_map/all_to_all | solution.py:26
  95.2 11.2 %shard_map.91 = f32[4,320,512]{2,1,0:T(8,128)} custom-call(bf16[6,960,512]{2,1,0:T(8,128)(2,1)} %fusion.5.x_ref, bf16[3,448,960]{2,1,0:T(8,128)(2,1)} %constant_dynamic-update-slice_fusion.w_ref, bf16[320,64]{1,0:T(8,128)(2,1)} %bitcast.72, f32[320,1]{1,0:T(8,128)} %reshape.436.s_ref, bf16[3,320,960]{2,1,0:T(8,128)(2,1)} %copy.47.k_ref.w_ref), custom_call_target="tpu_custom_call" | custom-call | flops 1845493760 | bytes 11100160 | tf_op jit(solution)/shard_map/pallas_call | solution.py:105
  106.4 2.1 %reduce_sum.127 = f32[320]{0:T(512)S(1)} reduce(f32[4,320,512]{2,1,0:T(8,128)} %shard_map.91, f32[]{:T(128)} %constant.70.clone.1), dimensions={0,2}, to_apply=%region_7.8 | reduce | flops 655040 | bytes 2622724 | tf_op jit(solution)/shard_map/reduce_sum | solution.py:34
  109.7 10.8 %all_to_all.37 = f32[16,2,1,32]{3,2,1,0:T(1,128)S(1)} all-to-all(f32[16,2,1,32]{3,2,1,0:T(1,128)S(1)} %broadcast_in_dim.64), channel_id=1, replica_groups=mesh['band'=16,'req'=16] {'band'}, dimensions={0} | all-to-all | bytes 8192 | tf_op jit(solution)/shard_map/all_to_all | solution.py:26
  121.9 2.3 %collective-permute-start.3 = (bf16[1,1,320,512]{3,2,1,0:T(8,128)(2,1)S(1)}, bf16[1,1,320,512]{3,2,1,0:T(8,128)(2,1)S(1)}, u32[]{:S(2)}, u32[]{:S(2)}) collective-permute-start(bf16[1,1,320,512]{3,2,1,0:T(8,128)(2,1)S(1)} %get-tuple-element.12), channel_id=1, source_target_pairs={{16,0},{32,16},{48,32},{64,48},{80,64},{96,80},{112,96},{128,112},... | collective-permute-start | bytes 983048 | tf_op jit(solution)/shard_map/ppermute | solution.py:18
  124.2 4.8 %collective-permute-start.2 = (bf16[1,1,320,512]{3,2,1,0:T(8,128)(2,1)S(1)}, bf16[1,1,320,512]{3,2,1,0:T(8,128)(2,1)S(1)}, u32[]{:S(2)}, u32[]{:S(2)}) collective-permute-start(bf16[1,1,320,512]{3,2,1,0:T(8,128)(2,1)S(1)} %get-tuple-element.11), channel_id=1, source_target_pairs={{0,16},{16,32},{32,48},{48,64},{64,80},{80,96},{96,112},{112,128},... | collective-permute-start | bytes 983048 | tf_op jit(solution)/shard_map/ppermute | solution.py:17
  129.0 2.8 %collective-permute-done.3 = bf16[1,1,320,512]{3,2,1,0:T(8,128)(2,1)S(1)} collective-permute-done((bf16[1,1,320,512]{3,2,1,0:T(8,128)(2,1)S(1)}, bf16[1,1,320,512]{3,2,1,0:T(8,128)(2,1)S(1)}, u32[]{:S(2)}, u32[]{:S(2)}) %collective-permute-start.3) | collective-permute-done | bytes 327712 | tf_op jit(solution)/shard_map/ppermute | solution.py:18
  134.4 3.5 %fusion.7.x_ref = bf16[6,960,512]{2,1,0:T(8,128)(2,1)} fusion(bf16[6,320,511]{2,1,0:T(8,128)(2,1)S(1)} %get-tuple-element.8, bf16[6,320,511]{2,1,0:T(8,128)(2,1)S(1)} %get-tuple-element.7, bf16[6,320,512]{2,1,0:T(8,128)(2,1)S(1)} %maximum_bitcast_fusion.1), kind=kLoop, calls=%fused_computation.11 | loop fusion | flops 29491200 | bytes 11788800 | tf_op jit(solution)/shard_map/concatenate | solution.py:64
  137.9 8.9 %shard_map.92 = bf16[4,320,512]{2,1,0:T(8,128)(2,1)} custom-call(bf16[6,960,512]{2,1,0:T(8,128)(2,1)} %fusion.7.x_ref, bf16[3,320,960]{2,1,0:T(8,128)(2,1)} %copy.47.k_ref.w_ref, bf16[4,320,512]{2,1,0:T(8,128)(2,1)} %bitcast.66), custom_call_target="tpu_custom_call" | custom-call | flops 1258291200 | bytes 10362880 | tf_op jit(solution)/shard_map/pallas_call | solution.py:127
  (94 shorter events, 22.8 us)
Async XLA Ops:
  0.0 59.1 %copy-start = (bf16[1280,320]{0,1:T(8,128)(2,1)S(1)}, bf16[1280,320]{0,1:T(8,128)(2,1)}, u32[]{:S(2)}) copy-start(bf16[1280,320]{0,1:T(8,128)(2,1)} %param.17) | copy-start | bytes 2457604
  0.0 15.5 %copy-start.6 = (bf16[1,64,320]{2,1,0:T(8,128)(2,1)S(1)}, bf16[1,64,320]{2,1,0:T(8,128)(2,1)}, u32[]{:S(2)}) copy-start(bf16[1,64,320]{2,1,0:T(8,128)(2,1)} %param.15) | copy-start | bytes 122884
  0.0 15.7 %copy-start.5 = (bf16[1,3,3,320,64]{3,4,2,1,0:T(8,128)(2,1)S(1)}, bf16[1,3,3,320,64]{3,4,2,1,0:T(8,128)(2,1)}, u32[]{:S(2)}) copy-start(bf16[1,3,3,320,64]{3,4,2,1,0:T(8,128)(2,1)} %param.14) | copy-start | bytes 1105924
  1.4 17.4 %all-to-all-start.1 = ((s32[16,1,1]{2,1,0:T(1,128)}), s32[16,1,1]{2,1,0:T(1,128)S(1)}, u32[]{:S(2)}, u32[]{:S(2)}) async-start(s32[16,1,1]{2,1,0:T(1,128)} %broadcast_in_dim.58), calls=%async_computation.1 | async-start | bytes 16384 | tf_op jit(solution)/shard_map/all_to_all | solution.py:26
  13.1 15.4 %copy-start.1 = (s32[256]{0:T(256)S(1)}, s32[256]{0:T(256)}, u32[]{:S(2)}) copy-start(s32[256]{0:T(256)} %param.12) | copy-start | bytes 3076
  15.3 24.3 %copy-start.3 = (bf16[1,4,512,320]{2,3,1,0:T(8,128)(2,1)S(1)}, bf16[1,4,512,320]{2,3,1,0:T(8,128)(2,1)}, u32[]{:S(2)}) copy-start(bf16[1,4,512,320]{2,3,1,0:T(8,128)(2,1)} %param.9) | copy-start | bytes 3932164
  19.4 16.1 %all-to-all-start = ((f32[16,2,1,32]{3,2,1,0:T(1,128)}), f32[16,2,1,32]{3,2,1,0:T(1,128)S(1)}, u32[]{:S(2)}, u32[]{:S(2)}) async-start(f32[16,2,1,32]{3,2,1,0:T(1,128)} %broadcast_in_dim.31), calls=%async_computation | async-start | bytes 32768 | tf_op jit(solution)/shard_map/all_to_all | solution.py:26
  35.4 14.6 %all-to-all-start.2 = ((bf16[16,112,128]{2,1,0:T(8,128)(2,1)}), bf16[16,112,128]{2,1,0:T(8,128)(2,1)S(1)}, u32[]{:S(2)}, u32[]{:S(2)}) async-start(bf16[16,112,128]{2,1,0:T(8,128)(2,1)} %bitcast.12), calls=%async_computation.2 | async-start | bytes 917504 | tf_op jit(solution)/shard_map/all_to_all | solution.py:151
  40.6 1.1 copy-start.4
  42.6 25.9 %collective-permute-start.1 = (bf16[1,1,320,512]{3,2,1,0:T(8,128)(2,1)}, bf16[1,1,320,512]{3,2,1,0:T(8,128)(2,1)}, u32[]{:S(2)}, u32[]{:S(2)}) collective-permute-start(bf16[1,1,320,512]{3,2,1,0:T(8,128)(2,1)} %get-tuple-element.14), channel_id=1, source_target_pairs={{16,0},{32,16},{48,32},{64,48},{80,64},{96,80},{112,96},{128,112},... | collective-permute-start | bytes 983048 | tf_op jit(solution)/shard_map/ppermute | solution.py:18
  44.7 23.8 %collective-permute-start = (bf16[1,1,320,512]{3,2,1,0:T(8,128)(2,1)}, bf16[1,1,320,512]{3,2,1,0:T(8,128)(2,1)}, u32[]{:S(2)}, u32[]{:S(2)}) collective-permute-start(bf16[1,1,320,512]{3,2,1,0:T(8,128)(2,1)} %get-tuple-element.13), channel_id=1, source_target_pairs={{0,16},{16,32},{32,48},{48,64},{64,80},{80,96},{96,112},{112,128},... | collective-permute-start | bytes 983048 | tf_op jit(solution)/shard_map/ppermute | solution.py:17
  51.5 7.5 %copy-start.7 = (bf16[1,1280]{1,0:T(2,128)(2,1)S(1)}, bf16[1,1280]{1,0:T(2,128)(2,1)}, u32[]{:S(2)}) copy-start(bf16[1,1280]{1,0:T(2,128)(2,1)} %param.10) | copy-start | bytes 7684
  51.5 21.7 %all-to-all-start.3 = ((bf16[16,112,128]{2,1,0:T(8,128)(2,1)}), bf16[16,112,128]{2,1,0:T(8,128)(2,1)S(1)}, u32[]{:S(2)}, u32[]{:S(2)}) async-start(bf16[16,112,128]{2,1,0:T(8,128)(2,1)} %broadcast_select_fusion), calls=%async_computation.3 | async-start | bytes 917504 | tf_op jit(solution)/shard_map/all_to_all | solution.py:153
  74.1 18.9 %all-to-all-start.4 = ((bf16[16,112,128]{2,1,0:T(8,128)(2,1)}), bf16[16,112,128]{2,1,0:T(8,128)(2,1)S(1)}, u32[]{:S(2)}, u32[]{:S(2)}) async-start(bf16[16,112,128]{2,1,0:T(8,128)(2,1)} %broadcast_in_dim.62), calls=%async_computation.4 | async-start | bytes 917504 | tf_op jit(solution)/shard_map/all_to_all | solution.py:26
  106.4 2.5 %copy-start.2 = (f32[4,320,512]{2,1,0:T(8,128)S(1)}, f32[4,320,512]{2,1,0:T(8,128)}, u32[]{:S(2)}) copy-start(f32[4,320,512]{2,1,0:T(8,128)} %shard_map.91) | copy-start | bytes 7864324
  121.9 9.9 %collective-permute-start.3 = (bf16[1,1,320,512]{3,2,1,0:T(8,128)(2,1)S(1)}, bf16[1,1,320,512]{3,2,1,0:T(8,128)(2,1)S(1)}, u32[]{:S(2)}, u32[]{:S(2)}) collective-permute-start(bf16[1,1,320,512]{3,2,1,0:T(8,128)(2,1)S(1)} %get-tuple-element.12), channel_id=1, source_target_pairs={{16,0},{32,16},{48,32},{64,48},{80,64},{96,80},{112,96},{128,112},... | collective-permute-start | bytes 983048 | tf_op jit(solution)/shard_map/ppermute | solution.py:18
  124.2 8.9 %collective-permute-start.2 = (bf16[1,1,320,512]{3,2,1,0:T(8,128)(2,1)S(1)}, bf16[1,1,320,512]{3,2,1,0:T(8,128)(2,1)S(1)}, u32[]{:S(2)}, u32[]{:S(2)}) collective-permute-start(bf16[1,1,320,512]{3,2,1,0:T(8,128)(2,1)S(1)} %get-tuple-element.11), channel_id=1, source_target_pairs={{0,16},{16,32},{32,48},{48,64},{64,80},{80,96},{96,112},{112,128},... | collective-permute-start | bytes 983048 | tf_op jit(solution)/shard_map/ppermute | solution.py:17

commit v7 on v5

--- a/solution.py
+++ b/solution.py
@@ -64,6 +64,10 @@
     return jnp.concatenate([left, field, right], axis=1)
 
 
+def wide_of(kernel):
+    return kernel.shape[1] * kernel.shape[2]
+
+
 def tap_weights(kernel):
     taps, cols, inner, outer = kernel.shape
     return jnp.transpose(kernel, (0, 3, 1, 2)).reshape(taps, outer, cols * inner)
@@ -86,7 +90,9 @@
     row = pl.program_id(0)
     total = None
     for tap in range(3):
-        t = jnp.dot(w_ref[tap], x_ref[row + tap], preferred_element_type=jnp.float32)
+        t = lax.dot_general(
+            w_ref[tap], x_ref[row + tap], (((0,), (0,)), ((), ())), preferred_element_type=jnp.float32
+        )
         total = t if total is None else total + t
     o_ref[0] = (r_ref[0].astype(jnp.float32) + total).astype(o_ref.dtype)
 
@@ -119,7 +125,7 @@
 
 def second_conv(cols, weight, residual):
     rows, wide, width = cols.shape[0] - 2, cols.shape[1], cols.shape[2]
-    out = weight.shape[1]
+    out = weight.shape[2]
     return pl.pallas_call(
         second_conv_kernel,
         grid=(rows,),
@@ -186,7 +192,7 @@
     )[None]
     result = second_conv(
         taps_by_column(conv_input(hidden, G)[0]),
-        tap_weights(second_conv_weight),
+        second_conv_weight.reshape(3, wide_of(second_conv_weight), channels),
         field[0],
     )
     return jnp.swapaxes(result[None], 2, 3)

time: 146 us -> 145 us (level)
  local copies, waits for them, and re-layouts: 25.3 us -> 20.1 us
  waiting for transfers between devices: 13 us -> 16.9 us
    reshape x3 -> x2, local copies, waits for them, and re-layouts: 7.1 us -> 3.04 us  [tap_weights(): jnp.transpose(kernel, (0, 3, 1, 2)).reshape(taps, outer, cols * inner)]
    ppermute x2, waiting for transfers between devices: 0.01 us -> 2.64 us  [with_halo(): after = lax.ppermute(initial, axis, down)]
  transfers between devices with their start and end apart: 9 -> 9, of which waited for: 4 -> 6; matrix products, arithmetic and copies ran while one was open for 22% -> 19% of each run, Pallas kernels for 0% -> 0%
where the time goes in v7:
time: 145 us; the launch traced here: 143 us
  starting transfers between devices  49.8 us (34%)
  other arithmetic  21.7 us (15%)
  Pallas kernels  20.3 us (14%)
  local copies, waits for them, and re-layouts  20.1 us (14%)
  waiting for transfers between devices  16.9 us (12%)
  blocking collectives  10.8 us (7%)
  between operations  3.01 us (2%)
    all_to_all x3, starting transfers between devices, exchange(): return lax.all_to_all(spread, axis, 0, 0, tiled=True)  27 us
    all_to_all x3, waiting for transfers between devices, exchange(): return lax.all_to_all(spread, axis, 0, 0, tiled=True)  12.6 us
    pallas_call x1, Pallas kernels, first_conv(): pl.pallas_call(first_conv_kernel, grid=(rows,), in_specs=[pl.BlockSpec(co...  11.2 us
    all_to_all x1, blocking collectives, exchange(): return lax.all_to_all(spread, axis, 0, 0, tiled=True)  10.8 us
    ppermute x2, starting transfers between devices, with_halo(): before = lax.ppermute(last, axis, up)  9.88 us
    concatenate x2, other arithmetic, taps_by_column(): return jnp.concatenate([left, field, right], axis=1)  9.21 us
    pallas_call x1, Pallas kernels, second_conv(): pl.pallas_call(second_conv_kernel, grid=(rows,), in_specs=[pl.BlockSpec(c...  9.11 us
    all_to_all x1, starting transfers between devices, fetch_adapter(): by_req = lax.all_to_all(wanted, 'req', 0, 0, tiled=True)  4.73 us
  transfers between devices with their start and end apart: 9, of which 6 were waited for; matrix products, arithmetic and copies ran while one was open for 19% of the time, Pallas kernels for 0%

profile of v7, /device:TPU:1, one launch (start us, length us, event | category | flops | bytes accessed | tf_op | source)
XLA Modules:
  0.0 143.0 jit_solution(14287589623293742170)
XLA Ops:
  1.4 10.1 %all-to-all-start.1 = ((s32[16,1,1]{2,1,0:T(1,128)}), s32[16,1,1]{2,1,0:T(1,128)S(1)}, u32[]{:S(2)}, u32[]{:S(2)}) async-start(s32[16,1,1]{2,1,0:T(1,128)} %broadcast_in_dim.58), calls=%async_computation.1 | async-start | bytes 16384 | tf_op jit(solution)/shard_map/all_to_all | solution.py:26
  11.5 1.6 %convert_reduce_fusion = f32[320]{0:T(512)S(1)} fusion(bf16[1,4,512,320]{2,3,1,0:T(8,128)(2,1)} %param.9), kind=kLoop, calls=%fused_computation.14 | loop fusion | flops 1310400 | bytes 1312000 | tf_op jit(solution)/shard_map/reduce_sum | solution.py:34
  13.5 1.8 %fusion.9 = f32[320]{0:T(512)S(1)} fusion(bf16[1,4,512,320]{2,3,1,0:T(8,128)(2,1)} %param.9, f32[320]{0:T(512)S(1)} %sub.103), kind=kLoop, calls=%fused_computation.16 | loop fusion | flops 2621120 | bytes 1313280 | tf_op jit(solution)/shard_map/reduce_sum | solution.py:36
  19.4 8.8 %all-to-all-start = ((f32[16,2,1,32]{3,2,1,0:T(1,128)}), f32[16,2,1,32]{3,2,1,0:T(1,128)S(1)}, u32[]{:S(2)}, u32[]{:S(2)}) async-start(f32[16,2,1,32]{3,2,1,0:T(1,128)} %broadcast_in_dim.31), calls=%async_computation | async-start | bytes 32768 | tf_op jit(solution)/shard_map/all_to_all | solution.py:26
  29.2 6.2 %all-to-all-done = f32[16,2,1,32]{3,2,1,0:T(1,128)S(1)} async-done(((f32[16,2,1,32]{3,2,1,0:T(1,128)}), f32[16,2,1,32]{3,2,1,0:T(1,128)S(1)}, u32[]{:S(2)}, u32[]{:S(2)}) %all-to-all-start) | async-done | bytes 4128 | tf_op jit(solution)/shard_map/all_to_all | solution.py:26
  35.4 3.7 %all-to-all-start.2 = ((bf16[16,112,128]{2,1,0:T(8,128)(2,1)}), bf16[16,112,128]{2,1,0:T(8,128)(2,1)S(1)}, u32[]{:S(2)}, u32[]{:S(2)}) async-start(bf16[16,112,128]{2,1,0:T(8,128)(2,1)} %bitcast.12), calls=%async_computation.2 | async-start | bytes 917504 | tf_op jit(solution)/shard_map/all_to_all | solution.py:153
  42.6 2.1 %collective-permute-start.1 = (bf16[1,1,320,512]{3,2,1,0:T(8,128)(2,1)}, bf16[1,1,320,512]{3,2,1,0:T(8,128)(2,1)}, u32[]{:S(2)}, u32[]{:S(2)}) collective-permute-start(bf16[1,1,320,512]{3,2,1,0:T(8,128)(2,1)} %get-tuple-element.14), channel_id=1, source_target_pairs={{16,0},{32,16},{48,32},{64,48},{80,64},{96,80},{112,96},{128,112},... | collective-permute-start | bytes 983048 | tf_op jit(solution)/shard_map/ppermute | solution.py:18
  44.7 4.9 %collective-permute-start = (bf16[1,1,320,512]{3,2,1,0:T(8,128)(2,1)}, bf16[1,1,320,512]{3,2,1,0:T(8,128)(2,1)}, u32[]{:S(2)}, u32[]{:S(2)}) collective-permute-start(bf16[1,1,320,512]{3,2,1,0:T(8,128)(2,1)} %get-tuple-element.13), channel_id=1, source_target_pairs={{0,16},{16,32},{32,48},{48,64},{64,80},{80,96},{96,112},{112,128},... | collective-permute-start | bytes 983048 | tf_op jit(solution)/shard_map/ppermute | solution.py:17
  51.5 4.7 %all-to-all-start.3 = ((bf16[16,112,128]{2,1,0:T(8,128)(2,1)}), bf16[16,112,128]{2,1,0:T(8,128)(2,1)S(1)}, u32[]{:S(2)}, u32[]{:S(2)}) async-start(bf16[16,112,128]{2,1,0:T(8,128)(2,1)} %broadcast_select_fusion), calls=%async_computation.3 | async-start | bytes 917504 | tf_op jit(solution)/shard_map/all_to_all | solution.py:155
  56.3 2.8 %copy.33 = bf16[3,320,960]{2,1,0:T(8,128)(2,1)S(1)} copy(bf16[3,320,960]{1,2,0:T(8,128)(2,1)} %bitcast.66) | data formatting | bytes 3686400 | tf_op jit(solution)/shard_map/reshape | solution.py:73
  60.2 1.9 %concatenate.20 = bf16[3,448,960]{2,1,0:T(8,128)(2,1)} pad(bf16[3,320,960]{2,1,0:T(8,128)(2,1)S(1)} %copy.33, bf16[]{:T(256)} %constant.77.clone.1), padding=0_0x128_0x0_0 | pad | bytes 4423682 | tf_op jit(solution)/shard_map/concatenate | solution.py:105
  64.6 1.7 %maximum_bitcast_fusion = bf16[6,320,512]{2,1,0:T(8,128)(2,1)S(1)} fusion(bf16[1,1,320,512]{3,2,1,0:T(8,128)(2,1)} %collective-permute-done.1, bf16[1,4,320,512]{3,2,1,0:T(8,128)(2,1)} %copy-done.4, bf16[1,1,320,512]{3,2,1,0:T(8,128)(2,1)} %collective-permute-done), kind=kLoop, calls=%fused_computation.26 | loop fusion | flops 1966080 | bytes 3932160 | tf_op jit(solution)/shard_map/squeeze | solution.py:187
  66.3 3.0 %fusion.33 = (bf16[6,320,511]{2,1,0:T(8,128)(2,1)}, bf16[6,320,511]{2,1,0:T(8,128)(2,1)}) fusion(bf16[6,320,512]{2,1,0:T(8,128)(2,1)S(1)} %maximum_bitcast_fusion), kind=kLoop, calls=%fused_computation.77 | loop fusion | bytes 7848960 | tf_op jit(solution)/shard_map/slice | solution.py:62
  70.1 8.2 %all-to-all-start.4 = ((bf16[16,112,128]{2,1,0:T(8,128)(2,1)}), bf16[16,112,128]{2,1,0:T(8,128)(2,1)S(1)}, u32[]{:S(2)}, u32[]{:S(2)}) async-start(bf16[16,112,128]{2,1,0:T(8,128)(2,1)} %broadcast_in_dim.62), calls=%async_computation.4 | async-start | bytes 917504 | tf_op jit(solution)/shard_map/all_to_all | solution.py:26
  78.3 5.7 %fusion.5.x_ref = bf16[6,960,512]{2,1,0:T(8,128)(2,1)} fusion(bf16[6,320,511]{2,1,0:T(8,128)(2,1)} %get-tuple-element.10, bf16[6,320,511]{2,1,0:T(8,128)(2,1)} %get-tuple-element.9, bf16[6,320,512]{2,1,0:T(8,128)(2,1)S(1)} %maximum_bitcast_fusion), kind=kLoop, calls=%fused_computation.9 | loop fusion | flops 29491200 | bytes 11788800 | tf_op jit(solution)/shard_map/concatenate | solution.py:64
  84.0 4.9 %all-to-all-done.4 = bf16[16,112,128]{2,1,0:T(8,128)(2,1)S(1)} async-done(((bf16[16,112,128]{2,1,0:T(8,128)(2,1)}), bf16[16,112,128]{2,1,0:T(8,128)(2,1)S(1)}, u32[]{:S(2)}, u32[]{:S(2)}) %all-to-all-start.4) | async-done | bytes 458784 | tf_op jit(solution)/shard_map/all_to_all | solution.py:26
  91.2 11.2 %shard_map.91 = f32[4,320,512]{2,1,0:T(8,128)} custom-call(bf16[6,960,512]{2,1,0:T(8,128)(2,1)} %fusion.5.x_ref, bf16[3,448,960]{2,1,0:T(8,128)(2,1)} %constant_dynamic-update-slice_fusion.w_ref, bf16[320,64]{1,0:T(8,128)(2,1)} %bitcast.70, f32[320,1]{1,0:T(8,128)} %reshape.436.s_ref), custom_call_target="tpu_custom_call" | custom-call | flops 1845493760 | bytes 11100160 | tf_op jit(solution)/shard_map/pallas_call | solution.py:108
  102.5 2.1 %reduce_sum.127 = f32[320]{0:T(512)S(1)} reduce(f32[4,320,512]{2,1,0:T(8,128)} %shard_map.91, f32[]{:T(128)} %constant.70.clone.1), dimensions={0,2}, to_apply=%region_7.8 | reduce | flops 655040 | bytes 2622724 | tf_op jit(solution)/shard_map/reduce_sum | solution.py:34
  105.7 10.8 %all_to_all.37 = f32[16,2,1,32]{3,2,1,0:T(1,128)S(1)} all-to-all(f32[16,2,1,32]{3,2,1,0:T(1,128)S(1)} %broadcast_in_dim.64), channel_id=1, replica_groups=mesh['band'=16,'req'=16] {'band'}, dimensions={0} | all-to-all | bytes 8192 | tf_op jit(solution)/shard_map/all_to_all | solution.py:26
  118.0 2.3 %collective-permute-start.3 = (bf16[1,1,320,512]{3,2,1,0:T(8,128)(2,1)S(1)}, bf16[1,1,320,512]{3,2,1,0:T(8,128)(2,1)S(1)}, u32[]{:S(2)}, u32[]{:S(2)}) collective-permute-start(bf16[1,1,320,512]{3,2,1,0:T(8,128)(2,1)S(1)} %get-tuple-element.12), channel_id=1, source_target_pairs={{16,0},{32,16},{48,32},{64,48},{80,64},{96,80},{112,96},{128,112},... | collective-permute-start | bytes 983048 | tf_op jit(solution)/shard_map/ppermute | solution.py:18
  120.3 4.9 %collective-permute-start.2 = (bf16[1,1,320,512]{3,2,1,0:T(8,128)(2,1)S(1)}, bf16[1,1,320,512]{3,2,1,0:T(8,128)(2,1)S(1)}, u32[]{:S(2)}, u32[]{:S(2)}) collective-permute-start(bf16[1,1,320,512]{3,2,1,0:T(8,128)(2,1)S(1)} %get-tuple-element.11), channel_id=1, source_target_pairs={{0,16},{16,32},{32,48},{48,64},{64,80},{80,96},{96,112},{112,128},... | collective-permute-start | bytes 983048 | tf_op jit(solution)/shard_map/ppermute | solution.py:17
  125.2 2.6 %collective-permute-done.3 = bf16[1,1,320,512]{3,2,1,0:T(8,128)(2,1)S(1)} collective-permute-done((bf16[1,1,320,512]{3,2,1,0:T(8,128)(2,1)S(1)}, bf16[1,1,320,512]{3,2,1,0:T(8,128)(2,1)S(1)}, u32[]{:S(2)}, u32[]{:S(2)}) %collective-permute-start.3) | collective-permute-done | bytes 327712 | tf_op jit(solution)/shard_map/ppermute | solution.py:18
  130.5 3.5 %fusion.7.x_ref = bf16[6,960,512]{2,1,0:T(8,128)(2,1)} fusion(bf16[6,320,511]{2,1,0:T(8,128)(2,1)S(1)} %get-tuple-element.8, bf16[6,320,511]{2,1,0:T(8,128)(2,1)S(1)} %get-tuple-element.7, bf16[6,320,512]{2,1,0:T(8,128)(2,1)S(1)} %maximum_bitcast_fusion.1), kind=kLoop, calls=%fused_computation.11 | loop fusion | flops 29491200 | bytes 11788800 | tf_op jit(solution)/shard_map/concatenate | solution.py:64
  133.9 9.1 %shard_map.92 = bf16[4,320,512]{2,1,0:T(8,128)(2,1)} custom-call(bf16[6,960,512]{2,1,0:T(8,128)(2,1)} %fusion.7.x_ref, bf16[3,960,320]{2,1,0:T(8,128)(2,1)} %bitcast.67, bf16[4,320,512]{2,1,0:T(8,128)(2,1)} %bitcast.64), custom_call_target="tpu_custom_call" | custom-call | flops 1258291200 | bytes 10362880 | tf_op jit(solution)/shard_map/pallas_call | solution.py:129
  (93 shorter events, 21.3 us)
Async XLA Ops:
  0.0 59.0 %copy-start = (bf16[1280,320]{0,1:T(8,128)(2,1)S(1)}, bf16[1280,320]{0,1:T(8,128)(2,1)}, u32[]{:S(2)}) copy-start(bf16[1280,320]{0,1:T(8,128)(2,1)} %param.17) | copy-start | bytes 2457604
  0.0 15.5 %copy-start.6 = (bf16[1,64,320]{2,1,0:T(8,128)(2,1)S(1)}, bf16[1,64,320]{2,1,0:T(8,128)(2,1)}, u32[]{:S(2)}) copy-start(bf16[1,64,320]{2,1,0:T(8,128)(2,1)} %param.15) | copy-start | bytes 122884
  0.0 15.7 %copy-start.5 = (bf16[1,3,3,320,64]{3,4,2,1,0:T(8,128)(2,1)S(1)}, bf16[1,3,3,320,64]{3,4,2,1,0:T(8,128)(2,1)}, u32[]{:S(2)}) copy-start(bf16[1,3,3,320,64]{3,4,2,1,0:T(8,128)(2,1)} %param.14) | copy-start | bytes 1105924
  1.4 17.4 %all-to-all-start.1 = ((s32[16,1,1]{2,1,0:T(1,128)}), s32[16,1,1]{2,1,0:T(1,128)S(1)}, u32[]{:S(2)}, u32[]{:S(2)}) async-start(s32[16,1,1]{2,1,0:T(1,128)} %broadcast_in_dim.58), calls=%async_computation.1 | async-start | bytes 16384 | tf_op jit(solution)/shard_map/all_to_all | solution.py:26
  13.1 15.4 %copy-start.1 = (s32[256]{0:T(256)S(1)}, s32[256]{0:T(256)}, u32[]{:S(2)}) copy-start(s32[256]{0:T(256)} %param.12) | copy-start | bytes 3076
  15.3 24.3 %copy-start.3 = (bf16[1,4,512,320]{2,3,1,0:T(8,128)(2,1)S(1)}, bf16[1,4,512,320]{2,3,1,0:T(8,128)(2,1)}, u32[]{:S(2)}) copy-start(bf16[1,4,512,320]{2,3,1,0:T(8,128)(2,1)} %param.9) | copy-start | bytes 3932164
  19.4 16.1 %all-to-all-start = ((f32[16,2,1,32]{3,2,1,0:T(1,128)}), f32[16,2,1,32]{3,2,1,0:T(1,128)S(1)}, u32[]{:S(2)}, u32[]{:S(2)}) async-start(f32[16,2,1,32]{3,2,1,0:T(1,128)} %broadcast_in_dim.31), calls=%async_computation | async-start | bytes 32768 | tf_op jit(solution)/shard_map/all_to_all | solution.py:26
  35.4 14.6 %all-to-all-start.2 = ((bf16[16,112,128]{2,1,0:T(8,128)(2,1)}), bf16[16,112,128]{2,1,0:T(8,128)(2,1)S(1)}, u32[]{:S(2)}, u32[]{:S(2)}) async-start(bf16[16,112,128]{2,1,0:T(8,128)(2,1)} %bitcast.12), calls=%async_computation.2 | async-start | bytes 917504 | tf_op jit(solution)/shard_map/all_to_all | solution.py:153
  40.6 1.1 copy-start.4
  42.6 22.1 %collective-permute-start.1 = (bf16[1,1,320,512]{3,2,1,0:T(8,128)(2,1)}, bf16[1,1,320,512]{3,2,1,0:T(8,128)(2,1)}, u32[]{:S(2)}, u32[]{:S(2)}) collective-permute-start(bf16[1,1,320,512]{3,2,1,0:T(8,128)(2,1)} %get-tuple-element.14), channel_id=1, source_target_pairs={{16,0},{32,16},{48,32},{64,48},{80,64},{96,80},{112,96},{128,112},... | collective-permute-start | bytes 983048 | tf_op jit(solution)/shard_map/ppermute | solution.py:18
  44.7 19.9 %collective-permute-start = (bf16[1,1,320,512]{3,2,1,0:T(8,128)(2,1)}, bf16[1,1,320,512]{3,2,1,0:T(8,128)(2,1)}, u32[]{:S(2)}, u32[]{:S(2)}) collective-permute-start(bf16[1,1,320,512]{3,2,1,0:T(8,128)(2,1)} %get-tuple-element.13), channel_id=1, source_target_pairs={{0,16},{16,32},{32,48},{48,64},{64,80},{80,96},{96,112},{112,128},... | collective-permute-start | bytes 983048 | tf_op jit(solution)/shard_map/ppermute | solution.py:17
  51.5 7.5 %copy-start.7 = (bf16[1,1280]{1,0:T(2,128)(2,1)S(1)}, bf16[1,1280]{1,0:T(2,128)(2,1)}, u32[]{:S(2)}) copy-start(bf16[1,1280]{1,0:T(2,128)(2,1)} %param.10) | copy-start | bytes 7684
  51.5 17.8 %all-to-all-start.3 = ((bf16[16,112,128]{2,1,0:T(8,128)(2,1)}), bf16[16,112,128]{2,1,0:T(8,128)(2,1)S(1)}, u32[]{:S(2)}, u32[]{:S(2)}) async-start(bf16[16,112,128]{2,1,0:T(8,128)(2,1)} %broadcast_select_fusion), calls=%async_computation.3 | async-start | bytes 917504 | tf_op jit(solution)/shard_map/all_to_all | solution.py:155
  70.1 18.8 %all-to-all-start.4 = ((bf16[16,112,128]{2,1,0:T(8,128)(2,1)}), bf16[16,112,128]{2,1,0:T(8,128)(2,1)S(1)}, u32[]{:S(2)}, u32[]{:S(2)}) async-start(bf16[16,112,128]{2,1,0:T(8,128)(2,1)} %broadcast_in_dim.62), calls=%async_computation.4 | async-start | bytes 917504 | tf_op jit(solution)/shard_map/all_to_all | solution.py:26
  102.5 2.5 %copy-start.2 = (f32[4,320,512]{2,1,0:T(8,128)S(1)}, f32[4,320,512]{2,1,0:T(8,128)}, u32[]{:S(2)}) copy-start(f32[4,320,512]{2,1,0:T(8,128)} %shard_map.91) | copy-start | bytes 7864324
  118.0 9.9 %collective-permute-start.3 = (bf16[1,1,320,512]{3,2,1,0:T(8,128)(2,1)S(1)}, bf16[1,1,320,512]{3,2,1,0:T(8,128)(2,1)S(1)}, u32[]{:S(2)}, u32[]{:S(2)}) collective-permute-start(bf16[1,1,320,512]{3,2,1,0:T(8,128)(2,1)S(1)} %get-tuple-element.12), channel_id=1, source_target_pairs={{16,0},{32,16},{48,32},{64,48},{80,64},{96,80},{112,96},{128,112},... | collective-permute-start | bytes 983048 | tf_op jit(solution)/shard_map/ppermute | solution.py:18
  120.3 8.9 %collective-permute-start.2 = (bf16[1,1,320,512]{3,2,1,0:T(8,128)(2,1)S(1)}, bf16[1,1,320,512]{3,2,1,0:T(8,128)(2,1)S(1)}, u32[]{:S(2)}, u32[]{:S(2)}) collective-permute-start(bf16[1,1,320,512]{3,2,1,0:T(8,128)(2,1)S(1)} %get-tuple-element.11), channel_id=1, source_target_pairs={{0,16},{16,32},{32,48},{48,64},{64,80},{80,96},{96,112},{112,128},... | collective-permute-start | bytes 983048 | tf_op jit(solution)/shard_map/ppermute | solution.py:17

commit v8 on v7

--- a/solution.py
+++ b/solution.py
@@ -73,15 +73,17 @@
     return jnp.transpose(kernel, (0, 3, 1, 2)).reshape(taps, outer, cols * inner)
 
 
-def first_conv_kernel(x_ref, w_ref, u_ref, s_ref, o_ref):
+def first_conv_kernel(x_ref, w_ref, d_ref, u_ref, s_ref, o_ref):
     row = pl.program_id(0)
-    total = None
+    main = None
+    low = None
     for tap in range(3):
-        t = jnp.dot(w_ref[tap], x_ref[row + tap], preferred_element_type=jnp.float32)
-        total = t if total is None else total + t
-    rank = u_ref.shape[1]
-    low = total[:rank]
-    main = total[w_ref.shape[1] - o_ref.shape[1] :]
+        piece = x_ref[row + tap]
+        dims = (((0,), (0,)), ((), ()))
+        m = lax.dot_general(w_ref[tap], piece, dims, preferred_element_type=jnp.float32)
+        l = lax.dot_general(d_ref[tap], piece, dims, preferred_element_type=jnp.float32)
+        main = m if main is None else main + m
+        low = l if low is None else low + l
     lifted = jnp.dot(u_ref[...], low.astype(jnp.bfloat16), preferred_element_type=jnp.float32)
     o_ref[0] = main + lifted + s_ref[...]
 
@@ -99,18 +101,16 @@
 
 def first_conv(cols, weight, down, up_t, shift):
     rows, wide, width = cols.shape[0] - 2, cols.shape[1], cols.shape[2]
-    out = weight.shape[1]
-    rank = down.shape[1]
-    lead = -(-rank // 128) * 128
-    base = jnp.concatenate([jnp.zeros((3, lead, wide), weight.dtype), weight], axis=1)
-    weight = lax.dynamic_update_slice(base, down, (0, 0, 0))
-    flops = 2 * rows * width * wide * (out + lead) + 2 * rows * width * rank * out
+    out = weight.shape[2]
+    rank = down.shape[2]
+    flops = 2 * rows * width * wide * (out + rank) + 2 * rows * width * rank * out
     return pl.pallas_call(
         first_conv_kernel,
         grid=(rows,),
         in_specs=[
             pl.BlockSpec(cols.shape, lambda h: (0, 0, 0)),
             pl.BlockSpec(weight.shape, lambda h: (0, 0, 0)),
+            pl.BlockSpec(down.shape, lambda h: (0, 0, 0)),
             pl.BlockSpec(up_t.shape, lambda h: (0, 0)),
             pl.BlockSpec(shift.shape, lambda h: (0, 0)),
         ],
@@ -118,9 +118,9 @@
         out_shape=jax.ShapeDtypeStruct((rows, out, width), jnp.float32),
         cost_estimate=pl.CostEstimate(
             flops=flops, transcendentals=0,
-            bytes_accessed=cols.size * 2 + weight.size * 2 + rows * width * out * 4,
+            bytes_accessed=cols.size * 2 + weight.size * 2 + down.size * 2 + rows * width * out * 4,
         ),
-    )(cols, weight, up_t, shift)
+    )(cols, weight, down, up_t, shift)
 
 
 def second_conv(cols, weight, residual):
@@ -185,8 +185,8 @@
     field = jnp.swapaxes(latents, 2, 3)
     hidden = first_conv(
         taps_by_column(conv_input(field, G)[0]),
-        tap_weights(first_conv_weight),
-        tap_weights(chosen_down),
+        first_conv_weight.reshape(3, wide_of(first_conv_weight), channels),
+        chosen_down.reshape(3, wide_of(chosen_down), chosen_down.shape[-1]),
         chosen_up.T,
         shift.reshape(channels, 1),
     )[None]

time: 145 us -> 144 us (level)
  waiting for transfers between devices: 16.9 us -> 25.5 us
  local copies, waits for them, and re-layouts: 20.1 us -> 14.4 us
  starting transfers between devices: 49.8 us -> 46.2 us
    all_to_all x1, waiting for transfers between devices: 0.01 us -> 3.91 us  [fetch_adapter(): by_req = lax.all_to_all(wanted, 'req', 0, 0, tiled=True)]
    reshape x3 -> x0, local copies, waits for them, and re-layouts: 3.36 us -> none  [the longest x2 3.04 us: tap_weights(): jnp.transpose(kernel, (0, 3, 1, 2)).reshape(taps, outer, cols * inner)]
    ppermute x2, waiting for transfers between devices: 2.64 us -> 5.9 us  [with_halo(): after = lax.ppermute(initial, axis, down)]
    ppermute x2, starting transfers between devices: 9.88 us -> 7.53 us  [with_halo(): before = lax.ppermute(last, axis, up)]
    concatenate x1 -> x0, local copies, waits for them, and re-layouts: 1.94 us -> none  [first_conv(): jnp.concatenate([jnp.zeros((3, lead, wide), weight.dtype), weight], axis=1)]
  transfers between devices with their start and end apart: 9 -> 9, of which waited for: 6 -> 7; matrix products, arithmetic and copies ran while one was open for 19% -> 15% of each run, Pallas kernels for 0% -> 0%
where the time goes in v8:
time: 144 us; the launch traced here: 143 us
  starting transfers between devices  46.2 us (32%)
  waiting for transfers between devices  25.5 us (18%)
  other arithmetic  21.7 us (15%)
  Pallas kernels  21.3 us (15%)
  local copies, waits for them, and re-layouts  14.4 us (10%)
  blocking collectives  10.8 us (8%)
  between operations  2.83 us (2%)
    all_to_all x3, starting transfers between devices, exchange(): return lax.all_to_all(spread, axis, 0, 0, tiled=True)  26.3 us
    all_to_all x3, waiting for transfers between devices, exchange(): return lax.all_to_all(spread, axis, 0, 0, tiled=True)  12.6 us
    pallas_call x1, Pallas kernels, first_conv(): pl.pallas_call(first_conv_kernel, grid=(rows,), in_specs=[pl.BlockSpec(co...  12.2 us
    all_to_all x1, blocking collectives, exchange(): return lax.all_to_all(spread, axis, 0, 0, tiled=True)  10.8 us
    concatenate x2, other arithmetic, taps_by_column(): return jnp.concatenate([left, field, right], axis=1)  9.21 us
    pallas_call x1, Pallas kernels, second_conv(): pl.pallas_call(second_conv_kernel, grid=(rows,), in_specs=[pl.BlockSpec(c...  9.1 us
    ppermute x2, starting transfers between devices, with_halo(): before = lax.ppermute(last, axis, up)  7.53 us
    ppermute x2, waiting for transfers between devices, with_halo(): after = lax.ppermute(initial, axis, down)  5.9 us
  transfers between devices with their start and end apart: 9, of which 7 were waited for; matrix products, arithmetic and copies ran while one was open for 15% of the time, Pallas kernels for 0%

profile of v8, /device:TPU:1, one launch (start us, length us, event | category | flops | bytes accessed | tf_op | source)
XLA Modules:
  0.0 143.0 jit_solution(5825172053813640355)
XLA Ops:
  1.4 10.1 %all-to-all-start.1 = ((s32[16,1,1]{2,1,0:T(1,128)}), s32[16,1,1]{2,1,0:T(1,128)S(1)}, u32[]{:S(2)}, u32[]{:S(2)}) async-start(s32[16,1,1]{2,1,0:T(1,128)} %broadcast_in_dim.57), calls=%async_computation.1 | async-start | bytes 16384 | tf_op jit(solution)/shard_map/all_to_all | solution.py:26
  11.5 1.6 %convert_reduce_fusion = f32[320]{0:T(512)S(1)} fusion(bf16[1,4,512,320]{2,3,1,0:T(8,128)(2,1)} %param.9), kind=kLoop, calls=%fused_computation.14 | loop fusion | flops 1310400 | bytes 1312000 | tf_op jit(solution)/shard_map/reduce_sum | solution.py:34
  13.5 1.8 %fusion.9 = f32[320]{0:T(512)S(1)} fusion(bf16[1,4,512,320]{2,3,1,0:T(8,128)(2,1)} %param.9, f32[320]{0:T(512)S(1)} %sub.103), kind=kLoop, calls=%fused_computation.16 | loop fusion | flops 2621120 | bytes 1313280 | tf_op jit(solution)/shard_map/reduce_sum | solution.py:36
  19.4 8.8 %all-to-all-start = ((f32[16,2,1,32]{3,2,1,0:T(1,128)}), f32[16,2,1,32]{3,2,1,0:T(1,128)S(1)}, u32[]{:S(2)}, u32[]{:S(2)}) async-start(f32[16,2,1,32]{3,2,1,0:T(1,128)} %broadcast_in_dim.31), calls=%async_computation | async-start | bytes 32768 | tf_op jit(solution)/shard_map/all_to_all | solution.py:26
  29.2 6.2 %all-to-all-done = f32[16,2,1,32]{3,2,1,0:T(1,128)S(1)} async-done(((f32[16,2,1,32]{3,2,1,0:T(1,128)}), f32[16,2,1,32]{3,2,1,0:T(1,128)S(1)}, u32[]{:S(2)}, u32[]{:S(2)}) %all-to-all-start) | async-done | bytes 4128 | tf_op jit(solution)/shard_map/all_to_all | solution.py:26
  35.4 3.7 %all-to-all-start.2 = ((bf16[16,112,128]{2,1,0:T(8,128)(2,1)}), bf16[16,112,128]{2,1,0:T(8,128)(2,1)S(1)}, u32[]{:S(2)}, u32[]{:S(2)}) async-start(bf16[16,112,128]{2,1,0:T(8,128)(2,1)} %bitcast.11), calls=%async_computation.2 | async-start | bytes 917504 | tf_op jit(solution)/shard_map/all_to_all | solution.py:153
  41.7 5.1 %collective-permute-start = (bf16[1,1,320,512]{3,2,1,0:T(8,128)(2,1)S(1)}, bf16[1,1,320,512]{3,2,1,0:T(8,128)(2,1)}, u32[]{:S(2)}, u32[]{:S(2)}) collective-permute-start(bf16[1,1,320,512]{3,2,1,0:T(8,128)(2,1)S(1)} %get-tuple-element.13), channel_id=1, source_target_pairs={{0,16},{16,32},{32,48},{48,64},{64,80},{80,96},{96,112},{112,128},... | collective-permute-start | bytes 983048 | tf_op jit(solution)/shard_map/ppermute | solution.py:17
  46.8 1.9 %collective-permute-start.1 = (bf16[1,1,320,512]{3,2,1,0:T(8,128)(2,1)S(1)}, bf16[1,1,320,512]{3,2,1,0:T(8,128)(2,1)}, u32[]{:S(2)}, u32[]{:S(2)}) collective-permute-start(bf16[1,1,320,512]{3,2,1,0:T(8,128)(2,1)S(1)} %get-tuple-element.14), channel_id=1, source_target_pairs={{16,0},{32,16},{48,32},{64,48},{80,64},{96,80},{112,96},{128,112},... | collective-permute-start | bytes 983048 | tf_op jit(solution)/shard_map/ppermute | solution.py:18
  51.4 4.6 %all-to-all-start.3 = ((bf16[16,112,128]{2,1,0:T(8,128)(2,1)}), bf16[16,112,128]{2,1,0:T(8,128)(2,1)S(1)}, u32[]{:S(2)}, u32[]{:S(2)}) async-start(bf16[16,112,128]{2,1,0:T(8,128)(2,1)} %broadcast_select_fusion), calls=%async_computation.3 | async-start | bytes 917504 | tf_op jit(solution)/shard_map/all_to_all | solution.py:155
  59.5 1.7 %maximum_bitcast_fusion = bf16[6,320,512]{2,1,0:T(8,128)(2,1)S(1)} fusion(bf16[1,1,320,512]{3,2,1,0:T(8,128)(2,1)} %collective-permute-done.1, bf16[1,4,320,512]{3,2,1,0:T(8,128)(2,1)} %copy-done.4, bf16[1,1,320,512]{3,2,1,0:T(8,128)(2,1)} %collective-permute-done), kind=kLoop, calls=%fused_computation.26 | loop fusion | flops 1966080 | bytes 3932160 | tf_op jit(solution)/shard_map/squeeze | solution.py:187
  61.2 3.0 %fusion.33 = (bf16[6,320,511]{2,1,0:T(8,128)(2,1)}, bf16[6,320,511]{2,1,0:T(8,128)(2,1)}) fusion(bf16[6,320,512]{2,1,0:T(8,128)(2,1)S(1)} %maximum_bitcast_fusion), kind=kLoop, calls=%fused_computation.76 | loop fusion | bytes 7848960 | tf_op jit(solution)/shard_map/slice | solution.py:62
  64.2 3.9 %all-to-all-done.3 = bf16[16,112,128]{2,1,0:T(8,128)(2,1)S(1)} async-done(((bf16[16,112,128]{2,1,0:T(8,128)(2,1)}), bf16[16,112,128]{2,1,0:T(8,128)(2,1)S(1)}, u32[]{:S(2)}, u32[]{:S(2)}) %all-to-all-start.3) | async-done | bytes 458784 | tf_op jit(solution)/shard_map/all_to_all | solution.py:155
  68.9 7.4 %all-to-all-start.4 = ((bf16[16,112,128]{2,1,0:T(8,128)(2,1)}), bf16[16,112,128]{2,1,0:T(8,128)(2,1)S(1)}, u32[]{:S(2)}, u32[]{:S(2)}) async-start(bf16[16,112,128]{2,1,0:T(8,128)(2,1)} %broadcast_in_dim.61), calls=%async_computation.4 | async-start | bytes 917504 | tf_op jit(solution)/shard_map/all_to_all | solution.py:26
  76.3 5.7 %fusion.5.x_ref = bf16[6,960,512]{2,1,0:T(8,128)(2,1)} fusion(bf16[6,320,511]{2,1,0:T(8,128)(2,1)} %get-tuple-element.10, bf16[6,320,511]{2,1,0:T(8,128)(2,1)} %get-tuple-element.9, bf16[6,320,512]{2,1,0:T(8,128)(2,1)S(1)} %maximum_bitcast_fusion), kind=kLoop, calls=%fused_computation.9 | loop fusion | flops 29491200 | bytes 11788800 | tf_op jit(solution)/shard_map/concatenate | solution.py:64
  82.1 4.9 %all-to-all-done.4 = bf16[16,112,128]{2,1,0:T(8,128)(2,1)S(1)} async-done(((bf16[16,112,128]{2,1,0:T(8,128)(2,1)}), bf16[16,112,128]{2,1,0:T(8,128)(2,1)S(1)}, u32[]{:S(2)}, u32[]{:S(2)}) %all-to-all-start.4) | async-done | bytes 458784 | tf_op jit(solution)/shard_map/all_to_all | solution.py:26
  89.1 12.2 %shard_map.91 = f32[4,320,512]{2,1,0:T(8,128)} custom-call(bf16[6,960,512]{2,1,0:T(8,128)(2,1)} %fusion.5.x_ref, bf16[3,960,320]{2,1,0:T(8,128)(2,1)} %bitcast.60, bf16[3,960,64]{2,1,0:T(8,128)(2,1)} %reshape_reshape.3.d_ref, bf16[320,64]{1,0:T(8,128)(2,1)} %bitcast.64, f32[320,1]{1,0:T(8,128)} %reshape.428.s_ref), custom_call_target="tpu_custom_call" | custom-call | flops 1593835520 | bytes 10731520 | tf_op jit(solution)/shard_map/pallas_call | solution.py:107
  101.3 2.1 %reduce_sum.127 = f32[320]{0:T(512)S(1)} reduce(f32[4,320,512]{2,1,0:T(8,128)} %shard_map.91, f32[]{:T(128)} %constant.69.clone.1), dimensions={0,2}, to_apply=%region_7.8 | reduce | flops 655040 | bytes 2622724 | tf_op jit(solution)/shard_map/reduce_sum | solution.py:34
  104.5 10.8 %all_to_all.37 = f32[16,2,1,32]{3,2,1,0:T(1,128)S(1)} all-to-all(f32[16,2,1,32]{3,2,1,0:T(1,128)S(1)} %broadcast_in_dim.63), channel_id=1, replica_groups=mesh['band'=16,'req'=16] {'band'}, dimensions={0} | all-to-all | bytes 8192 | tf_op jit(solution)/shard_map/all_to_all | solution.py:26
  116.8 2.5 %collective-permute-start.2 = (bf16[1,1,320,512]{3,2,1,0:T(8,128)(2,1)S(1)}, bf16[1,1,320,512]{3,2,1,0:T(8,128)(2,1)S(1)}, u32[]{:S(2)}, u32[]{:S(2)}) collective-permute-start(bf16[1,1,320,512]{3,2,1,0:T(8,128)(2,1)S(1)} %get-tuple-element.11), channel_id=1, source_target_pairs={{0,16},{16,32},{32,48},{48,64},{64,80},{80,96},{96,112},{112,128},... | collective-permute-start | bytes 983048 | tf_op jit(solution)/shard_map/ppermute | solution.py:17
  119.3 2.1 %collective-permute-start.3 = (bf16[1,1,320,512]{3,2,1,0:T(8,128)(2,1)S(1)}, bf16[1,1,320,512]{3,2,1,0:T(8,128)(2,1)S(1)}, u32[]{:S(2)}, u32[]{:S(2)}) collective-permute-start(bf16[1,1,320,512]{3,2,1,0:T(8,128)(2,1)S(1)} %get-tuple-element.12), channel_id=1, source_target_pairs={{16,0},{32,16},{48,32},{64,48},{80,64},{96,80},{112,96},{128,112},... | collective-permute-start | bytes 983048 | tf_op jit(solution)/shard_map/ppermute | solution.py:18
  121.4 1.9 %collective-permute-done.2 = bf16[1,1,320,512]{3,2,1,0:T(8,128)(2,1)S(1)} collective-permute-done((bf16[1,1,320,512]{3,2,1,0:T(8,128)(2,1)S(1)}, bf16[1,1,320,512]{3,2,1,0:T(8,128)(2,1)S(1)}, u32[]{:S(2)}, u32[]{:S(2)}) %collective-permute-start.2) | collective-permute-done | bytes 327712 | tf_op jit(solution)/shard_map/ppermute | solution.py:17
  123.2 5.9 %collective-permute-done.3 = bf16[1,1,320,512]{3,2,1,0:T(8,128)(2,1)S(1)} collective-permute-done((bf16[1,1,320,512]{3,2,1,0:T(8,128)(2,1)S(1)}, bf16[1,1,320,512]{3,2,1,0:T(8,128)(2,1)S(1)}, u32[]{:S(2)}, u32[]{:S(2)}) %collective-permute-start.3) | collective-permute-done | bytes 327712 | tf_op jit(solution)/shard_map/ppermute | solution.py:18
  130.5 3.5 %fusion.7.x_ref = bf16[6,960,512]{2,1,0:T(8,128)(2,1)} fusion(bf16[6,320,511]{2,1,0:T(8,128)(2,1)S(1)} %get-tuple-element.8, bf16[6,320,511]{2,1,0:T(8,128)(2,1)S(1)} %get-tuple-element.7, bf16[6,320,512]{2,1,0:T(8,128)(2,1)S(1)} %maximum_bitcast_fusion.1), kind=kLoop, calls=%fused_computation.11 | loop fusion | flops 29491200 | bytes 11788800 | tf_op jit(solution)/shard_map/concatenate | solution.py:64
  133.9 9.1 %shard_map.92 = bf16[4,320,512]{2,1,0:T(8,128)(2,1)} custom-call(bf16[6,960,512]{2,1,0:T(8,128)(2,1)} %fusion.7.x_ref, bf16[3,960,320]{2,1,0:T(8,128)(2,1)} %bitcast.61, bf16[4,320,512]{2,1,0:T(8,128)(2,1)} %bitcast.59), custom_call_target="tpu_custom_call" | custom-call | flops 1258291200 | bytes 10362880 | tf_op jit(solution)/shard_map/pallas_call | solution.py:129
  (89 shorter events, 19.7 us)
Async XLA Ops:
  0.0 56.0 %copy-start = (bf16[1280,320]{0,1:T(8,128)(2,1)S(1)}, bf16[1280,320]{0,1:T(8,128)(2,1)}, u32[]{:S(2)}) copy-start(bf16[1280,320]{0,1:T(8,128)(2,1)} %param.17) | copy-start | bytes 2457604
  0.0 15.5 %copy-start.5 = (bf16[1,3,3,320,64]{3,4,2,1,0:T(8,128)(2,1)S(1)}, bf16[1,3,3,320,64]{3,4,2,1,0:T(8,128)(2,1)}, u32[]{:S(2)}) copy-start(bf16[1,3,3,320,64]{3,4,2,1,0:T(8,128)(2,1)} %param.14) | copy-start | bytes 1105924
  0.0 16.3 %copy-start.6 = (bf16[1,64,320]{2,1,0:T(8,128)(2,1)S(1)}, bf16[1,64,320]{2,1,0:T(8,128)(2,1)}, u32[]{:S(2)}) copy-start(bf16[1,64,320]{2,1,0:T(8,128)(2,1)} %param.15) | copy-start | bytes 122884
  1.4 17.4 %all-to-all-start.1 = ((s32[16,1,1]{2,1,0:T(1,128)}), s32[16,1,1]{2,1,0:T(1,128)S(1)}, u32[]{:S(2)}, u32[]{:S(2)}) async-start(s32[16,1,1]{2,1,0:T(1,128)} %broadcast_in_dim.57), calls=%async_computation.1 | async-start | bytes 16384 | tf_op jit(solution)/shard_map/all_to_all | solution.py:26
  13.1 15.4 %copy-start.1 = (s32[256]{0:T(256)S(1)}, s32[256]{0:T(256)}, u32[]{:S(2)}) copy-start(s32[256]{0:T(256)} %param.12) | copy-start | bytes 3076
  15.3 24.3 %copy-start.3 = (bf16[1,4,512,320]{2,3,1,0:T(8,128)(2,1)S(1)}, bf16[1,4,512,320]{2,3,1,0:T(8,128)(2,1)}, u32[]{:S(2)}) copy-start(bf16[1,4,512,320]{2,3,1,0:T(8,128)(2,1)} %param.9) | copy-start | bytes 3932164
  19.4 16.1 %all-to-all-start = ((f32[16,2,1,32]{3,2,1,0:T(1,128)}), f32[16,2,1,32]{3,2,1,0:T(1,128)S(1)}, u32[]{:S(2)}, u32[]{:S(2)}) async-start(f32[16,2,1,32]{3,2,1,0:T(1,128)} %broadcast_in_dim.31), calls=%async_computation | async-start | bytes 32768 | tf_op jit(solution)/shard_map/all_to_all | solution.py:26
  35.4 14.5 %all-to-all-start.2 = ((bf16[16,112,128]{2,1,0:T(8,128)(2,1)}), bf16[16,112,128]{2,1,0:T(8,128)(2,1)S(1)}, u32[]{:S(2)}, u32[]{:S(2)}) async-start(bf16[16,112,128]{2,1,0:T(8,128)(2,1)} %bitcast.11), calls=%async_computation.2 | async-start | bytes 917504 | tf_op jit(solution)/shard_map/all_to_all | solution.py:153
  40.6 1.1 copy-start.4
  41.7 14.4 %copy-start.7 = (bf16[1,1280]{1,0:T(2,128)(2,1)S(1)}, bf16[1,1280]{1,0:T(2,128)(2,1)}, u32[]{:S(2)}) copy-start(bf16[1,1280]{1,0:T(2,128)(2,1)} %param.10) | copy-start | bytes 7684
  41.7 17.8 %collective-permute-start = (bf16[1,1,320,512]{3,2,1,0:T(8,128)(2,1)S(1)}, bf16[1,1,320,512]{3,2,1,0:T(8,128)(2,1)}, u32[]{:S(2)}, u32[]{:S(2)}) collective-permute-start(bf16[1,1,320,512]{3,2,1,0:T(8,128)(2,1)S(1)} %get-tuple-element.13), channel_id=1, source_target_pairs={{0,16},{16,32},{32,48},{48,64},{64,80},{80,96},{96,112},{112,128},... | collective-permute-start | bytes 983048 | tf_op jit(solution)/shard_map/ppermute | solution.py:17
  46.8 12.7 %collective-permute-start.1 = (bf16[1,1,320,512]{3,2,1,0:T(8,128)(2,1)S(1)}, bf16[1,1,320,512]{3,2,1,0:T(8,128)(2,1)}, u32[]{:S(2)}, u32[]{:S(2)}) collective-permute-start(bf16[1,1,320,512]{3,2,1,0:T(8,128)(2,1)S(1)} %get-tuple-element.14), channel_id=1, source_target_pairs={{16,0},{32,16},{48,32},{64,48},{80,64},{96,80},{112,96},{128,112},... | collective-permute-start | bytes 983048 | tf_op jit(solution)/shard_map/ppermute | solution.py:18
  51.4 16.6 %all-to-all-start.3 = ((bf16[16,112,128]{2,1,0:T(8,128)(2,1)}), bf16[16,112,128]{2,1,0:T(8,128)(2,1)S(1)}, u32[]{:S(2)}, u32[]{:S(2)}) async-start(bf16[16,112,128]{2,1,0:T(8,128)(2,1)} %broadcast_select_fusion), calls=%async_computation.3 | async-start | bytes 917504 | tf_op jit(solution)/shard_map/all_to_all | solution.py:155
  68.9 18.1 %all-to-all-start.4 = ((bf16[16,112,128]{2,1,0:T(8,128)(2,1)}), bf16[16,112,128]{2,1,0:T(8,128)(2,1)S(1)}, u32[]{:S(2)}, u32[]{:S(2)}) async-start(bf16[16,112,128]{2,1,0:T(8,128)(2,1)} %broadcast_in_dim.61), calls=%async_computation.4 | async-start | bytes 917504 | tf_op jit(solution)/shard_map/all_to_all | solution.py:26
  101.3 2.5 %copy-start.2 = (f32[4,320,512]{2,1,0:T(8,128)S(1)}, f32[4,320,512]{2,1,0:T(8,128)}, u32[]{:S(2)}) copy-start(f32[4,320,512]{2,1,0:T(8,128)} %shard_map.91) | copy-start | bytes 7864324
  116.8 6.5 %collective-permute-start.2 = (bf16[1,1,320,512]{3,2,1,0:T(8,128)(2,1)S(1)}, bf16[1,1,320,512]{3,2,1,0:T(8,128)(2,1)S(1)}, u32[]{:S(2)}, u32[]{:S(2)}) collective-permute-start(bf16[1,1,320,512]{3,2,1,0:T(8,128)(2,1)S(1)} %get-tuple-element.11), channel_id=1, source_target_pairs={{0,16},{16,32},{32,48},{48,64},{64,80},{80,96},{96,112},{112,128},... | collective-permute-start | bytes 983048 | tf_op jit(solution)/shard_map/ppermute | solution.py:17
  119.3 9.9 %collective-permute-start.3 = (bf16[1,1,320,512]{3,2,1,0:T(8,128)(2,1)S(1)}, bf16[1,1,320,512]{3,2,1,0:T(8,128)(2,1)S(1)}, u32[]{:S(2)}, u32[]{:S(2)}) collective-permute-start(bf16[1,1,320,512]{3,2,1,0:T(8,128)(2,1)S(1)} %get-tuple-element.12), channel_id=1, source_target_pairs={{16,0},{32,16},{48,32},{64,48},{80,64},{96,80},{112,96},{128,112},... | collective-permute-start | bytes 983048 | tf_op jit(solution)/shard_map/ppermute | solution.py:18

commit v9 on v8

--- a/solution.py
+++ b/solution.py
@@ -26,7 +26,7 @@
     return lax.all_to_all(spread, axis, 0, 0, tiled=True)
 
 
-def norm_stats(field, groups):
+def local_stats(field, groups):
     field = field.astype(jnp.float32)
     requests, rows, channels, width = field.shape
     grouped = field.reshape(requests, rows, groups, channels // groups, width)
@@ -34,7 +34,10 @@
     local_mean = jnp.sum(grouped, axis=(1, 3, 4)) / count
     deviation = grouped - local_mean[:, None, :, None, None]
     local_m2 = jnp.sum(deviation * deviation, axis=(1, 3, 4))
-    stats = exchange(jnp.stack([local_mean, local_m2]), "band")
+    return jnp.stack([local_mean, local_m2]), count
+
+
+def combine_stats(stats, count):
     means, m2s = stats[:, 0], stats[:, 1]
     bands = means.shape[0]
     mean = jnp.sum(means, axis=0) / bands
@@ -44,6 +47,11 @@
     return mean, lax.rsqrt(spread + 1e-05)
 
 
+def norm_stats(field, groups):
+    stats, count = local_stats(field, groups)
+    return combine_stats(exchange(stats, "band"), count)
+
+
 def norm_silu(field, mean, scale, groups):
     field = field.astype(jnp.float32)
     requests, rows, channels, width = field.shape
@@ -52,8 +60,8 @@
     return jax.nn.silu(normed.reshape(field.shape)).astype(jnp.bfloat16)
 
 
-def conv_input(field, groups):
-    mean, scale = norm_stats(field, groups)
+def conv_input(field, groups, norm=None):
+    mean, scale = norm_stats(field, groups) if norm is None else norm
     return with_halo(norm_silu(field, mean, scale, groups), (("band", 1),), 1)
 
 
@@ -143,14 +151,20 @@
     )(cols, weight, residual)
 
 
-def fetch_adapter(slots, down, up):
+def fetch_adapter(slots, down, up, extra):
     bands, reqs = lax.axis_size("band"), lax.axis_size("req")
     flat = jnp.concatenate([down.reshape(-1), up.reshape(-1)])
     lanes, sublanes = 128, 16
     piece_rows = -(-flat.size // (bands * lanes * sublanes)) * sublanes
     flat = jnp.pad(flat, (0, bands * piece_rows * lanes - flat.size))
-    pieces = flat.reshape(bands, piece_rows, lanes)
-    by_band = lax.all_to_all(pieces, "band", 0, 0, tiled=True)
+    pieces = flat.reshape(bands, piece_rows, lanes).astype(jnp.float32)
+    extra_flat = extra.reshape(-1)
+    extra_rows = -(-extra_flat.size // (lanes * 8)) * 8
+    extra_block = jnp.pad(extra_flat, (0, extra_rows * lanes - extra_flat.size)).reshape(extra_rows, lanes)
+    sent = jnp.concatenate([pieces, jnp.broadcast_to(extra_block[None], (bands, extra_rows, lanes))], axis=1)
+    received = lax.all_to_all(sent, "band", 0, 0, tiled=True)
+    by_band = received[:, :piece_rows].astype(jnp.bfloat16)
+    extras = received[:, piece_rows:].reshape(bands, -1)[:, : extra_flat.size].reshape((bands,) + extra.shape)
     wanted = jnp.take(by_band, slots // reqs, axis=0)
     by_req = lax.all_to_all(wanted, "req", 0, 0, tiled=True)
     own = lax.axis_index("req")
@@ -159,7 +173,7 @@
     down_size = down.size
     chosen_down = whole[:down_size].reshape(down.shape[1:])
     chosen_up = whole[down_size : down_size + up.size].reshape(up.shape[1:])
-    return chosen_down, chosen_up
+    return chosen_down, chosen_up, extras
 
 
 def shards(
@@ -176,15 +190,18 @@
     requests, rows, width, channels = latents.shape
     every_adapter = exchange(request_adapter[0, 0], "req")
     slots = jnp.take(adapter_stored_row, every_adapter, axis=0)
-    chosen_down, chosen_up = fetch_adapter(slots, stored_down_weight, stored_up_weight)
+    field = jnp.swapaxes(latents, 2, 3)
+    first_stats, first_count = local_stats(field, G)
+    chosen_down, chosen_up, every_stats = fetch_adapter(
+        slots, stored_down_weight, stored_up_weight, first_stats
+    )
     shift = jnp.dot(
         jax.nn.silu(request_time_embedding.astype(jnp.float32)).astype(jnp.bfloat16),
         time_projection_weight,
         preferred_element_type=jnp.float32,
     )
-    field = jnp.swapaxes(latents, 2, 3)
     hidden = first_conv(
-        taps_by_column(conv_input(field, G)[0]),
+        taps_by_column(conv_input(field, G, combine_stats(every_stats, first_count))[0]),
         first_conv_weight.reshape(3, wide_of(first_conv_weight), channels),
         chosen_down.reshape(3, wide_of(chosen_down), chosen_down.shape[-1]),
         chosen_up.T,

time: 144 us -> 148 us (1.028)
  waiting for transfers between devices: 25.5 us -> 35.3 us
  starting transfers between devices: 46.2 us -> 40.1 us
    all_to_all x1, waiting for transfers between devices: 1.2 us -> 15 us  [fetch_adapter(): received = lax.all_to_all(sent, 'band', 0, 0, tiled=True)]
    all_to_all x3 -> x2, starting transfers between devices: 26.3 us -> 16.8 us  [exchange(): return lax.all_to_all(spread, axis, 0, 0, tiled=True)]
    all_to_all x3 -> x2, waiting for transfers between devices: 12.6 us -> 6.12 us  [exchange(): return lax.all_to_all(spread, axis, 0, 0, tiled=True)]
    all_to_all x1, starting transfers between devices: 3.75 us -> 8.6 us  [fetch_adapter(): received = lax.all_to_all(sent, 'band', 0, 0, tiled=True)]
    all_to_all x1, waiting for transfers between devices: 3.91 us -> 6.32 us  [fetch_adapter(): by_req = lax.all_to_all(wanted, 'req', 0, 0, tiled=True)]
    ppermute x2, starting transfers between devices: 7.53 us -> 5.5 us  [with_halo(): before = lax.ppermute(last, axis, up)]
  transfers between devices with their start and end apart: 9 -> 8, of which waited for: 7 -> 6; matrix products, arithmetic and copies ran while one was open for 15% -> 14% of each run, Pallas kernels for 0% -> 0%
where the time goes in v9:
time: 148 us
  starting transfers between devices  40.1 us (27%)
  waiting for transfers between devices  35.3 us (24%)
  other arithmetic  22 us (15%)
  Pallas kernels  21.2 us (14%)
  local copies, waits for them, and re-layouts  14.7 us (10%)
  blocking collectives  10.8 us (7%)
  between operations  3.06 us (2%)
    all_to_all x2, starting transfers between devices, exchange(): return lax.all_to_all(spread, axis, 0, 0, tiled=True)  16.8 us
    all_to_all x1, waiting for transfers between devices, fetch_adapter(): received = lax.all_to_all(sent, 'band', 0, 0, tiled=True)  15 us
    pallas_call x1, Pallas kernels, first_conv(): pl.pallas_call(first_conv_kernel, grid=(rows,), in_specs=[pl.BlockSpec(co...  12.2 us
    all_to_all x1, blocking collectives, exchange(): return lax.all_to_all(spread, axis, 0, 0, tiled=True)  10.8 us
    concatenate x2, other arithmetic, taps_by_column(): return jnp.concatenate([left, field, right], axis=1)  9.21 us
    pallas_call x1, Pallas kernels, second_conv(): pl.pallas_call(second_conv_kernel, grid=(rows,), in_specs=[pl.BlockSpec(c...  9.1 us
    all_to_all x1, starting transfers between devices, fetch_adapter(): received = lax.all_to_all(sent, 'band', 0, 0, tiled=True)  8.6 us
    all_to_all x1, waiting for transfers between devices, fetch_adapter(): by_req = lax.all_to_all(wanted, 'req', 0, 0, tiled=True)  6.32 us
  transfers between devices with their start and end apart: 8, of which 6 were waited for; matrix products, arithmetic and copies ran while one was open for 14% of the time, Pallas kernels for 0%

profile of v9, /device:TPU:1, one launch (start us, length us, event | category | flops | bytes accessed | tf_op | source)
XLA Modules:
  0.0 147.6 jit_solution(11000466229430489076)
XLA Ops:
  1.4 10.1 %all-to-all-start.1 = ((s32[16,1,1]{2,1,0:T(1,128)}), s32[16,1,1]{2,1,0:T(1,128)S(1)}, u32[]{:S(2)}, u32[]{:S(2)}) async-start(s32[16,1,1]{2,1,0:T(1,128)} %broadcast_in_dim.56), calls=%async_computation.1 | async-start | bytes 16384 | tf_op jit(solution)/shard_map/all_to_all | solution.py:26
  11.5 1.6 %convert_reduce_fusion = f32[320]{0:T(512)S(1)} fusion(bf16[1,4,512,320]{2,3,1,0:T(8,128)(2,1)} %param.9), kind=kLoop, calls=%fused_computation.14 | loop fusion | flops 1310400 | bytes 1312000 | tf_op jit(solution)/shard_map/reduce_sum | solution.py:34
  13.5 1.8 %fusion.9 = f32[320]{0:T(512)S(1)} fusion(bf16[1,4,512,320]{2,3,1,0:T(8,128)(2,1)} %param.9, f32[320]{0:T(512)S(1)} %sub.103), kind=kLoop, calls=%fused_computation.16 | loop fusion | flops 2621120 | bytes 1313280 | tf_op jit(solution)/shard_map/reduce_sum | solution.py:36
  18.8 8.6 %all-to-all-start = ((f32[16,120,128]{2,1,0:T(8,128)}), f32[16,120,128]{2,1,0:T(8,128)S(1)}, u32[]{:S(2)}, u32[]{:S(2)}) async-start(f32[16,120,128]{2,1,0:T(8,128)} %pad_maximum_fusion), calls=%async_computation | async-start | bytes 1966080 | tf_op jit(solution)/shard_map/all_to_all | solution.py:165
  28.6 15.0 %all-to-all-done = f32[16,120,128]{2,1,0:T(8,128)S(1)} async-done(((f32[16,120,128]{2,1,0:T(8,128)}), f32[16,120,128]{2,1,0:T(8,128)S(1)}, u32[]{:S(2)}, u32[]{:S(2)}) %all-to-all-start) | async-done | bytes 983072 | tf_op jit(solution)/shard_map/all_to_all | solution.py:165
  47.0 3.0 %collective-permute-start = (bf16[1,1,320,512]{3,2,1,0:T(8,128)(2,1)}, bf16[1,1,320,512]{3,2,1,0:T(8,128)(2,1)}, u32[]{:S(2)}, u32[]{:S(2)}) collective-permute-start(bf16[1,1,320,512]{3,2,1,0:T(8,128)(2,1)} %get-tuple-element.13), channel_id=1, source_target_pairs={{0,16},{16,32},{32,48},{48,64},{64,80},{80,96},{96,112},{112,128},... | collective-permute-start | bytes 983048 | tf_op jit(solution)/shard_map/ppermute | solution.py:17
  50.0 2.1 %collective-permute-start.1 = (bf16[1,1,320,512]{3,2,1,0:T(8,128)(2,1)S(1)}, bf16[1,1,320,512]{3,2,1,0:T(8,128)(2,1)}, u32[]{:S(2)}, u32[]{:S(2)}) collective-permute-start(bf16[1,1,320,512]{3,2,1,0:T(8,128)(2,1)S(1)} %get-tuple-element.14), channel_id=1, source_target_pairs={{16,0},{32,16},{48,32},{64,48},{80,64},{96,80},{112,96},{128,112},... | collective-permute-start | bytes 983048 | tf_op jit(solution)/shard_map/ppermute | solution.py:18
  53.7 5.1 %all-to-all-start.2 = ((bf16[16,112,128]{2,1,0:T(8,128)(2,1)}), bf16[16,112,128]{2,1,0:T(8,128)(2,1)S(1)}, u32[]{:S(2)}, u32[]{:S(2)}) async-start(bf16[16,112,128]{2,1,0:T(8,128)(2,1)} %broadcast_select_fusion), calls=%async_computation.2 | async-start | bytes 917504 | tf_op jit(solution)/shard_map/all_to_all | solution.py:169
  62.4 1.7 %maximum_bitcast_fusion = bf16[6,320,512]{2,1,0:T(8,128)(2,1)S(1)} fusion(bf16[1,1,320,512]{3,2,1,0:T(8,128)(2,1)} %collective-permute-done.1, bf16[1,4,320,512]{3,2,1,0:T(8,128)(2,1)} %copy-done.4, bf16[1,1,320,512]{3,2,1,0:T(8,128)(2,1)} %collective-permute-done), kind=kLoop, calls=%fused_computation.26 | loop fusion | flops 1966080 | bytes 3932160 | tf_op jit(solution)/shard_map/squeeze | solution.py:204
  64.1 3.0 %fusion.33 = (bf16[6,320,511]{2,1,0:T(8,128)(2,1)}, bf16[6,320,511]{2,1,0:T(8,128)(2,1)}) fusion(bf16[6,320,512]{2,1,0:T(8,128)(2,1)S(1)} %maximum_bitcast_fusion), kind=kLoop, calls=%fused_computation.80 | loop fusion | bytes 7848960 | tf_op jit(solution)/shard_map/slice | solution.py:70
  67.1 6.3 %all-to-all-done.2 = bf16[16,112,128]{2,1,0:T(8,128)(2,1)S(1)} async-done(((bf16[16,112,128]{2,1,0:T(8,128)(2,1)}), bf16[16,112,128]{2,1,0:T(8,128)(2,1)S(1)}, u32[]{:S(2)}, u32[]{:S(2)}) %all-to-all-start.2) | async-done | bytes 458784 | tf_op jit(solution)/shard_map/all_to_all | solution.py:169
  74.2 6.7 %all-to-all-start.3 = ((bf16[16,112,128]{2,1,0:T(8,128)(2,1)}), bf16[16,112,128]{2,1,0:T(8,128)(2,1)S(1)}, u32[]{:S(2)}, u32[]{:S(2)}) async-start(bf16[16,112,128]{2,1,0:T(8,128)(2,1)} %broadcast_in_dim.60), calls=%async_computation.3 | async-start | bytes 917504 | tf_op jit(solution)/shard_map/all_to_all | solution.py:26
  80.9 5.7 %fusion.5.x_ref = bf16[6,960,512]{2,1,0:T(8,128)(2,1)} fusion(bf16[6,320,511]{2,1,0:T(8,128)(2,1)} %get-tuple-element.10, bf16[6,320,511]{2,1,0:T(8,128)(2,1)} %get-tuple-element.9, bf16[6,320,512]{2,1,0:T(8,128)(2,1)S(1)} %maximum_bitcast_fusion), kind=kLoop, calls=%fused_computation.9 | loop fusion | flops 29491200 | bytes 11788800 | tf_op jit(solution)/shard_map/concatenate | solution.py:72
  86.7 4.9 %all-to-all-done.3 = bf16[16,112,128]{2,1,0:T(8,128)(2,1)S(1)} async-done(((bf16[16,112,128]{2,1,0:T(8,128)(2,1)}), bf16[16,112,128]{2,1,0:T(8,128)(2,1)S(1)}, u32[]{:S(2)}, u32[]{:S(2)}) %all-to-all-start.3) | async-done | bytes 458784 | tf_op jit(solution)/shard_map/all_to_all | solution.py:26
  92.5 1.2 reshape_reshape.3.d_ref
  93.7 12.2 %shard_map.91 = f32[4,320,512]{2,1,0:T(8,128)} custom-call(bf16[6,960,512]{2,1,0:T(8,128)(2,1)} %fusion.5.x_ref, bf16[3,960,320]{2,1,0:T(8,128)(2,1)} %bitcast.66, bf16[3,960,64]{2,1,0:T(8,128)(2,1)} %reshape_reshape.3.d_ref, bf16[320,64]{1,0:T(8,128)(2,1)} %bitcast.71, f32[320,1]{1,0:T(8,128)} %reshape.438.s_ref), custom_call_target="tpu_custom_call" | custom-call | flops 1593835520 | bytes 10731520 | tf_op jit(solution)/shard_map/pallas_call | solution.py:115
  105.8 2.1 %reduce_sum.127 = f32[320]{0:T(512)S(1)} reduce(f32[4,320,512]{2,1,0:T(8,128)} %shard_map.91, f32[]{:T(128)} %constant.71.clone.1), dimensions={0,2}, to_apply=%region_7.8 | reduce | flops 655040 | bytes 2622724 | tf_op jit(solution)/shard_map/reduce_sum | solution.py:34
  109.1 10.8 %all_to_all.32 = f32[16,2,1,32]{3,2,1,0:T(1,128)S(1)} all-to-all(f32[16,2,1,32]{3,2,1,0:T(1,128)S(1)} %broadcast_in_dim.62), channel_id=1, replica_groups=mesh['band'=16,'req'=16] {'band'}, dimensions={0} | all-to-all | bytes 8192 | tf_op jit(solution)/shard_map/all_to_all | solution.py:26
  121.4 2.5 %collective-permute-start.2 = (bf16[1,1,320,512]{3,2,1,0:T(8,128)(2,1)S(1)}, bf16[1,1,320,512]{3,2,1,0:T(8,128)(2,1)S(1)}, u32[]{:S(2)}, u32[]{:S(2)}) collective-permute-start(bf16[1,1,320,512]{3,2,1,0:T(8,128)(2,1)S(1)} %get-tuple-element.11), channel_id=1, source_target_pairs={{0,16},{16,32},{32,48},{48,64},{64,80},{80,96},{96,112},{112,128},... | collective-permute-start | bytes 983048 | tf_op jit(solution)/shard_map/ppermute | solution.py:17
  123.8 2.1 %collective-permute-start.3 = (bf16[1,1,320,512]{3,2,1,0:T(8,128)(2,1)S(1)}, bf16[1,1,320,512]{3,2,1,0:T(8,128)(2,1)S(1)}, u32[]{:S(2)}, u32[]{:S(2)}) collective-permute-start(bf16[1,1,320,512]{3,2,1,0:T(8,128)(2,1)S(1)} %get-tuple-element.12), channel_id=1, source_target_pairs={{16,0},{32,16},{48,32},{64,48},{80,64},{96,80},{112,96},{128,112},... | collective-permute-start | bytes 983048 | tf_op jit(solution)/shard_map/ppermute | solution.py:18
  126.0 1.9 %collective-permute-done.2 = bf16[1,1,320,512]{3,2,1,0:T(8,128)(2,1)S(1)} collective-permute-done((bf16[1,1,320,512]{3,2,1,0:T(8,128)(2,1)S(1)}, bf16[1,1,320,512]{3,2,1,0:T(8,128)(2,1)S(1)}, u32[]{:S(2)}, u32[]{:S(2)}) %collective-permute-start.2) | collective-permute-done | bytes 327712 | tf_op jit(solution)/shard_map/ppermute | solution.py:17
  127.8 5.9 %collective-permute-done.3 = bf16[1,1,320,512]{3,2,1,0:T(8,128)(2,1)S(1)} collective-permute-done((bf16[1,1,320,512]{3,2,1,0:T(8,128)(2,1)S(1)}, bf16[1,1,320,512]{3,2,1,0:T(8,128)(2,1)S(1)}, u32[]{:S(2)}, u32[]{:S(2)}) %collective-permute-start.3) | collective-permute-done | bytes 327712 | tf_op jit(solution)/shard_map/ppermute | solution.py:18
  135.1 3.5 %fusion.7.x_ref = bf16[6,960,512]{2,1,0:T(8,128)(2,1)} fusion(bf16[6,320,511]{2,1,0:T(8,128)(2,1)S(1)} %get-tuple-element.8, bf16[6,320,511]{2,1,0:T(8,128)(2,1)S(1)} %get-tuple-element.7, bf16[6,320,512]{2,1,0:T(8,128)(2,1)S(1)} %maximum_bitcast_fusion.1), kind=kLoop, calls=%fused_computation.11 | loop fusion | flops 29491200 | bytes 11788800 | tf_op jit(solution)/shard_map/concatenate | solution.py:72
  138.5 9.1 %shard_map.92 = bf16[4,320,512]{2,1,0:T(8,128)(2,1)} custom-call(bf16[6,960,512]{2,1,0:T(8,128)(2,1)} %fusion.7.x_ref, bf16[3,960,320]{2,1,0:T(8,128)(2,1)} %bitcast.67, bf16[4,320,512]{2,1,0:T(8,128)(2,1)} %bitcast.65), custom_call_target="tpu_custom_call" | custom-call | flops 1258291200 | bytes 10362880 | tf_op jit(solution)/shard_map/pallas_call | solution.py:137
  (96 shorter events, 17.7 us)
Async XLA Ops:
  0.0 58.7 %copy-start = (bf16[1280,320]{0,1:T(8,128)(2,1)S(1)}, bf16[1280,320]{0,1:T(8,128)(2,1)}, u32[]{:S(2)}) copy-start(bf16[1280,320]{0,1:T(8,128)(2,1)} %param.17) | copy-start | bytes 2457604
  0.0 15.7 %copy-start.6 = (bf16[1,64,320]{2,1,0:T(8,128)(2,1)S(1)}, bf16[1,64,320]{2,1,0:T(8,128)(2,1)}, u32[]{:S(2)}) copy-start(bf16[1,64,320]{2,1,0:T(8,128)(2,1)} %param.15) | copy-start | bytes 122884
  0.0 15.8 %copy-start.5 = (bf16[1,3,3,320,64]{3,4,2,1,0:T(8,128)(2,1)S(1)}, bf16[1,3,3,320,64]{3,4,2,1,0:T(8,128)(2,1)}, u32[]{:S(2)}) copy-start(bf16[1,3,3,320,64]{3,4,2,1,0:T(8,128)(2,1)} %param.14) | copy-start | bytes 1105924
  1.4 17.5 %all-to-all-start.1 = ((s32[16,1,1]{2,1,0:T(1,128)}), s32[16,1,1]{2,1,0:T(1,128)S(1)}, u32[]{:S(2)}, u32[]{:S(2)}) async-start(s32[16,1,1]{2,1,0:T(1,128)} %broadcast_in_dim.56), calls=%async_computation.1 | async-start | bytes 16384 | tf_op jit(solution)/shard_map/all_to_all | solution.py:26
  16.5 11.3 %copy-start.1 = (s32[256]{0:T(256)S(1)}, s32[256]{0:T(256)}, u32[]{:S(2)}) copy-start(s32[256]{0:T(256)} %param.12) | copy-start | bytes 3076
  16.6 27.6 %copy-start.3 = (bf16[1,4,512,320]{2,3,1,0:T(8,128)(2,1)S(1)}, bf16[1,4,512,320]{2,3,1,0:T(8,128)(2,1)}, u32[]{:S(2)}) copy-start(bf16[1,4,512,320]{2,3,1,0:T(8,128)(2,1)} %param.9) | copy-start | bytes 3932164
  18.8 24.8 %all-to-all-start = ((f32[16,120,128]{2,1,0:T(8,128)}), f32[16,120,128]{2,1,0:T(8,128)S(1)}, u32[]{:S(2)}, u32[]{:S(2)}) async-start(f32[16,120,128]{2,1,0:T(8,128)} %pad_maximum_fusion), calls=%async_computation | async-start | bytes 1966080 | tf_op jit(solution)/shard_map/all_to_all | solution.py:165
  45.1 1.1 copy-start.4
  46.2 12.6 %copy-start.7 = (bf16[1,1280]{1,0:T(2,128)(2,1)S(1)}, bf16[1,1280]{1,0:T(2,128)(2,1)}, u32[]{:S(2)}) copy-start(bf16[1,1280]{1,0:T(2,128)(2,1)} %param.10) | copy-start | bytes 7684
  47.0 15.4 %collective-permute-start = (bf16[1,1,320,512]{3,2,1,0:T(8,128)(2,1)}, bf16[1,1,320,512]{3,2,1,0:T(8,128)(2,1)}, u32[]{:S(2)}, u32[]{:S(2)}) collective-permute-start(bf16[1,1,320,512]{3,2,1,0:T(8,128)(2,1)} %get-tuple-element.13), channel_id=1, source_target_pairs={{0,16},{16,32},{32,48},{48,64},{64,80},{80,96},{96,112},{112,128},... | collective-permute-start | bytes 983048 | tf_op jit(solution)/shard_map/ppermute | solution.py:17
  50.0 12.4 %collective-permute-start.1 = (bf16[1,1,320,512]{3,2,1,0:T(8,128)(2,1)S(1)}, bf16[1,1,320,512]{3,2,1,0:T(8,128)(2,1)}, u32[]{:S(2)}, u32[]{:S(2)}) collective-permute-start(bf16[1,1,320,512]{3,2,1,0:T(8,128)(2,1)S(1)} %get-tuple-element.14), channel_id=1, source_target_pairs={{16,0},{32,16},{48,32},{64,48},{80,64},{96,80},{112,96},{128,112},... | collective-permute-start | bytes 983048 | tf_op jit(solution)/shard_map/ppermute | solution.py:18
  53.7 19.7 %all-to-all-start.2 = ((bf16[16,112,128]{2,1,0:T(8,128)(2,1)}), bf16[16,112,128]{2,1,0:T(8,128)(2,1)S(1)}, u32[]{:S(2)}, u32[]{:S(2)}) async-start(bf16[16,112,128]{2,1,0:T(8,128)(2,1)} %broadcast_select_fusion), calls=%async_computation.2 | async-start | bytes 917504 | tf_op jit(solution)/shard_map/all_to_all | solution.py:169
  74.2 17.4 %all-to-all-start.3 = ((bf16[16,112,128]{2,1,0:T(8,128)(2,1)}), bf16[16,112,128]{2,1,0:T(8,128)(2,1)S(1)}, u32[]{:S(2)}, u32[]{:S(2)}) async-start(bf16[16,112,128]{2,1,0:T(8,128)(2,1)} %broadcast_in_dim.60), calls=%async_computation.3 | async-start | bytes 917504 | tf_op jit(solution)/shard_map/all_to_all | solution.py:26
  105.8 2.5 %copy-start.2 = (f32[4,320,512]{2,1,0:T(8,128)S(1)}, f32[4,320,512]{2,1,0:T(8,128)}, u32[]{:S(2)}) copy-start(f32[4,320,512]{2,1,0:T(8,128)} %shard_map.91) | copy-start | bytes 7864324
  121.4 6.5 %collective-permute-start.2 = (bf16[1,1,320,512]{3,2,1,0:T(8,128)(2,1)S(1)}, bf16[1,1,320,512]{3,2,1,0:T(8,128)(2,1)S(1)}, u32[]{:S(2)}, u32[]{:S(2)}) collective-permute-start(bf16[1,1,320,512]{3,2,1,0:T(8,128)(2,1)S(1)} %get-tuple-element.11), channel_id=1, source_target_pairs={{0,16},{16,32},{32,48},{48,64},{64,80},{80,96},{96,112},{112,128},... | collective-permute-start | bytes 983048 | tf_op jit(solution)/shard_map/ppermute | solution.py:17
  123.8 9.9 %collective-permute-start.3 = (bf16[1,1,320,512]{3,2,1,0:T(8,128)(2,1)S(1)}, bf16[1,1,320,512]{3,2,1,0:T(8,128)(2,1)S(1)}, u32[]{:S(2)}, u32[]{:S(2)}) collective-permute-start(bf16[1,1,320,512]{3,2,1,0:T(8,128)(2,1)S(1)} %get-tuple-element.12), channel_id=1, source_target_pairs={{16,0},{32,16},{48,32},{64,48},{80,64},{96,80},{112,96},{128,112},... | collective-permute-start | bytes 983048 | tf_op jit(solution)/shard_map/ppermute | solution.py:18

commit v10 on v8

--- a/solution.py
+++ b/solution.py
@@ -55,6 +55,16 @@
 def conv_input(field, groups):
     mean, scale = norm_stats(field, groups)
     return with_halo(norm_silu(field, mean, scale, groups), (("band", 1),), 1)
+
+
+def conv_input_early(field, groups):
+    extended = with_halo(field, (("band", 1),), 1)
+    mean, scale = norm_stats(field, groups)
+    normed = norm_silu(extended, mean, scale, groups)
+    band, bands = lax.axis_index("band"), lax.axis_size("band")
+    row = lax.broadcasted_iota(jnp.int32, (1, normed.shape[1], 1, 1), 1)
+    outside = ((row == 0) & (band == 0)) | ((row == normed.shape[1] - 1) & (band == bands - 1))
+    return jnp.where(outside, jnp.zeros((), normed.dtype), normed)
 
 
 def taps_by_column(field):
@@ -191,7 +201,7 @@
         shift.reshape(channels, 1),
     )[None]
     result = second_conv(
-        taps_by_column(conv_input(hidden, G)[0]),
+        taps_by_column(conv_input_early(hidden, G)[0]),
         second_conv_weight.reshape(3, wide_of(second_conv_weight), channels),
         field[0],
     )

time: 144 us -> 148 us (1.028)
  blocking collectives: 10.8 us -> 0 us
  starting transfers between devices: 46.2 us -> 52.9 us
  waiting for transfers between devices: 25.5 us -> 31 us
  local copies, waits for them, and re-layouts: 14.4 us -> 16.1 us
    all_to_all x1 -> x0, blocking collectives: 10.8 us -> none  [exchange(): return lax.all_to_all(spread, axis, 0, 0, tiled=True)]
    ppermute x2, waiting for transfers between devices: 1.89 us -> 7.38 us  [with_halo(): before = lax.ppermute(last, axis, up)]
    all_to_all x3 -> x4, starting transfers between devices: 26.3 us -> 30.2 us  [exchange(): return lax.all_to_all(spread, axis, 0, 0, tiled=True)]
    select_n x0 -> x1, other arithmetic: none -> 2.59 us  [conv_input_early(): return jnp.where(outside, jnp.zeros((), normed.dtype), normed)]
    ppermute x2, starting transfers between devices: 7.53 us -> 10.1 us  [with_halo(): before = lax.ppermute(last, axis, up)]
    all_to_all x3 -> x4, waiting for transfers between devices: 12.6 us -> 12.6 us  [exchange(): return lax.all_to_all(spread, axis, 0, 0, tiled=True)]
  transfers between devices with their start and end apart: 9 -> 10, of which waited for: 7 -> 7; matrix products, arithmetic and copies ran while one was open for 15% -> 16% of each run, Pallas kernels for 0% -> 0%
where the time goes in v10:
time: 148 us; the launch traced here: 147 us
  starting transfers between devices  52.9 us (36%)
  waiting for transfers between devices  31 us (21%)
  other arithmetic  23.1 us (16%)
  Pallas kernels  21.3 us (14%)
  local copies, waits for them, and re-layouts  16.1 us (11%)
  between operations  2.82 us (2%)
    all_to_all x4, starting transfers between devices, exchange(): return lax.all_to_all(spread, axis, 0, 0, tiled=True)  30.2 us
    all_to_all x4, waiting for transfers between devices, exchange(): return lax.all_to_all(spread, axis, 0, 0, tiled=True)  12.6 us
    pallas_call x1, Pallas kernels, first_conv(): pl.pallas_call(first_conv_kernel, grid=(rows,), in_specs=[pl.BlockSpec(co...  12.2 us
    ppermute x2, starting transfers between devices, with_halo(): before = lax.ppermute(last, axis, up)  10.1 us
    concatenate x2, other arithmetic, taps_by_column(): return jnp.concatenate([left, field, right], axis=1)  9.21 us
    pallas_call x1, Pallas kernels, second_conv(): pl.pallas_call(second_conv_kernel, grid=(rows,), in_specs=[pl.BlockSpec(c...  9.11 us
    ppermute x2, waiting for transfers between devices, with_halo(): before = lax.ppermute(last, axis, up)  7.38 us
    ppermute x2, waiting for transfers between devices, with_halo(): after = lax.ppermute(initial, axis, down)  5.98 us
  transfers between devices with their start and end apart: 10, of which 7 were waited for; matrix products, arithmetic and copies ran while one was open for 16% of the time, Pallas kernels for 0%

profile of v10, /device:TPU:1, one launch (start us, length us, event | category | flops | bytes accessed | tf_op | source)
XLA Modules:
  0.0 147.5 jit_solution(9830595326223279739)
XLA Ops:
  1.4 10.1 %all-to-all-start.1 = ((s32[16,1,1]{2,1,0:T(1,128)}), s32[16,1,1]{2,1,0:T(1,128)S(1)}, u32[]{:S(2)}, u32[]{:S(2)}) async-start(s32[16,1,1]{2,1,0:T(1,128)} %broadcast_in_dim.74), calls=%async_computation.1 | async-start | bytes 16384 | tf_op jit(solution)/shard_map/all_to_all | solution.py:26
  13.5 1.8 %fusion.10 = f32[320]{0:T(512)S(1)} fusion(bf16[1,4,512,320]{2,3,1,0:T(8,128)(2,1)} %param.9, f32[320]{0:T(512)S(1)} %sub.107), kind=kLoop, calls=%fused_computation.19 | loop fusion | flops 2621120 | bytes 1313280 | tf_op jit(solution)/shard_map/reduce_sum | solution.py:36
  19.4 8.8 %all-to-all-start = ((f32[16,2,1,32]{3,2,1,0:T(1,128)}), f32[16,2,1,32]{3,2,1,0:T(1,128)S(1)}, u32[]{:S(2)}, u32[]{:S(2)}) async-start(f32[16,2,1,32]{3,2,1,0:T(1,128)} %broadcast_in_dim.72), calls=%async_computation | async-start | bytes 32768 | tf_op jit(solution)/shard_map/all_to_all | solution.py:26
  29.2 6.2 %all-to-all-done = f32[16,2,1,32]{3,2,1,0:T(1,128)S(1)} async-done(((f32[16,2,1,32]{3,2,1,0:T(1,128)}), f32[16,2,1,32]{3,2,1,0:T(1,128)S(1)}, u32[]{:S(2)}, u32[]{:S(2)}) %all-to-all-start) | async-done | bytes 4128 | tf_op jit(solution)/shard_map/all_to_all | solution.py:26
  35.4 3.7 %all-to-all-start.2 = ((bf16[16,112,128]{2,1,0:T(8,128)(2,1)}), bf16[16,112,128]{2,1,0:T(8,128)(2,1)S(1)}, u32[]{:S(2)}, u32[]{:S(2)}) async-start(bf16[16,112,128]{2,1,0:T(8,128)(2,1)} %bitcast.11), calls=%async_computation.2 | async-start | bytes 917504 | tf_op jit(solution)/shard_map/all_to_all | solution.py:163
  41.7 2.1 %collective-permute-start.1 = (bf16[1,1,320,512]{3,2,1,0:T(8,128)(2,1)S(1)}, bf16[1,1,320,512]{3,2,1,0:T(8,128)(2,1)}, u32[]{:S(2)}, u32[]{:S(2)}) collective-permute-start(bf16[1,1,320,512]{3,2,1,0:T(8,128)(2,1)S(1)} %get-tuple-element.14), channel_id=1, source_target_pairs={{16,0},{32,16},{48,32},{64,48},{80,64},{96,80},{112,96},{128,112},... | collective-permute-start | bytes 983048 | tf_op jit(solution)/shard_map/ppermute | solution.py:18
  43.9 4.9 %collective-permute-start = (bf16[1,1,320,512]{3,2,1,0:T(8,128)(2,1)S(1)}, bf16[1,1,320,512]{3,2,1,0:T(8,128)(2,1)}, u32[]{:S(2)}, u32[]{:S(2)}) collective-permute-start(bf16[1,1,320,512]{3,2,1,0:T(8,128)(2,1)S(1)} %get-tuple-element.13), channel_id=1, source_target_pairs={{0,16},{16,32},{32,48},{48,64},{64,80},{80,96},{96,112},{112,128},... | collective-permute-start | bytes 983048 | tf_op jit(solution)/shard_map/ppermute | solution.py:17
  51.4 4.6 %all-to-all-start.3 = ((bf16[16,112,128]{2,1,0:T(8,128)(2,1)}), bf16[16,112,128]{2,1,0:T(8,128)(2,1)S(1)}, u32[]{:S(2)}, u32[]{:S(2)}) async-start(bf16[16,112,128]{2,1,0:T(8,128)(2,1)} %broadcast_select_fusion), calls=%async_computation.3 | async-start | bytes 917504 | tf_op jit(solution)/shard_map/all_to_all | solution.py:165
  59.5 1.7 %maximum_bitcast_fusion = bf16[6,320,512]{2,1,0:T(8,128)(2,1)S(1)} fusion(bf16[1,1,320,512]{3,2,1,0:T(8,128)(2,1)} %collective-permute-done.1, bf16[1,4,320,512]{3,2,1,0:T(8,128)(2,1)} %copy-done.4, bf16[1,1,320,512]{3,2,1,0:T(8,128)(2,1)} %collective-permute-done), kind=kLoop, calls=%fused_computation.28 | loop fusion | flops 1966080 | bytes 3932160 | tf_op jit(solution)/shard_map/squeeze | solution.py:197
  61.2 3.0 %fusion.35 = (bf16[6,320,511]{2,1,0:T(8,128)(2,1)}, bf16[6,320,511]{2,1,0:T(8,128)(2,1)}) fusion(bf16[6,320,512]{2,1,0:T(8,128)(2,1)S(1)} %maximum_bitcast_fusion), kind=kLoop, calls=%fused_computation.79 | loop fusion | bytes 7848960 | tf_op jit(solution)/shard_map/slice | solution.py:72
  64.2 3.9 %all-to-all-done.3 = bf16[16,112,128]{2,1,0:T(8,128)(2,1)S(1)} async-done(((bf16[16,112,128]{2,1,0:T(8,128)(2,1)}), bf16[16,112,128]{2,1,0:T(8,128)(2,1)S(1)}, u32[]{:S(2)}, u32[]{:S(2)}) %all-to-all-start.3) | async-done | bytes 458784 | tf_op jit(solution)/shard_map/all_to_all | solution.py:165
  68.9 7.0 %all-to-all-start.4 = ((bf16[16,112,128]{2,1,0:T(8,128)(2,1)}), bf16[16,112,128]{2,1,0:T(8,128)(2,1)S(1)}, u32[]{:S(2)}, u32[]{:S(2)}) async-start(bf16[16,112,128]{2,1,0:T(8,128)(2,1)} %broadcast_in_dim.78), calls=%async_computation.4 | async-start | bytes 917504 | tf_op jit(solution)/shard_map/all_to_all | solution.py:26
  75.9 5.7 %fusion.5.x_ref = bf16[6,960,512]{2,1,0:T(8,128)(2,1)} fusion(bf16[6,320,511]{2,1,0:T(8,128)(2,1)} %get-tuple-element.12, bf16[6,320,511]{2,1,0:T(8,128)(2,1)} %get-tuple-element.11, bf16[6,320,512]{2,1,0:T(8,128)(2,1)S(1)} %maximum_bitcast_fusion), kind=kLoop, calls=%fused_computation.9 | loop fusion | flops 29491200 | bytes 11788800 | tf_op jit(solution)/shard_map/concatenate | solution.py:74
  81.7 4.9 %all-to-all-done.4 = bf16[16,112,128]{2,1,0:T(8,128)(2,1)S(1)} async-done(((bf16[16,112,128]{2,1,0:T(8,128)(2,1)}), bf16[16,112,128]{2,1,0:T(8,128)(2,1)S(1)}, u32[]{:S(2)}, u32[]{:S(2)}) %all-to-all-start.4) | async-done | bytes 458784 | tf_op jit(solution)/shard_map/all_to_all | solution.py:26
  88.7 12.2 %shard_map.91 = f32[4,320,512]{2,1,0:T(8,128)} custom-call(bf16[6,960,512]{2,1,0:T(8,128)(2,1)} %fusion.5.x_ref, bf16[3,960,320]{2,1,0:T(8,128)(2,1)} %bitcast.60, bf16[3,960,64]{2,1,0:T(8,128)(2,1)} %reshape_reshape.3.d_ref, bf16[320,64]{1,0:T(8,128)(2,1)} %bitcast.64, f32[320,1]{1,0:T(8,128)} %reshape.492.s_ref), custom_call_target="tpu_custom_call" | custom-call | flops 1593835520 | bytes 10731520 | tf_op jit(solution)/shard_map/pallas_call | solution.py:117
  100.8 2.1 %reduce_sum.127 = f32[320]{0:T(512)S(1)} reduce(f32[4,320,512]{2,1,0:T(8,128)} %shard_map.91, f32[]{:T(128)} %constant.82.clone.1), dimensions={0,2}, to_apply=%region_7.8 | reduce | flops 655040 | bytes 2622724 | tf_op jit(solution)/shard_map/reduce_sum | solution.py:34
  104.7 4.3 %all-to-all-start.5 = ((f32[16,2,1,32]{3,2,1,0:T(1,128)}), f32[16,2,1,32]{3,2,1,0:T(1,128)S(1)}, u32[]{:S(2)}, u32[]{:S(2)}) async-start(f32[16,2,1,32]{3,2,1,0:T(1,128)} %broadcast_in_dim.81), calls=%async_computation.5 | async-start | bytes 32768 | tf_op jit(solution)/shard_map/all_to_all | solution.py:26
  110.1 2.1 %collective-permute-start.3 = (f32[1,1,320,512]{3,2,1,0:T(8,128)}, f32[1,1,320,512]{3,2,1,0:T(8,128)}, u32[]{:S(2)}, u32[]{:S(2)}) collective-permute-start(f32[1,1,320,512]{3,2,1,0:T(8,128)} %get-tuple-element.8), channel_id=1, source_target_pairs={{16,0},{32,16},{48,32},{64,48},{80,64},{96,80},{112,96},{128,112},... | collective-permute-start | bytes 1966088 | tf_op jit(solution)/shard_map/ppermute | solution.py:18
  112.3 5.1 %collective-permute-start.2 = (f32[1,1,320,512]{3,2,1,0:T(8,128)}, f32[1,1,320,512]{3,2,1,0:T(8,128)}, u32[]{:S(2)}, u32[]{:S(2)}) collective-permute-start(f32[1,1,320,512]{3,2,1,0:T(8,128)} %get-tuple-element.7), channel_id=1, source_target_pairs={{0,16},{16,32},{32,48},{48,64},{64,80},{80,96},{96,112},{112,128},... | collective-permute-start | bytes 1966088 | tf_op jit(solution)/shard_map/ppermute | solution.py:17
  117.9 6.0 %collective-permute-done.3 = f32[1,1,320,512]{3,2,1,0:T(8,128)} collective-permute-done((f32[1,1,320,512]{3,2,1,0:T(8,128)}, f32[1,1,320,512]{3,2,1,0:T(8,128)}, u32[]{:S(2)}, u32[]{:S(2)}) %collective-permute-start.3) | collective-permute-done | bytes 655392 | tf_op jit(solution)/shard_map/ppermute | solution.py:18
  123.9 7.4 %collective-permute-done.2 = f32[1,1,320,512]{3,2,1,0:T(8,128)} collective-permute-done((f32[1,1,320,512]{3,2,1,0:T(8,128)}, f32[1,1,320,512]{3,2,1,0:T(8,128)}, u32[]{:S(2)}, u32[]{:S(2)}) %collective-permute-start.2) | collective-permute-done | bytes 655392 | tf_op jit(solution)/shard_map/ppermute | solution.py:17
  131.2 2.6 %fusion.18 = bf16[6,320,512]{2,1,0:T(8,128)(2,1)S(1)} fusion(f32[320]{0:T(512)S(1)} %mul.120, f32[320]{0:T(512)S(1)} %sub.123, f32[1,320,512]{2,1,0:T(8,128)} %bitcast.20, f32[4,320,512]{2,1,0:T(8,128)S(1)} %copy-done.2, f32[1,320,512]{2,1,0:T(8,128)} %bitcast.19, pred[6]{0:T(512)(128)(4,1)S(1)} %and_or_fusion), kind=kLoop, calls=%fused_computation.29 | loop fusion | flops 9830400 | bytes 5900806 | tf_op jit(solution)/shard_map/jit(_where)/select_n | solution.py:67
  134.9 3.5 %fusion.7.x_ref = bf16[6,960,512]{2,1,0:T(8,128)(2,1)} fusion(bf16[6,320,511]{2,1,0:T(8,128)(2,1)S(1)} %get-tuple-element.10, bf16[6,320,511]{2,1,0:T(8,128)(2,1)S(1)} %get-tuple-element.9, bf16[6,320,512]{2,1,0:T(8,128)(2,1)S(1)} %fusion.18), kind=kLoop, calls=%fused_computation.11 | loop fusion | flops 29491200 | bytes 11788800 | tf_op jit(solution)/shard_map/concatenate | solution.py:74
  138.4 9.1 %shard_map.92 = bf16[4,320,512]{2,1,0:T(8,128)(2,1)} custom-call(bf16[6,960,512]{2,1,0:T(8,128)(2,1)} %fusion.7.x_ref, bf16[3,960,320]{2,1,0:T(8,128)(2,1)} %bitcast.61, bf16[4,320,512]{2,1,0:T(8,128)(2,1)} %bitcast.59), custom_call_target="tpu_custom_call" | custom-call | flops 1258291200 | bytes 10362880 | tf_op jit(solution)/shard_map/pallas_call | solution.py:139
  (90 shorter events, 21.8 us)
Async XLA Ops:
  0.0 56.0 %copy-start = (bf16[1280,320]{0,1:T(8,128)(2,1)S(1)}, bf16[1280,320]{0,1:T(8,128)(2,1)}, u32[]{:S(2)}) copy-start(bf16[1280,320]{0,1:T(8,128)(2,1)} %param.17) | copy-start | bytes 2457604
  0.0 15.5 %copy-start.6 = (bf16[1,64,320]{2,1,0:T(8,128)(2,1)S(1)}, bf16[1,64,320]{2,1,0:T(8,128)(2,1)}, u32[]{:S(2)}) copy-start(bf16[1,64,320]{2,1,0:T(8,128)(2,1)} %param.15) | copy-start | bytes 122884
  0.0 15.7 %copy-start.5 = (bf16[1,3,3,320,64]{3,4,2,1,0:T(8,128)(2,1)S(1)}, bf16[1,3,3,320,64]{3,4,2,1,0:T(8,128)(2,1)}, u32[]{:S(2)}) copy-start(bf16[1,3,3,320,64]{3,4,2,1,0:T(8,128)(2,1)} %param.14) | copy-start | bytes 1105924
  1.4 17.4 %all-to-all-start.1 = ((s32[16,1,1]{2,1,0:T(1,128)}), s32[16,1,1]{2,1,0:T(1,128)S(1)}, u32[]{:S(2)}, u32[]{:S(2)}) async-start(s32[16,1,1]{2,1,0:T(1,128)} %broadcast_in_dim.74), calls=%async_computation.1 | async-start | bytes 16384 | tf_op jit(solution)/shard_map/all_to_all | solution.py:26
  13.1 15.4 %copy-start.1 = (s32[256]{0:T(256)S(1)}, s32[256]{0:T(256)}, u32[]{:S(2)}) copy-start(s32[256]{0:T(256)} %param.12) | copy-start | bytes 3076
  15.3 24.3 %copy-start.3 = (bf16[1,4,512,320]{2,3,1,0:T(8,128)(2,1)S(1)}, bf16[1,4,512,320]{2,3,1,0:T(8,128)(2,1)}, u32[]{:S(2)}) copy-start(bf16[1,4,512,320]{2,3,1,0:T(8,128)(2,1)} %param.9) | copy-start | bytes 3932164
  19.4 16.1 %all-to-all-start = ((f32[16,2,1,32]{3,2,1,0:T(1,128)}), f32[16,2,1,32]{3,2,1,0:T(1,128)S(1)}, u32[]{:S(2)}, u32[]{:S(2)}) async-start(f32[16,2,1,32]{3,2,1,0:T(1,128)} %broadcast_in_dim.72), calls=%async_computation | async-start | bytes 32768 | tf_op jit(solution)/shard_map/all_to_all | solution.py:26
  35.4 14.5 %all-to-all-start.2 = ((bf16[16,112,128]{2,1,0:T(8,128)(2,1)}), bf16[16,112,128]{2,1,0:T(8,128)(2,1)S(1)}, u32[]{:S(2)}, u32[]{:S(2)}) async-start(bf16[16,112,128]{2,1,0:T(8,128)(2,1)} %bitcast.11), calls=%async_computation.2 | async-start | bytes 917504 | tf_op jit(solution)/shard_map/all_to_all | solution.py:163
  40.6 1.1 copy-start.4
  41.7 14.4 %copy-start.7 = (bf16[1,1280]{1,0:T(2,128)(2,1)S(1)}, bf16[1,1280]{1,0:T(2,128)(2,1)}, u32[]{:S(2)}) copy-start(bf16[1,1280]{1,0:T(2,128)(2,1)} %param.10) | copy-start | bytes 7684
  41.7 17.8 %collective-permute-start.1 = (bf16[1,1,320,512]{3,2,1,0:T(8,128)(2,1)S(1)}, bf16[1,1,320,512]{3,2,1,0:T(8,128)(2,1)}, u32[]{:S(2)}, u32[]{:S(2)}) collective-permute-start(bf16[1,1,320,512]{3,2,1,0:T(8,128)(2,1)S(1)} %get-tuple-element.14), channel_id=1, source_target_pairs={{16,0},{32,16},{48,32},{64,48},{80,64},{96,80},{112,96},{128,112},... | collective-permute-start | bytes 983048 | tf_op jit(solution)/shard_map/ppermute | solution.py:18
  43.9 15.6 %collective-permute-start = (bf16[1,1,320,512]{3,2,1,0:T(8,128)(2,1)S(1)}, bf16[1,1,320,512]{3,2,1,0:T(8,128)(2,1)}, u32[]{:S(2)}, u32[]{:S(2)}) collective-permute-start(bf16[1,1,320,512]{3,2,1,0:T(8,128)(2,1)S(1)} %get-tuple-element.13), channel_id=1, source_target_pairs={{0,16},{16,32},{32,48},{48,64},{64,80},{80,96},{96,112},{112,128},... | collective-permute-start | bytes 983048 | tf_op jit(solution)/shard_map/ppermute | solution.py:17
  51.4 16.6 %all-to-all-start.3 = ((bf16[16,112,128]{2,1,0:T(8,128)(2,1)}), bf16[16,112,128]{2,1,0:T(8,128)(2,1)S(1)}, u32[]{:S(2)}, u32[]{:S(2)}) async-start(bf16[16,112,128]{2,1,0:T(8,128)(2,1)} %broadcast_select_fusion), calls=%async_computation.3 | async-start | bytes 917504 | tf_op jit(solution)/shard_map/all_to_all | solution.py:165
  68.9 17.7 %all-to-all-start.4 = ((bf16[16,112,128]{2,1,0:T(8,128)(2,1)}), bf16[16,112,128]{2,1,0:T(8,128)(2,1)S(1)}, u32[]{:S(2)}, u32[]{:S(2)}) async-start(bf16[16,112,128]{2,1,0:T(8,128)(2,1)} %broadcast_in_dim.78), calls=%async_computation.4 | async-start | bytes 917504 | tf_op jit(solution)/shard_map/all_to_all | solution.py:26
  100.8 2.5 %copy-start.2 = (f32[4,320,512]{2,1,0:T(8,128)S(1)}, f32[4,320,512]{2,1,0:T(8,128)}, u32[]{:S(2)}) copy-start(f32[4,320,512]{2,1,0:T(8,128)} %shard_map.91) | copy-start | bytes 7864324
  104.7 12.7 %all-to-all-start.5 = ((f32[16,2,1,32]{3,2,1,0:T(1,128)}), f32[16,2,1,32]{3,2,1,0:T(1,128)S(1)}, u32[]{:S(2)}, u32[]{:S(2)}) async-start(f32[16,2,1,32]{3,2,1,0:T(1,128)} %broadcast_in_dim.81), calls=%async_computation.5 | async-start | bytes 32768 | tf_op jit(solution)/shard_map/all_to_all | solution.py:26
  110.1 13.7 %collective-permute-start.3 = (f32[1,1,320,512]{3,2,1,0:T(8,128)}, f32[1,1,320,512]{3,2,1,0:T(8,128)}, u32[]{:S(2)}, u32[]{:S(2)}) collective-permute-start(f32[1,1,320,512]{3,2,1,0:T(8,128)} %get-tuple-element.8), channel_id=1, source_target_pairs={{16,0},{32,16},{48,32},{64,48},{80,64},{96,80},{112,96},{128,112},... | collective-permute-start | bytes 1966088 | tf_op jit(solution)/shard_map/ppermute | solution.py:18
  112.3 19.0 %collective-permute-start.2 = (f32[1,1,320,512]{3,2,1,0:T(8,128)}, f32[1,1,320,512]{3,2,1,0:T(8,128)}, u32[]{:S(2)}, u32[]{:S(2)}) collective-permute-start(f32[1,1,320,512]{3,2,1,0:T(8,128)} %get-tuple-element.7), channel_id=1, source_target_pairs={{0,16},{16,32},{32,48},{48,64},{64,80},{80,96},{96,112},{112,128},... | collective-permute-start | bytes 1966088 | tf_op jit(solution)/shard_map/ppermute | solution.py:17

commit v11 on v8

--- a/solution.py
+++ b/solution.py
@@ -84,7 +84,9 @@
         l = lax.dot_general(d_ref[tap], piece, dims, preferred_element_type=jnp.float32)
         main = m if main is None else main + m
         low = l if low is None else low + l
-    lifted = jnp.dot(u_ref[...], low.astype(jnp.bfloat16), preferred_element_type=jnp.float32)
+    lifted = lax.dot_general(
+        u_ref[...], low.astype(jnp.bfloat16), dims, preferred_element_type=jnp.float32
+    )
     o_ref[0] = main + lifted + s_ref[...]
 
 
@@ -187,7 +189,7 @@
         taps_by_column(conv_input(field, G)[0]),
         first_conv_weight.reshape(3, wide_of(first_conv_weight), channels),
         chosen_down.reshape(3, wide_of(chosen_down), chosen_down.shape[-1]),
-        chosen_up.T,
+        chosen_up,
         shift.reshape(channels, 1),
     )[None]
     result = second_conv(

time: 144 us -> 144 us (level)
  no operation moved by 1% of the time
where the time goes in v11:
time: 144 us; the launch traced here: 143 us
  starting transfers between devices  46.2 us (32%)
  waiting for transfers between devices  25.5 us (18%)
  other arithmetic  21.7 us (15%)
  Pallas kernels  21.3 us (15%)
  local copies, waits for them, and re-layouts  14.2 us (10%)
  blocking collectives  10.8 us (8%)
  between operations  2.83 us (2%)
    all_to_all x3, starting transfers between devices, exchange(): return lax.all_to_all(spread, axis, 0, 0, tiled=True)  26.3 us
    all_to_all x3, waiting for transfers between devices, exchange(): return lax.all_to_all(spread, axis, 0, 0, tiled=True)  12.6 us
    pallas_call x1, Pallas kernels, first_conv(): pl.pallas_call(first_conv_kernel, grid=(rows,), in_specs=[pl.BlockSpec(co...  12.2 us
    all_to_all x1, blocking collectives, exchange(): return lax.all_to_all(spread, axis, 0, 0, tiled=True)  10.8 us
    concatenate x2, other arithmetic, taps_by_column(): return jnp.concatenate([left, field, right], axis=1)  9.21 us
    pallas_call x1, Pallas kernels, second_conv(): pl.pallas_call(second_conv_kernel, grid=(rows,), in_specs=[pl.BlockSpec(c...  9.1 us
    ppermute x2, starting transfers between devices, with_halo(): before = lax.ppermute(last, axis, up)  7.53 us
    ppermute x2, waiting for transfers between devices, with_halo(): after = lax.ppermute(initial, axis, down)  5.9 us
  transfers between devices with their start and end apart: 9, of which 7 were waited for; matrix products, arithmetic and copies ran while one was open for 15% of the time, Pallas kernels for 0%

profile of v11, /device:TPU:1, one launch (start us, length us, event | category | flops | bytes accessed | tf_op | source)
XLA Modules:
  0.0 142.9 jit_solution(11101998746652738759)
XLA Ops:
  1.4 10.1 %all-to-all-start.1 = ((s32[16,1,1]{2,1,0:T(1,128)}), s32[16,1,1]{2,1,0:T(1,128)S(1)}, u32[]{:S(2)}, u32[]{:S(2)}) async-start(s32[16,1,1]{2,1,0:T(1,128)} %broadcast_in_dim.57), calls=%async_computation.1 | async-start | bytes 16384 | tf_op jit(solution)/shard_map/all_to_all | solution.py:26
  11.5 1.6 %convert_reduce_fusion = f32[320]{0:T(512)S(1)} fusion(bf16[1,4,512,320]{2,3,1,0:T(8,128)(2,1)} %param.9), kind=kLoop, calls=%fused_computation.14 | loop fusion | flops 1310400 | bytes 1312000 | tf_op jit(solution)/shard_map/reduce_sum | solution.py:34
  13.5 1.8 %fusion.9 = f32[320]{0:T(512)S(1)} fusion(bf16[1,4,512,320]{2,3,1,0:T(8,128)(2,1)} %param.9, f32[320]{0:T(512)S(1)} %sub.103), kind=kLoop, calls=%fused_computation.16 | loop fusion | flops 2621120 | bytes 1313280 | tf_op jit(solution)/shard_map/reduce_sum | solution.py:36
  19.4 8.8 %all-to-all-start = ((f32[16,2,1,32]{3,2,1,0:T(1,128)}), f32[16,2,1,32]{3,2,1,0:T(1,128)S(1)}, u32[]{:S(2)}, u32[]{:S(2)}) async-start(f32[16,2,1,32]{3,2,1,0:T(1,128)} %broadcast_in_dim.31), calls=%async_computation | async-start | bytes 32768 | tf_op jit(solution)/shard_map/all_to_all | solution.py:26
  29.2 6.2 %all-to-all-done = f32[16,2,1,32]{3,2,1,0:T(1,128)S(1)} async-done(((f32[16,2,1,32]{3,2,1,0:T(1,128)}), f32[16,2,1,32]{3,2,1,0:T(1,128)S(1)}, u32[]{:S(2)}, u32[]{:S(2)}) %all-to-all-start) | async-done | bytes 4128 | tf_op jit(solution)/shard_map/all_to_all | solution.py:26
  35.4 3.7 %all-to-all-start.2 = ((bf16[16,112,128]{2,1,0:T(8,128)(2,1)}), bf16[16,112,128]{2,1,0:T(8,128)(2,1)S(1)}, u32[]{:S(2)}, u32[]{:S(2)}) async-start(bf16[16,112,128]{2,1,0:T(8,128)(2,1)} %bitcast.11), calls=%async_computation.2 | async-start | bytes 917504 | tf_op jit(solution)/shard_map/all_to_all | solution.py:155
  41.7 5.1 %collective-permute-start = (bf16[1,1,320,512]{3,2,1,0:T(8,128)(2,1)S(1)}, bf16[1,1,320,512]{3,2,1,0:T(8,128)(2,1)}, u32[]{:S(2)}, u32[]{:S(2)}) collective-permute-start(bf16[1,1,320,512]{3,2,1,0:T(8,128)(2,1)S(1)} %get-tuple-element.13), channel_id=1, source_target_pairs={{0,16},{16,32},{32,48},{48,64},{64,80},{80,96},{96,112},{112,128},... | collective-permute-start | bytes 983048 | tf_op jit(solution)/shard_map/ppermute | solution.py:17
  46.8 1.9 %collective-permute-start.1 = (bf16[1,1,320,512]{3,2,1,0:T(8,128)(2,1)S(1)}, bf16[1,1,320,512]{3,2,1,0:T(8,128)(2,1)}, u32[]{:S(2)}, u32[]{:S(2)}) collective-permute-start(bf16[1,1,320,512]{3,2,1,0:T(8,128)(2,1)S(1)} %get-tuple-element.14), channel_id=1, source_target_pairs={{16,0},{32,16},{48,32},{64,48},{80,64},{96,80},{112,96},{128,112},... | collective-permute-start | bytes 983048 | tf_op jit(solution)/shard_map/ppermute | solution.py:18
  51.4 4.6 %all-to-all-start.3 = ((bf16[16,112,128]{2,1,0:T(8,128)(2,1)}), bf16[16,112,128]{2,1,0:T(8,128)(2,1)S(1)}, u32[]{:S(2)}, u32[]{:S(2)}) async-start(bf16[16,112,128]{2,1,0:T(8,128)(2,1)} %broadcast_select_fusion), calls=%async_computation.3 | async-start | bytes 917504 | tf_op jit(solution)/shard_map/all_to_all | solution.py:157
  59.5 1.7 %maximum_bitcast_fusion = bf16[6,320,512]{2,1,0:T(8,128)(2,1)S(1)} fusion(bf16[1,1,320,512]{3,2,1,0:T(8,128)(2,1)} %collective-permute-done.1, bf16[1,4,320,512]{3,2,1,0:T(8,128)(2,1)} %copy-done.4, bf16[1,1,320,512]{3,2,1,0:T(8,128)(2,1)} %collective-permute-done), kind=kLoop, calls=%fused_computation.26 | loop fusion | flops 1966080 | bytes 3932160 | tf_op jit(solution)/shard_map/squeeze | solution.py:189
  61.2 3.0 %fusion.33 = (bf16[6,320,511]{2,1,0:T(8,128)(2,1)}, bf16[6,320,511]{2,1,0:T(8,128)(2,1)}) fusion(bf16[6,320,512]{2,1,0:T(8,128)(2,1)S(1)} %maximum_bitcast_fusion), kind=kLoop, calls=%fused_computation.76 | loop fusion | bytes 7848960 | tf_op jit(solution)/shard_map/slice | solution.py:62
  64.2 3.9 %all-to-all-done.3 = bf16[16,112,128]{2,1,0:T(8,128)(2,1)S(1)} async-done(((bf16[16,112,128]{2,1,0:T(8,128)(2,1)}), bf16[16,112,128]{2,1,0:T(8,128)(2,1)S(1)}, u32[]{:S(2)}, u32[]{:S(2)}) %all-to-all-start.3) | async-done | bytes 458784 | tf_op jit(solution)/shard_map/all_to_all | solution.py:157
  68.9 7.4 %all-to-all-start.4 = ((bf16[16,112,128]{2,1,0:T(8,128)(2,1)}), bf16[16,112,128]{2,1,0:T(8,128)(2,1)S(1)}, u32[]{:S(2)}, u32[]{:S(2)}) async-start(bf16[16,112,128]{2,1,0:T(8,128)(2,1)} %broadcast_in_dim.61), calls=%async_computation.4 | async-start | bytes 917504 | tf_op jit(solution)/shard_map/all_to_all | solution.py:26
  76.3 5.7 %fusion.5.x_ref = bf16[6,960,512]{2,1,0:T(8,128)(2,1)} fusion(bf16[6,320,511]{2,1,0:T(8,128)(2,1)} %get-tuple-element.10, bf16[6,320,511]{2,1,0:T(8,128)(2,1)} %get-tuple-element.9, bf16[6,320,512]{2,1,0:T(8,128)(2,1)S(1)} %maximum_bitcast_fusion), kind=kLoop, calls=%fused_computation.9 | loop fusion | flops 29491200 | bytes 11788800 | tf_op jit(solution)/shard_map/concatenate | solution.py:64
  82.1 4.9 %all-to-all-done.4 = bf16[16,112,128]{2,1,0:T(8,128)(2,1)S(1)} async-done(((bf16[16,112,128]{2,1,0:T(8,128)(2,1)}), bf16[16,112,128]{2,1,0:T(8,128)(2,1)S(1)}, u32[]{:S(2)}, u32[]{:S(2)}) %all-to-all-start.4) | async-done | bytes 458784 | tf_op jit(solution)/shard_map/all_to_all | solution.py:26
  89.0 12.2 %shard_map.91 = f32[4,320,512]{2,1,0:T(8,128)} custom-call(bf16[6,960,512]{2,1,0:T(8,128)(2,1)} %fusion.5.x_ref, bf16[3,960,320]{2,1,0:T(8,128)(2,1)} %bitcast.59, bf16[3,960,64]{2,1,0:T(8,128)(2,1)} %reshape_reshape.3.d_ref, bf16[64,320]{1,0:T(8,128)(2,1)} %reshape.404.u_ref, f32[320,1]{1,0:T(8,128)} %reshape.428.s_ref), custom_call_target="tpu_custom_call" | custom-call | flops 1593835520 | bytes 10731520 | tf_op jit(solution)/shard_map/pallas_call | solution.py:109
  101.2 2.1 %reduce_sum.127 = f32[320]{0:T(512)S(1)} reduce(f32[4,320,512]{2,1,0:T(8,128)} %shard_map.91, f32[]{:T(128)} %constant.69.clone.1), dimensions={0,2}, to_apply=%region_7.8 | reduce | flops 655040 | bytes 2622724 | tf_op jit(solution)/shard_map/reduce_sum | solution.py:34
  104.4 10.8 %all_to_all.37 = f32[16,2,1,32]{3,2,1,0:T(1,128)S(1)} all-to-all(f32[16,2,1,32]{3,2,1,0:T(1,128)S(1)} %broadcast_in_dim.63), channel_id=1, replica_groups=mesh['band'=16,'req'=16] {'band'}, dimensions={0} | all-to-all | bytes 8192 | tf_op jit(solution)/shard_map/all_to_all | solution.py:26
  116.6 2.5 %collective-permute-start.2 = (bf16[1,1,320,512]{3,2,1,0:T(8,128)(2,1)S(1)}, bf16[1,1,320,512]{3,2,1,0:T(8,128)(2,1)S(1)}, u32[]{:S(2)}, u32[]{:S(2)}) collective-permute-start(bf16[1,1,320,512]{3,2,1,0:T(8,128)(2,1)S(1)} %get-tuple-element.11), channel_id=1, source_target_pairs={{0,16},{16,32},{32,48},{48,64},{64,80},{80,96},{96,112},{112,128},... | collective-permute-start | bytes 983048 | tf_op jit(solution)/shard_map/ppermute | solution.py:17
  119.1 2.1 %collective-permute-start.3 = (bf16[1,1,320,512]{3,2,1,0:T(8,128)(2,1)S(1)}, bf16[1,1,320,512]{3,2,1,0:T(8,128)(2,1)S(1)}, u32[]{:S(2)}, u32[]{:S(2)}) collective-permute-start(bf16[1,1,320,512]{3,2,1,0:T(8,128)(2,1)S(1)} %get-tuple-element.12), channel_id=1, source_target_pairs={{16,0},{32,16},{48,32},{64,48},{80,64},{96,80},{112,96},{128,112},... | collective-permute-start | bytes 983048 | tf_op jit(solution)/shard_map/ppermute | solution.py:18
  121.2 1.9 %collective-permute-done.2 = bf16[1,1,320,512]{3,2,1,0:T(8,128)(2,1)S(1)} collective-permute-done((bf16[1,1,320,512]{3,2,1,0:T(8,128)(2,1)S(1)}, bf16[1,1,320,512]{3,2,1,0:T(8,128)(2,1)S(1)}, u32[]{:S(2)}, u32[]{:S(2)}) %collective-permute-start.2) | collective-permute-done | bytes 327712 | tf_op jit(solution)/shard_map/ppermute | solution.py:17
  123.1 5.9 %collective-permute-done.3 = bf16[1,1,320,512]{3,2,1,0:T(8,128)(2,1)S(1)} collective-permute-done((bf16[1,1,320,512]{3,2,1,0:T(8,128)(2,1)S(1)}, bf16[1,1,320,512]{3,2,1,0:T(8,128)(2,1)S(1)}, u32[]{:S(2)}, u32[]{:S(2)}) %collective-permute-start.3) | collective-permute-done | bytes 327712 | tf_op jit(solution)/shard_map/ppermute | solution.py:18
  130.3 3.5 %fusion.7.x_ref = bf16[6,960,512]{2,1,0:T(8,128)(2,1)} fusion(bf16[6,320,511]{2,1,0:T(8,128)(2,1)S(1)} %get-tuple-element.8, bf16[6,320,511]{2,1,0:T(8,128)(2,1)S(1)} %get-tuple-element.7, bf16[6,320,512]{2,1,0:T(8,128)(2,1)S(1)} %maximum_bitcast_fusion.1), kind=kLoop, calls=%fused_computation.11 | loop fusion | flops 29491200 | bytes 11788800 | tf_op jit(solution)/shard_map/concatenate | solution.py:64
  133.8 9.1 %shard_map.92 = bf16[4,320,512]{2,1,0:T(8,128)(2,1)} custom-call(bf16[6,960,512]{2,1,0:T(8,128)(2,1)} %fusion.7.x_ref, bf16[3,960,320]{2,1,0:T(8,128)(2,1)} %bitcast.60, bf16[4,320,512]{2,1,0:T(8,128)(2,1)} %bitcast.58), custom_call_target="tpu_custom_call" | custom-call | flops 1258291200 | bytes 10362880 | tf_op jit(solution)/shard_map/pallas_call | solution.py:131
  (88 shorter events, 19.6 us)
Async XLA Ops:
  0.0 56.0 %copy-start = (bf16[1280,320]{0,1:T(8,128)(2,1)S(1)}, bf16[1280,320]{0,1:T(8,128)(2,1)}, u32[]{:S(2)}) copy-start(bf16[1280,320]{0,1:T(8,128)(2,1)} %param.17) | copy-start | bytes 2457604
  0.0 15.5 %copy-start.5 = (bf16[1,3,3,320,64]{3,4,2,1,0:T(8,128)(2,1)S(1)}, bf16[1,3,3,320,64]{3,4,2,1,0:T(8,128)(2,1)}, u32[]{:S(2)}) copy-start(bf16[1,3,3,320,64]{3,4,2,1,0:T(8,128)(2,1)} %param.14) | copy-start | bytes 1105924
  0.0 16.3 %copy-start.6 = (bf16[1,64,320]{2,1,0:T(8,128)(2,1)S(1)}, bf16[1,64,320]{2,1,0:T(8,128)(2,1)}, u32[]{:S(2)}) copy-start(bf16[1,64,320]{2,1,0:T(8,128)(2,1)} %param.15) | copy-start | bytes 122884
  1.4 17.4 %all-to-all-start.1 = ((s32[16,1,1]{2,1,0:T(1,128)}), s32[16,1,1]{2,1,0:T(1,128)S(1)}, u32[]{:S(2)}, u32[]{:S(2)}) async-start(s32[16,1,1]{2,1,0:T(1,128)} %broadcast_in_dim.57), calls=%async_computation.1 | async-start | bytes 16384 | tf_op jit(solution)/shard_map/all_to_all | solution.py:26
  13.1 15.4 %copy-start.1 = (s32[256]{0:T(256)S(1)}, s32[256]{0:T(256)}, u32[]{:S(2)}) copy-start(s32[256]{0:T(256)} %param.12) | copy-start | bytes 3076
  15.3 24.3 %copy-start.3 = (bf16[1,4,512,320]{2,3,1,0:T(8,128)(2,1)S(1)}, bf16[1,4,512,320]{2,3,1,0:T(8,128)(2,1)}, u32[]{:S(2)}) copy-start(bf16[1,4,512,320]{2,3,1,0:T(8,128)(2,1)} %param.9) | copy-start | bytes 3932164
  19.4 16.1 %all-to-all-start = ((f32[16,2,1,32]{3,2,1,0:T(1,128)}), f32[16,2,1,32]{3,2,1,0:T(1,128)S(1)}, u32[]{:S(2)}, u32[]{:S(2)}) async-start(f32[16,2,1,32]{3,2,1,0:T(1,128)} %broadcast_in_dim.31), calls=%async_computation | async-start | bytes 32768 | tf_op jit(solution)/shard_map/all_to_all | solution.py:26
  35.4 14.5 %all-to-all-start.2 = ((bf16[16,112,128]{2,1,0:T(8,128)(2,1)}), bf16[16,112,128]{2,1,0:T(8,128)(2,1)S(1)}, u32[]{:S(2)}, u32[]{:S(2)}) async-start(bf16[16,112,128]{2,1,0:T(8,128)(2,1)} %bitcast.11), calls=%async_computation.2 | async-start | bytes 917504 | tf_op jit(solution)/shard_map/all_to_all | solution.py:155
  40.6 1.1 copy-start.4
  41.7 14.4 %copy-start.7 = (bf16[1,1280]{1,0:T(2,128)(2,1)S(1)}, bf16[1,1280]{1,0:T(2,128)(2,1)}, u32[]{:S(2)}) copy-start(bf16[1,1280]{1,0:T(2,128)(2,1)} %param.10) | copy-start | bytes 7684
  41.7 17.8 %collective-permute-start = (bf16[1,1,320,512]{3,2,1,0:T(8,128)(2,1)S(1)}, bf16[1,1,320,512]{3,2,1,0:T(8,128)(2,1)}, u32[]{:S(2)}, u32[]{:S(2)}) collective-permute-start(bf16[1,1,320,512]{3,2,1,0:T(8,128)(2,1)S(1)} %get-tuple-element.13), channel_id=1, source_target_pairs={{0,16},{16,32},{32,48},{48,64},{64,80},{80,96},{96,112},{112,128},... | collective-permute-start | bytes 983048 | tf_op jit(solution)/shard_map/ppermute | solution.py:17
  46.8 12.7 %collective-permute-start.1 = (bf16[1,1,320,512]{3,2,1,0:T(8,128)(2,1)S(1)}, bf16[1,1,320,512]{3,2,1,0:T(8,128)(2,1)}, u32[]{:S(2)}, u32[]{:S(2)}) collective-permute-start(bf16[1,1,320,512]{3,2,1,0:T(8,128)(2,1)S(1)} %get-tuple-element.14), channel_id=1, source_target_pairs={{16,0},{32,16},{48,32},{64,48},{80,64},{96,80},{112,96},{128,112},... | collective-permute-start | bytes 983048 | tf_op jit(solution)/shard_map/ppermute | solution.py:18
  51.4 16.6 %all-to-all-start.3 = ((bf16[16,112,128]{2,1,0:T(8,128)(2,1)}), bf16[16,112,128]{2,1,0:T(8,128)(2,1)S(1)}, u32[]{:S(2)}, u32[]{:S(2)}) async-start(bf16[16,112,128]{2,1,0:T(8,128)(2,1)} %broadcast_select_fusion), calls=%async_computation.3 | async-start | bytes 917504 | tf_op jit(solution)/shard_map/all_to_all | solution.py:157
  68.9 18.1 %all-to-all-start.4 = ((bf16[16,112,128]{2,1,0:T(8,128)(2,1)}), bf16[16,112,128]{2,1,0:T(8,128)(2,1)S(1)}, u32[]{:S(2)}, u32[]{:S(2)}) async-start(bf16[16,112,128]{2,1,0:T(8,128)(2,1)} %broadcast_in_dim.61), calls=%async_computation.4 | async-start | bytes 917504 | tf_op jit(solution)/shard_map/all_to_all | solution.py:26
  101.2 2.5 %copy-start.2 = (f32[4,320,512]{2,1,0:T(8,128)S(1)}, f32[4,320,512]{2,1,0:T(8,128)}, u32[]{:S(2)}) copy-start(f32[4,320,512]{2,1,0:T(8,128)} %shard_map.91) | copy-start | bytes 7864324
  116.6 6.5 %collective-permute-start.2 = (bf16[1,1,320,512]{3,2,1,0:T(8,128)(2,1)S(1)}, bf16[1,1,320,512]{3,2,1,0:T(8,128)(2,1)S(1)}, u32[]{:S(2)}, u32[]{:S(2)}) collective-permute-start(bf16[1,1,320,512]{3,2,1,0:T(8,128)(2,1)S(1)} %get-tuple-element.11), channel_id=1, source_target_pairs={{0,16},{16,32},{32,48},{48,64},{64,80},{80,96},{96,112},{112,128},... | collective-permute-start | bytes 983048 | tf_op jit(solution)/shard_map/ppermute | solution.py:17
  119.1 9.9 %collective-permute-start.3 = (bf16[1,1,320,512]{3,2,1,0:T(8,128)(2,1)S(1)}, bf16[1,1,320,512]{3,2,1,0:T(8,128)(2,1)S(1)}, u32[]{:S(2)}, u32[]{:S(2)}) collective-permute-start(bf16[1,1,320,512]{3,2,1,0:T(8,128)(2,1)S(1)} %get-tuple-element.12), channel_id=1, source_target_pairs={{16,0},{32,16},{48,32},{64,48},{80,64},{96,80},{112,96},{128,112},... | collective-permute-start | bytes 983048 | tf_op jit(solution)/shard_map/ppermute | solution.py:18
